TPU v7x, 32 devices: a whole 2x2x4 slice. The times are simulated.
32 devices in a mesh: pair: 4 (over z), gen: 8 (over y, x, core).
Axes of the slice: x: 2, y: 2, z: 4, core: 2. Of those that a mesh axis runs over, the one named last changes fastest.
Arguments:
- tokens: bfloat16 [32768, 2048], P(('pair', 'gen')), may hold values from -6 to 6
- cotangent: bfloat16 [32768, 256], P(('pair', 'gen')), may hold values from -6 to 6
- block_pair: int32 [32, 1], replicated, may hold values from 0 to 15
- src_lang: int32 [16], replicated, may hold values from 0 to 95
- tgt_lang: int32 [16], replicated, may hold values from 0 to 95
- lang_embed: float32 [96, 512], P(None, 'pair'), may hold values from -5 to 5
- generator: bfloat16 [512, 524288], P('pair', 'gen'), may hold values from -0.005859375 to 0.005859375
Outputs:
- grad_tokens: bfloat16 [32768, 2048], P(('pair', 'gen'))
- grad_generator: bfloat16 [512, 524288], P('pair', 'gen')
- grad_embed: float32 [96, 512], P(None, 'pair')
Inputs may be any that keep to these rules, and one draw needn't show every extreme that they name: `block_pair`: every pair owns at least one block; block counts per pair are uneven.
All inputs are finite; a program needn't handle non-finite values.
Results may differ from a plain program's by a relative error of at most 0.007.
Values may be sent and summed in bfloat16 or wider, within the bound.
No kernel may reach another device: no remote copies, remote signals or barrier semaphores. Data moves between devices by JAX's collectives and lax.ppermute only.
A program may use at most 128 MiB of HBM per device.

v0:
```python
import jax
import jax.numpy as jnp
from jax import lax
from jax.sharding import PartitionSpec as P

BLK = 1024


def shards(tokens, cotangent, block_pair, src_lang, tgt_lang, lang_embed, generator):
    gen_count = lax.axis_size("gen")
    pair_index = lax.axis_index("pair")
    blocks_here = tokens.shape[0] // BLK
    model_width = tokens.shape[1]
    adapter_rank = cotangent.shape[1]
    languages = lang_embed.shape[0]
    pair_count = src_lang.shape[0]
    lang_ids = jnp.arange(languages, dtype=jnp.int32)
    hot_both = (src_lang[:, None] == lang_ids[None, :]).astype(jnp.float32) + (
        tgt_lang[:, None] == lang_ids[None, :]
    ).astype(jnp.float32)
    pair_embed = jnp.dot(hot_both, lang_embed, precision=lax.Precision.HIGHEST).astype(jnp.bfloat16)
    partial_value = jnp.dot(pair_embed, generator, preferred_element_type=jnp.float32)
    adapter_cols = lax.psum(partial_value, "pair").astype(jnp.bfloat16)
    flat_pairs = block_pair[:, 0]
    row_pairs = lax.dynamic_slice_in_dim(
        flat_pairs, pair_index * (gen_count * blocks_here), gen_count * blocks_here
    )
    send_order = row_pairs.reshape(gen_count, blocks_here).T
    outgoing = jnp.take(adapter_cols, send_order, axis=0).reshape(
        blocks_here, gen_count * adapter_cols.shape[1]
    )
    own_adapters = lax.all_to_all(outgoing, "gen", split_axis=1, concat_axis=1, tiled=True)
    adapters = own_adapters.reshape(blocks_here, model_width, adapter_rank)
    token_blocks = tokens.reshape(blocks_here, BLK, model_width)
    cot_blocks = cotangent.reshape(blocks_here, BLK, adapter_rank)
    hidden = jnp.einsum("btd,bdr->btr", token_blocks, adapters, preferred_element_type=jnp.float32)
    logistic = jax.nn.sigmoid(hidden)
    grad_hidden = (
        cot_blocks.astype(jnp.float32) * logistic * (1.0 + hidden * (1.0 - logistic))
    ).astype(jnp.bfloat16)
    grad_tokens = (
        jnp.einsum("btr,bdr->btd", grad_hidden, adapters, preferred_element_type=jnp.float32)
        .astype(jnp.bfloat16)
        .reshape(tokens.shape)
    )
    outer_grads = jnp.einsum(
        "btd,btr->bdr", token_blocks, grad_hidden, preferred_element_type=jnp.float32
    ).reshape(blocks_here, model_width * adapter_rank)
    returned = lax.all_to_all(outer_grads, "gen", split_axis=1, concat_axis=0, tiled=True)
    pair_ids = jnp.arange(pair_count, dtype=jnp.int32)
    segment_hot = (pair_ids[:, None] == row_pairs[None, :]).astype(jnp.float32)
    row_grad = jnp.dot(segment_hot, returned, precision=lax.Precision.HIGHEST)
    grad_rounded = lax.psum(row_grad, "pair").astype(jnp.bfloat16)
    grad_generator = jnp.einsum(
        "pe,pc->ec", pair_embed, grad_rounded, preferred_element_type=jnp.float32
    ).astype(jnp.bfloat16)
    partial_pair = jnp.einsum(
        "pc,ec->pe", grad_rounded, generator, preferred_element_type=jnp.float32
    )
    grad_pair = lax.psum(partial_pair, "gen")
    grad_embed = jnp.dot(hot_both.T, grad_pair, precision=lax.Precision.HIGHEST)
    return (grad_tokens, grad_generator, grad_embed)


def solution(mesh):
    placed = (
        P(("pair", "gen"), None),
        P(("pair", "gen"), None),
        P(),
        P(),
        P(),
        P(None, "pair"),
        P("pair", "gen"),
    )
    return jax.shard_map(
        shards,
        mesh=mesh,
        in_specs=placed,
        out_specs=(P(("pair", "gen"), None), P("pair", "gen"), P(None, "pair")),
        check_vma=False,
    )
```

profile of v0, /device:TPU:0, one launch (start us, length us, event | category | flops | bytes accessed | tf_op | source)
XLA Modules:
  0.0 421.6 jit_solution(15591775119214140472)
XLA Ops:
  0.6 0.0 copy-start
  0.7 0.7 fusion.16
  1.4 0.7 compare_and_fusion
  2.1 0.0 copy-done
  2.1 0.9 convolution_convert_fusion.2
  3.0 10.1 %fusion.21 = f32[16,65536]{1,0:T(8,128)} fusion(bf16[16,128]{1,0:T(8,128)(2,1)S(1)} %convolution_convert_fusion.2, bf16[128,65536]{1,0:T(8,128)(2,1)} %param.13), kind=kOutput, calls=%fused_computation.39 | convolution fusion | flops 268435456 | bytes 20975616 | tf_op jit(solution)/shard_map/dot_general | solution.py:22
  13.1 149.0 %all-reduce.2 = bf16[16,65536]{1,0:T(8,128)(2,1)S(1)} all-reduce(f32[16,65536]{1,0:T(8,128)} %fusion.21), channel_id=1, replica_groups=mesh['pair'=4,'gen'=8] {'pair'}, use_global_device_ids=true, to_apply=%region_0.0 | all-reduce | flops 1048576 | bytes 6291456 | tf_op jit(solution)/shard_map/psum | solution.py:23
  162.1 1.2 gather_fusion
  163.4 0.2 bitcast_select_fusion
  163.5 1.6 copy.27
  165.2 0.5 broadcast.100
  165.7 7.0 %reduce.2 = bf16[8,65536]{1,0:T(8,128)(2,1)S(1)} reduce(bf16[8,1,65536]{2,1,0:T(2,128)(2,1)S(1)} %bitcast.33, bf16[]{:T(256)} %broadcast.100), dimensions={1}, to_apply=%bitcast.32.reduce_sub_computation | reduce | bytes 2097154
  172.7 0.0 copy-start.4
  172.7 1.9 reshape.166
  174.6 3.8 all-to-all-start
  178.4 0.0 copy-done.4
  178.4 1.0 copy.17
  179.4 14.3 %all-to-all-done = bf16[8,2,32768]{2,1,0:T(2,128)(2,1)S(1)} async-done(((bf16[8,2,32768]{2,1,0:T(2,128)(2,1)}), bf16[8,2,32768]{2,1,0:T(2,128)(2,1)S(1)}, u32[]{:S(2)}, u32[]{:S(2)}) %all-to-all-start) | async-done | bytes 1048608 | tf_op jit(solution)/shard_map/all_to_all | solution.py:32
  193.7 1.0 reshape.167
  194.8 6.0 %bitcast_reduce_fusion = bf16[8,65536]{1,0:T(8,128)(2,1)S(1)} fusion(bf16[8,1,65536]{2,1,0:T(2,128)(2,1)S(1)} %reshape.167), kind=kLoop, calls=%fused_computation.37 | loop fusion | bytes 2097152 | tf_op jit(solution)/shard_map/all_to_all | solution.py:32
  200.8 0.5 reshape.156
  201.2 0.0 copy-start.2
  201.3 0.0 copy-start.5
  201.3 0.0 copy-start.6
  201.3 3.9 convolution_bitcast_fusion.1
  205.2 0.0 copy-done.2
  205.2 0.0 copy-start.9
  205.2 1.0 copy-done.9
  206.2 0.0 copy-done.5
  206.2 0.0 copy-done.6
  206.2 2.9 convolution_bitcast_fusion
  209.0 1.9 copy.19
  211.0 0.0 copy-start.3
  211.0 4.2 all_to_all.20
  215.1 3.9 all-to-all-start.1
  219.0 0.0 copy-done.3
  219.0 5.0 %convolution_convert_fusion.1 = bf16[1024,2048]{1,0:T(8,128)(2,1)} fusion(bf16[2048,256]{1,0:T(8,128)(2,1)S(1)} %copy-done.3, f32[1024,256]{0,1:T(8,128)} %copy-done.9, bf16[1024,256]{0,1:T(8,128)(2,1)} %copy.17), kind=kOutput, calls=%fused_computation.2 | convolution fusion | flops 1078460416 | bytes 6815744 | tf_op jit(solution)/shard_map/btr,bdr->btd/dot_general | solution.py:42
  224.0 21.3 %all-to-all-done.1 = f32[1,8,65536]{2,0,1:T(1,128)S(1)} async-done(((f32[1,8,65536]{2,0,1:T(1,128)}), f32[1,8,65536]{2,0,1:T(1,128)S(1)}, u32[]{:S(2)}, u32[]{:S(2)}) %all-to-all-start.1) | async-done | bytes 2097184 | tf_op jit(solution)/shard_map/all_to_all | solution.py:49
  245.3 4.8 %fusion = f32[16,65536]{1,0:T(8,128)} fusion(f32[1,8,65536]{2,0,1:T(1,128)S(1)} %all-to-all-done.1, s32[8]{0:T(128)S(1)} %get-tuple-element.4), kind=kOutput, calls=%fused_computation.4 | convolution fusion | flops 100663424 | bytes 6291488 | tf_op jit(solution)/shard_map/dot_general | solution.py:52
  250.1 141.2 %all-reduce.3 = bf16[16,65536]{1,0:T(8,128)(2,1)S(1)} all-reduce(f32[16,65536]{1,0:T(8,128)} %fusion), channel_id=1, replica_groups=mesh['pair'=4,'gen'=8] {'pair'}, use_global_device_ids=true, to_apply=%region_1.2 | all-reduce | flops 1048576 | bytes 6291456 | tf_op jit(solution)/shard_map/psum | solution.py:53
  391.4 8.5 %convolution_convert_fusion = bf16[128,65536]{1,0:T(8,128)(2,1)} fusion(bf16[16,128]{1,0:T(8,128)(2,1)S(1)} %convolution_convert_fusion.2, bf16[16,65536]{1,0:T(8,128)(2,1)S(1)} %all-reduce.3), kind=kOutput, calls=%fused_computation.1 | convolution fusion | flops 276824064 | bytes 18878464 | tf_op jit(solution)/shard_map/pe,pc->ec/dot_general | solution.py:54
  399.9 0.0 copy-start.7
  399.9 8.1 %fusion.22 = f32[16,128]{1,0:T(8,128)S(1)} fusion(bf16[16,65536]{1,0:T(8,128)(2,1)S(1)} %all-reduce.3, bf16[128,65536]{1,0:T(8,128)(2,1)} %param.13), kind=kOutput, calls=%fused_computation.40 | convolution fusion | flops 268435456 | bytes 18882560 | tf_op jit(solution)/shard_map/pc,ec->pe/dot_general | solution.py:57
  408.0 12.6 %psum.23 = f32[16,128]{1,0:T(8,128)S(1)} all-reduce(f32[16,128]{1,0:T(8,128)S(1)} %fusion.22), channel_id=1, replica_groups=mesh['pair'=4,'gen'=8] {'gen'}, use_global_device_ids=true, to_apply=%region_2.3 | all-reduce | flops 2048 | bytes 16384 | tf_op jit(solution)/shard_map/psum | solution.py:60
  420.6 0.0 copy-done.7
  420.6 0.0 copy-done.8
  420.6 1.0 fusion.10
  421.6 0.0 copy-done.1
  (3 shorter events, 0.0 us)
Async XLA Ops:
  0.6 1.5 copy-start
  172.7 5.7 %copy-start.4 = (bf16[1024,256]{1,0:T(8,128)(2,1)S(1)}, bf16[1024,256]{1,0:T(8,128)(2,1)}, u32[]{:S(2)}) copy-start(bf16[1024,256]{1,0:T(8,128)(2,1)} %param.8) | copy-start | bytes 1572868
  174.6 19.1 %all-to-all-start = ((bf16[8,2,32768]{2,1,0:T(2,128)(2,1)}), bf16[8,2,32768]{2,1,0:T(2,128)(2,1)S(1)}, u32[]{:S(2)}, u32[]{:S(2)}) async-start(bf16[8,2,32768]{2,1,0:T(2,128)(2,1)} %reshape.166), calls=%async_computation | async-start | bytes 2097152 | tf_op jit(solution)/shard_map/all_to_all | solution.py:32
  201.2 3.9 copy-start.2
  201.3 4.9 %copy-start.5 = (bf16[1024,256]{0,1:T(8,128)(2,1)S(1)}, bf16[1024,256]{0,1:T(8,128)(2,1)}, u32[]{:S(2)}) copy-start(bf16[1024,256]{0,1:T(8,128)(2,1)} %copy.17) | copy-start | bytes 1572868
  201.3 4.9 %copy-start.6 = (bf16[1024,2048]{1,0:T(8,128)(2,1)S(1)}, bf16[1024,2048]{1,0:T(8,128)(2,1)}, u32[]{:S(2)}) copy-start(bf16[1024,2048]{1,0:T(8,128)(2,1)} %param.7) | copy-start | bytes 12582916
  205.2 1.0 copy-start.9
  211.0 8.0 %copy-start.3 = (bf16[2048,256]{1,0:T(8,128)(2,1)S(1)}, bf16[2048,256]{1,0:T(8,128)(2,1)}, u32[]{:S(2)}) copy-start(bf16[2048,256]{1,0:T(8,128)(2,1)} %copy-done.2) | copy-start | bytes 3145732
  215.1 30.2 %all-to-all-start.1 = ((f32[1,8,65536]{2,0,1:T(1,128)}), f32[1,8,65536]{2,0,1:T(1,128)S(1)}, u32[]{:S(2)}, u32[]{:S(2)}) async-start(f32[1,8,65536]{2,0,1:T(1,128)} %all_to_all.20), calls=%async_computation.1 | async-start | bytes 4194304 | tf_op jit(solution)/shard_map/all_to_all | solution.py:49
  399.9 20.7 %copy-start.7 = (s32[16]{0:T(128)S(1)}, s32[16]{0:T(128)}, u32[]{:S(2)}) copy-start(s32[16]{0:T(128)} %param.11) | copy-start | bytes 196
  399.9 20.7 %copy-start.8 = (s32[16]{0:T(128)S(1)}, s32[16]{0:T(128)}, u32[]{:S(2)}) copy-start(s32[16]{0:T(128)} %param.10) | copy-start | bytes 196
  399.9 21.7 %copy-start.1 = (f32[96,128]{1,0:T(8,128)S(1)}, f32[96,128]{1,0:T(8,128)}, u32[]{:S(2)}) copy-start(f32[96,128]{1,0:T(8,128)} %param.12) | copy-start | bytes 147460
where the time goes:
time: 422 us
  blocking collectives  303 us (72%)
  matrix products  45 us (11%)
  waiting for transfers between devices  35.7 us (8%)
  local copies, waits for them, and re-layouts  20.8 us (5%)
  other arithmetic  8.67 us (2%)
  starting transfers between devices  7.64 us (2%)
    psum x1, blocking collectives, shards(): adapter_cols = lax.psum(partial_value, 'pair').astype(jnp.bfloat16)  149 us
    psum x1, blocking collectives, shards(): grad_rounded = lax.psum(row_grad, 'pair').astype(jnp.bfloat16)  141 us
    all_to_all x1, waiting for transfers between devices, shards(): lax.all_to_all(outer_grads, 'gen', split_axis=1, concat_axis=0, tiled=True)  21.3 us
    all_to_all x1, waiting for transfers between devices, shards(): lax.all_to_all(outgoing, 'gen', split_axis=1, concat_axis=1, tiled=True)  14.3 us
    psum x1, blocking collectives, shards(): grad_pair = lax.psum(partial_pair, 'gen')  12.6 us
    dot_general x1, matrix products, shards(): jnp.dot(pair_embed, generator, preferred_element_type=jnp.float32)  10.1 us
    dot_general x1, matrix products, shards(): jnp.einsum('pe,pc->ec', pair_embed, grad_rounded, preferred_element_type=...  8.54 us
  transfers between devices with their start and end apart: 2, of which 2 were waited for; matrix products, arithmetic and copies ran while one was open for 1% of the time, Pallas kernels for 0%

commit v1 on v0

--- a/solution.py
+++ b/solution.py
@@ -8,29 +8,31 @@
 
 def shards(tokens, cotangent, block_pair, src_lang, tgt_lang, lang_embed, generator):
     gen_count = lax.axis_size("gen")
-    pair_index = lax.axis_index("pair")
+    pair_count_axis = lax.axis_size("pair")
     blocks_here = tokens.shape[0] // BLK
     model_width = tokens.shape[1]
     adapter_rank = cotangent.shape[1]
     languages = lang_embed.shape[0]
     pair_count = src_lang.shape[0]
+    chunk = generator.shape[1]
+    quarter = chunk // pair_count_axis
     lang_ids = jnp.arange(languages, dtype=jnp.int32)
     hot_both = (src_lang[:, None] == lang_ids[None, :]).astype(jnp.float32) + (
         tgt_lang[:, None] == lang_ids[None, :]
     ).astype(jnp.float32)
     pair_embed = jnp.dot(hot_both, lang_embed, precision=lax.Precision.HIGHEST).astype(jnp.bfloat16)
     partial_value = jnp.dot(pair_embed, generator, preferred_element_type=jnp.float32)
-    adapter_cols = lax.psum(partial_value, "pair").astype(jnp.bfloat16)
+    adapter_part = lax.psum_scatter(
+        partial_value, "pair", scatter_dimension=1, tiled=True
+    ).astype(jnp.bfloat16)
     flat_pairs = block_pair[:, 0]
-    row_pairs = lax.dynamic_slice_in_dim(
-        flat_pairs, pair_index * (gen_count * blocks_here), gen_count * blocks_here
+    outgoing = jnp.take(adapter_part, flat_pairs, axis=0)
+    incoming = lax.all_to_all(outgoing, ("pair", "gen"), 0, 0, tiled=True)
+    adapters = (
+        incoming.reshape(pair_count_axis, gen_count, quarter)
+        .transpose(1, 0, 2)
+        .reshape(blocks_here, model_width, adapter_rank)
     )
-    send_order = row_pairs.reshape(gen_count, blocks_here).T
-    outgoing = jnp.take(adapter_cols, send_order, axis=0).reshape(
-        blocks_here, gen_count * adapter_cols.shape[1]
-    )
-    own_adapters = lax.all_to_all(outgoing, "gen", split_axis=1, concat_axis=1, tiled=True)
-    adapters = own_adapters.reshape(blocks_here, model_width, adapter_rank)
     token_blocks = tokens.reshape(blocks_here, BLK, model_width)
     cot_blocks = cotangent.reshape(blocks_here, BLK, adapter_rank)
     hidden = jnp.einsum("btd,bdr->btr", token_blocks, adapters, preferred_element_type=jnp.float32)
@@ -45,12 +47,17 @@
     )
     outer_grads = jnp.einsum(
         "btd,btr->bdr", token_blocks, grad_hidden, preferred_element_type=jnp.float32
-    ).reshape(blocks_here, model_width * adapter_rank)
-    returned = lax.all_to_all(outer_grads, "gen", split_axis=1, concat_axis=0, tiled=True)
+    )
+    by_owner = (
+        outer_grads.reshape(gen_count, pair_count_axis, quarter)
+        .transpose(1, 0, 2)
+        .reshape(pair_count_axis * gen_count, quarter)
+    )
+    returned = lax.all_to_all(by_owner, ("pair", "gen"), 0, 0, tiled=True)
     pair_ids = jnp.arange(pair_count, dtype=jnp.int32)
-    segment_hot = (pair_ids[:, None] == row_pairs[None, :]).astype(jnp.float32)
-    row_grad = jnp.dot(segment_hot, returned, precision=lax.Precision.HIGHEST)
-    grad_rounded = lax.psum(row_grad, "pair").astype(jnp.bfloat16)
+    segment_hot = (pair_ids[:, None] == flat_pairs[None, :]).astype(jnp.float32)
+    row_grad = jnp.dot(segment_hot, returned, precision=lax.Precision.HIGHEST).astype(jnp.bfloat16)
+    grad_rounded = lax.all_gather(row_grad, "pair", axis=1, tiled=True)
     grad_generator = jnp.einsum(
         "pe,pc->ec", pair_embed, grad_rounded, preferred_element_type=jnp.float32
     ).astype(jnp.bfloat16)

time: 422 us -> 298 us (0.71)
  blocking collectives: 303 us -> 65.9 us
  waiting for transfers between devices: 35.7 us -> 146 us
  between operations: 0.86 us -> 14.2 us
  other arithmetic: 8.67 us -> 2.9 us
    psum x2 -> x0, blocking collectives: 290 us -> none  [the longest x1 149 us: shards(): adapter_cols = lax.psum(partial_value, 'pair').astype(jnp.bfloat16)]
    reduce_scatter x0 -> x1, waiting for transfers between devices: none -> 79 us  [shards(): lax.psum_scatter(partial_value, 'pair', scatter_dimension=1, tiled=True)]
    all_to_all x0 -> x1, blocking collectives: none -> 52.1 us  [shards(): returned = lax.all_to_all(by_owner, ('pair', 'gen'), 0, 0, tiled=True)]
    all_gather x0 -> x1, waiting for transfers between devices: none -> 41.5 us  [shards(): grad_rounded = lax.all_gather(row_grad, 'pair', axis=1, tiled=True)]
    all_to_all x2 -> x1, waiting for transfers between devices: 35.7 us -> 25 us  [shards(): incoming = lax.all_to_all(outgoing, ('pair', 'gen'), 0, 0, tiled=True)]
    all_to_all x2 -> x1, local copies, waits for them, and re-layouts: 10.2 us -> 2.16 us  [shards(): returned = lax.all_to_all(by_owner, ('pair', 'gen'), 0, 0, tiled=True)]
    unnamed x1 -> x0, other arithmetic: 7.03 us -> none
  transfers between devices with their start and end apart: 2 -> 3, of which waited for: 2 -> 3; matrix products, arithmetic and copies ran while one was open for 1% -> 2% of each run, Pallas kernels for 0% -> 0%
where the time goes in v1:
time: 298 us
  waiting for transfers between devices  146 us (49%)
  blocking collectives  65.9 us (22%)
  matrix products  44.3 us (15%)
  local copies, waits for them, and re-layouts  19.4 us (7%)
  between operations  14.2 us (5%)
  starting transfers between devices  5.37 us (2%)
    reduce_scatter x1, waiting for transfers between devices, shards(): lax.psum_scatter(partial_value, 'pair', scatter_dimension=1, tiled=True)  79 us
    all_to_all x1, blocking collectives, shards(): returned = lax.all_to_all(by_owner, ('pair', 'gen'), 0, 0, tiled=True)  52.1 us
    all_gather x1, waiting for transfers between devices, shards(): grad_rounded = lax.all_gather(row_grad, 'pair', axis=1, tiled=True)  41.5 us
    all_to_all x1, waiting for transfers between devices, shards(): incoming = lax.all_to_all(outgoing, ('pair', 'gen'), 0, 0, tiled=True)  25 us
    psum x1, blocking collectives, shards(): grad_pair = lax.psum(partial_pair, 'gen')  13.8 us
    dot_general x1, matrix products, shards(): jnp.einsum('pc,ec->pe', grad_rounded, generator, preferred_element_type=j...  11 us
    dot_general x1, matrix products, shards(): jnp.dot(pair_embed, generator, preferred_element_type=jnp.float32)  10.1 us
    dot_general x1, matrix products, shards(): jnp.einsum('pe,pc->ec', pair_embed, grad_rounded, preferred_element_type=...  8.52 us
  transfers between devices with their start and end apart: 3, of which 3 were waited for; matrix products, arithmetic and copies ran while one was open for 2% of the time, Pallas kernels for 0%

profile of v1, /device:TPU:0, one launch (start us, length us, event | category | flops | bytes accessed | tf_op | source)
XLA Modules:
  0.0 297.6 jit_solution(7529678986350545936)
XLA Ops:
  7.2 0.0 copy-start
  7.2 0.0 reduce-scatter.2.cloned.1.call-start
  7.2 0.7 copy-done
  8.0 0.9 convolution_convert_fusion.3
  8.8 10.1 %fusion.15 = f32[16,65536]{1,0:T(8,128)} fusion(bf16[16,128]{1,0:T(8,128)(2,1)S(1)} %convolution_convert_fusion.3, bf16[128,65536]{1,0:T(8,128)(2,1)} %param.13), kind=kOutput, calls=%fused_computation.33 | convolution fusion | flops 268435456 | bytes 20975616 | tf_op jit(solution)/shard_map/dot_general | solution.py:24
  18.9 0.0 reduce-scatter.2.cloned.1.call-update
  19.0 0.6 copy-done.6
  19.6 79.0 %reduce-scatter.2.cloned.1.call-done = f32[16,16384]{1,0:T(8,128)} async-done(((f32[16,65536]{1,0:T(8,128)}), f32[16,16384]{1,0:T(8,128)}) %reduce-scatter.2.cloned.1.call-update) | async-done | bytes 1048592 | tf_op jit(solution)/shard_map/reduce_scatter | solution.py:25
  98.6 1.3 convert_element_type.35
  99.9 1.2 gather_fusion
  101.1 0.0 copy-start.3
  101.1 0.2 bitcast_select_fusion
  101.3 0.5 broadcast.56
  101.8 1.4 reduce
  103.2 1.6 reshape.103
  104.8 5.1 %all-to-all-start = ((bf16[32,2,8192]{2,1,0:T(2,128)(2,1)}), bf16[32,2,8192]{2,1,0:T(2,128)(2,1)S(1)}, u32[]{:S(2)}, u32[]{:S(2)}) async-start(bf16[32,2,8192]{2,1,0:T(2,128)(2,1)} %reshape.103), calls=%async_computation.1 | async-start | bytes 2097152 | tf_op jit(solution)/shard_map/all_to_all | solution.py:30
  109.9 0.2 all-gather.2.cloned.1.call-start
  110.2 0.0 copy-done.3
  110.2 1.0 copy.21
  111.2 25.0 %all-to-all-done = bf16[32,2,8192]{2,1,0:T(2,128)(2,1)S(1)} async-done(((bf16[32,2,8192]{2,1,0:T(2,128)(2,1)}), bf16[32,2,8192]{2,1,0:T(2,128)(2,1)S(1)}, u32[]{:S(2)}, u32[]{:S(2)}) %all-to-all-start) | async-done | bytes 1048608 | tf_op jit(solution)/shard_map/all_to_all | solution.py:30
  136.2 1.0 reshape.104
  137.2 1.2 copy.36
  138.4 0.8 copy.23
  139.2 0.8 reshape.93
  139.9 0.0 copy-start.4
  140.0 0.0 copy-start.7
  140.0 3.6 %convolution_bitcast_fusion.1 = f32[1024,256]{0,1:T(8,128)S(1)} fusion(bf16[2048,256]{1,0:T(8,128)(2,1)S(1)} %reshape.93, bf16[1024,2048]{1,0:T(8,128)(2,1)} %param.7), kind=kOutput, calls=%fused_computation.8 | convolution fusion | flops 1073741824 | bytes 6291456 | tf_op jit(solution)/shard_map/btd,bdr->btr/dot_general | solution.py:38
  143.6 0.0 copy-start.10
  143.6 1.0 copy-done.10
  144.6 0.0 copy-done.7
  144.6 2.8 convolution_bitcast_fusion
  147.4 1.9 copy.24
  149.4 2.0 reshape.94
  151.4 2.8 copy.35
  154.2 2.2 copy.26
  156.4 0.0 copy-start.5
  156.4 0.0 copy-start.11
  156.4 52.1 %all_to_all.18 = f32[32,1,16384]{2,1,0:T(1,128)S(1)} all-to-all(f32[32,1,16384]{2,1,0:T(1,128)S(1)} %copy.26), channel_id=1, replica_groups=mesh['pair'=4,'gen'=8] {'pair','gen'}, dimensions={0} | all-to-all | bytes 4194304 | tf_op jit(solution)/shard_map/all_to_all | solution.py:56
  208.5 2.8 convolution_convert_fusion.1
  211.3 0.0 all-gather.2.cloned.1.call-update
  211.3 3.6 %convolution_convert_fusion.2 = bf16[1024,2048]{1,0:T(8,128)(2,1)} fusion(bf16[2048,256]{1,0:T(8,128)(2,1)S(1)} %reshape.93, f32[1024,256]{0,1:T(8,128)S(1)} %copy-done.11, bf16[1024,256]{0,1:T(8,128)(2,1)S(1)} %copy-done.5), kind=kOutput, calls=%fused_computation.3 | convolution fusion | flops 1078460416 | bytes 6815744 | tf_op jit(solution)/shard_map/btr,bdr->btd/dot_general | solution.py:44
  215.0 41.5 %all-gather.2.cloned.1.call-done = bf16[16,65536]{1,0:T(8,128)(2,1)} async-done(((bf16[16,16384]{1,0:T(8,128)(2,1)}), bf16[16,65536]{1,0:T(8,128)(2,1)}) %all-gather.2.cloned.1.call-update) | async-done | bytes 2097168 | tf_op jit(solution)/shard_map/all_gather | solution.py:60
  256.5 11.0 %fusion.16 = f32[16,128]{1,0:T(8,128)S(1)} fusion(bf16[16,65536]{1,0:T(8,128)(2,1)} %all-gather.2.cloned.1.call-done, bf16[128,65536]{1,0:T(8,128)(2,1)} %param.13), kind=kOutput, calls=%fused_computation.34 | convolution fusion | flops 268435456 | bytes 18882560 | tf_op jit(solution)/shard_map/pc,ec->pe/dot_general | solution.py:64
  267.5 13.8 %psum.7 = f32[16,128]{1,0:T(8,128)S(1)} all-reduce(f32[16,128]{1,0:T(8,128)S(1)} %fusion.16), channel_id=1, replica_groups=mesh['pair'=4,'gen'=8] {'gen'}, use_global_device_ids=true, to_apply=%region_1.2 | all-reduce | flops 2048 | bytes 16384 | tf_op jit(solution)/shard_map/psum | solution.py:67
  281.3 0.0 copy-done.8
  281.3 0.0 copy-done.9
  281.3 1.0 fusion.6
  282.3 8.5 %convolution_convert_fusion = bf16[128,65536]{1,0:T(8,128)(2,1)} fusion(bf16[16,128]{1,0:T(8,128)(2,1)S(1)} %convolution_convert_fusion.3, bf16[16,65536]{1,0:T(8,128)(2,1)S(1)} %copy-done.2), kind=kOutput, calls=%fused_computation.1 | convolution fusion | flops 276824064 | bytes 18878464 | tf_op jit(solution)/shard_map/pe,pc->ec/dot_general | solution.py:61
  (13 shorter events, 0.0 us)
Async XLA Ops:
  7.2 0.8 copy-start
  7.2 91.4 %reduce-scatter.2.cloned.1.call-start = ((), (), s32[]{:S(2)}) async-start(), calls=%async_computation.3 | async-start | bytes 5242880 | tf_op jit(solution)/shard_map/reduce_scatter | solution.py:25
  18.9 0.7 copy-start.6
  101.1 9.1 %copy-start.3 = (bf16[1024,256]{1,0:T(8,128)(2,1)S(1)}, bf16[1024,256]{1,0:T(8,128)(2,1)}, u32[]{:S(2)}) copy-start(bf16[1024,256]{1,0:T(8,128)(2,1)} %param.8) | copy-start | bytes 1572868
  104.8 31.4 %all-to-all-start = ((bf16[32,2,8192]{2,1,0:T(2,128)(2,1)}), bf16[32,2,8192]{2,1,0:T(2,128)(2,1)S(1)}, u32[]{:S(2)}, u32[]{:S(2)}) async-start(bf16[32,2,8192]{2,1,0:T(2,128)(2,1)} %reshape.103), calls=%async_computation.1 | async-start | bytes 2097152 | tf_op jit(solution)/shard_map/all_to_all | solution.py:30
  109.9 146.6 %all-gather.2.cloned.1.call-start = ((), (), s32[]{:S(2)}) async-start(), calls=%async_computation.4 | async-start | bytes 2621440 | tf_op jit(solution)/shard_map/all_gather | solution.py:60
  139.9 4.6 %copy-start.4 = (bf16[1024,256]{0,1:T(8,128)(2,1)S(1)}, bf16[1024,256]{0,1:T(8,128)(2,1)}, u32[]{:S(2)}) copy-start(bf16[1024,256]{0,1:T(8,128)(2,1)} %copy.21) | copy-start | bytes 1572868
  140.0 4.6 %copy-start.7 = (bf16[1024,2048]{1,0:T(8,128)(2,1)S(1)}, bf16[1024,2048]{1,0:T(8,128)(2,1)}, u32[]{:S(2)}) copy-start(bf16[1024,2048]{1,0:T(8,128)(2,1)} %param.7) | copy-start | bytes 12582916
  143.6 1.0 copy-start.10
  156.4 55.0 %copy-start.5 = (bf16[1024,256]{0,1:T(8,128)(2,1)S(1)}, bf16[1024,256]{0,1:T(8,128)(2,1)}, u32[]{:S(2)}) copy-start(bf16[1024,256]{0,1:T(8,128)(2,1)} %copy.21) | copy-start | bytes 1572868
  156.4 55.0 %copy-start.11 = (f32[1024,256]{0,1:T(8,128)S(1)}, f32[1024,256]{0,1:T(8,128)}, u32[]{:S(2)}) copy-start(f32[1024,256]{0,1:T(8,128)} %copy-done.10) | copy-start | bytes 3145732
  215.0 66.3 %copy-start.8 = (s32[16]{0:T(128)S(1)}, s32[16]{0:T(128)}, u32[]{:S(2)}) copy-start(s32[16]{0:T(128)} %param.11) | copy-start | bytes 196
  215.0 66.3 %copy-start.9 = (s32[16]{0:T(128)S(1)}, s32[16]{0:T(128)}, u32[]{:S(2)}) copy-start(s32[16]{0:T(128)} %param.10) | copy-start | bytes 196
  256.5 25.8 %copy-start.2 = (bf16[16,65536]{1,0:T(8,128)(2,1)S(1)}, bf16[16,65536]{1,0:T(8,128)(2,1)}, u32[]{:S(2)}) copy-start(bf16[16,65536]{1,0:T(8,128)(2,1)} %all-gather.2.cloned.1.call-done) | copy-start | bytes 6291460
  282.3 8.5 %copy-start.1 = (f32[96,128]{1,0:T(8,128)S(1)}, f32[96,128]{1,0:T(8,128)}, u32[]{:S(2)}) copy-start(f32[96,128]{1,0:T(8,128)} %param.12) | copy-start | bytes 147460
Sparse Core Ops, SparseCore 0:
  19.1 79.4 reduce-scatter.1
  211.4 44.9 all-gather.1

commit v2 on v1

--- a/solution.py
+++ b/solution.py
@@ -23,8 +23,8 @@
     pair_embed = jnp.dot(hot_both, lang_embed, precision=lax.Precision.HIGHEST).astype(jnp.bfloat16)
     partial_value = jnp.dot(pair_embed, generator, preferred_element_type=jnp.float32)
     adapter_part = lax.psum_scatter(
-        partial_value, "pair", scatter_dimension=1, tiled=True
-    ).astype(jnp.bfloat16)
+        partial_value.astype(jnp.bfloat16), "pair", scatter_dimension=1, tiled=True
+    )
     flat_pairs = block_pair[:, 0]
     outgoing = jnp.take(adapter_part, flat_pairs, axis=0)
     incoming = lax.all_to_all(outgoing, ("pair", "gen"), 0, 0, tiled=True)
@@ -52,11 +52,12 @@
         outer_grads.reshape(gen_count, pair_count_axis, quarter)
         .transpose(1, 0, 2)
         .reshape(pair_count_axis * gen_count, quarter)
+        .astype(jnp.bfloat16)
     )
     returned = lax.all_to_all(by_owner, ("pair", "gen"), 0, 0, tiled=True)
     pair_ids = jnp.arange(pair_count, dtype=jnp.int32)
     segment_hot = (pair_ids[:, None] == flat_pairs[None, :]).astype(jnp.float32)
-    row_grad = jnp.dot(segment_hot, returned, precision=lax.Precision.HIGHEST).astype(jnp.bfloat16)
+    row_grad = jnp.dot(segment_hot, returned.astype(jnp.float32), precision=lax.Precision.HIGHEST).astype(jnp.bfloat16)
     grad_rounded = lax.all_gather(row_grad, "pair", axis=1, tiled=True)
     grad_generator = jnp.einsum(
         "pe,pc->ec", pair_embed, grad_rounded, preferred_element_type=jnp.float32

time: 298 us -> 236 us (0.79)
  waiting for transfers between devices: 146 us -> 111 us
  blocking collectives: 65.9 us -> 43.5 us
  local copies, waits for them, and re-layouts: 19.4 us -> 15.6 us
    reduce_scatter x1, waiting for transfers between devices: 79 us -> 46.7 us  [shards(): lax.psum_scatter(partial_value.astype(jnp.bfloat16), 'pair', scatter_dime...]
    all_to_all x1, blocking collectives: 52.1 us -> 29.7 us  [shards(): returned = lax.all_to_all(by_owner, ('pair', 'gen'), 0, 0, tiled=True)]
  transfers between devices with their start and end apart: 3 -> 3, of which waited for: 3 -> 3; matrix products, arithmetic and copies ran while one was open for 2% -> 3% of each run, Pallas kernels for 0% -> 0%
where the time goes in v2:
time: 236 us
  waiting for transfers between devices  111 us (47%)
  blocking collectives  43.5 us (18%)
  matrix products  43.4 us (18%)
  local copies, waits for them, and re-layouts  15.6 us (7%)
  between operations  14.3 us (6%)
  starting transfers between devices  4.17 us (2%)
  other arithmetic  3.07 us (1%)
    reduce_scatter x1, waiting for transfers between devices, shards(): lax.psum_scatter(partial_value.astype(jnp.bfloat16), 'pair', scatter_dime...  46.7 us
    all_gather x1, waiting for transfers between devices, shards(): grad_rounded = lax.all_gather(row_grad, 'pair', axis=1, tiled=True)  39.8 us
    all_to_all x1, blocking collectives, shards(): returned = lax.all_to_all(by_owner, ('pair', 'gen'), 0, 0, tiled=True)  29.7 us
    all_to_all x1, waiting for transfers between devices, shards(): incoming = lax.all_to_all(outgoing, ('pair', 'gen'), 0, 0, tiled=True)  25 us
    psum x1, blocking collectives, shards(): grad_pair = lax.psum(partial_pair, 'gen')  13.8 us
    dot_general x1, matrix products, shards(): jnp.einsum('pc,ec->pe', grad_rounded, generator, preferred_element_type=j...  11 us
    dot_general x1, matrix products, shards(): jnp.dot(pair_embed, generator, preferred_element_type=jnp.float32)  9.4 us
    dot_general x1, matrix products, shards(): jnp.einsum('pe,pc->ec', pair_embed, grad_rounded, preferred_element_type=...  8.52 us
  transfers between devices with their start and end apart: 3, of which 3 were waited for; matrix products, arithmetic and copies ran while one was open for 3% of the time, Pallas kernels for 0%

profile of v2, /device:TPU:0, one launch (start us, length us, event | category | flops | bytes accessed | tf_op | source)
XLA Modules:
  0.0 235.5 jit_solution(6820055431846227179)
XLA Ops:
  7.2 0.0 copy-start
  7.2 0.0 reduce-scatter.2.cloned.1.call-start
  7.2 0.7 copy-done
  8.0 0.9 convolution_convert_fusion.5
  8.8 0.0 copy-start.6
  8.9 9.4 %convolution_convert_fusion.1 = bf16[16,65536]{1,0:T(8,128)(2,1)} fusion(bf16[16,128]{1,0:T(8,128)(2,1)S(1)} %convolution_convert_fusion.5, bf16[128,65536]{1,0:T(8,128)(2,1)} %param.13), kind=kOutput, calls=%fused_computation.2 | convolution fusion | flops 269484032 | bytes 18878464 | tf_op jit(solution)/shard_map/dot_general | solution.py:24
  18.3 0.0 reduce-scatter.2.cloned.1.call-update
  18.3 0.0 copy-done.6
  18.3 46.7 %reduce-scatter.2.cloned.1.call-done = bf16[16,16384]{1,0:T(8,128)(2,1)} async-done(((bf16[16,65536]{1,0:T(8,128)(2,1)}), bf16[16,16384]{1,0:T(8,128)(2,1)}) %reduce-scatter.2.cloned.1.call-update) | async-done | bytes 524304 | tf_op jit(solution)/shard_map/reduce_scatter | solution.py:25
  65.0 3.2 %gather_fusion = bf16[32,16384]{1,0:T(8,128)(2,1)S(1)} fusion(bf16[16,16384]{1,0:T(8,128)(2,1)} %reduce-scatter.2.cloned.1.call-done, s32[1024]{0:T(1024)S(1)} %pad_clamp_fusion), kind=kCustom, calls=%fused_computation | custom fusion | bytes 2097280 | tf_op jit(solution)/shard_map/jit(_take)/gather | solution.py:29
  68.2 0.0 copy-start.4
  68.3 0.2 bitcast_select_fusion
  68.4 0.5 broadcast.56
  68.9 1.4 reduce
  70.4 1.6 reshape.111
  72.0 3.9 %all-to-all-start = ((bf16[32,2,8192]{2,1,0:T(2,128)(2,1)}), bf16[32,2,8192]{2,1,0:T(2,128)(2,1)S(1)}, u32[]{:S(2)}, u32[]{:S(2)}) async-start(bf16[32,2,8192]{2,1,0:T(2,128)(2,1)} %reshape.111), calls=%async_computation.1 | async-start | bytes 2097152 | tf_op jit(solution)/shard_map/all_to_all | solution.py:30
  75.9 0.2 all-gather.2.cloned.1.call-start
  76.1 0.0 copy-done.4
  76.1 1.0 copy.21
  77.1 25.0 %all-to-all-done = bf16[32,2,8192]{2,1,0:T(2,128)(2,1)S(1)} async-done(((bf16[32,2,8192]{2,1,0:T(2,128)(2,1)}), bf16[32,2,8192]{2,1,0:T(2,128)(2,1)S(1)}, u32[]{:S(2)}, u32[]{:S(2)}) %all-to-all-start) | async-done | bytes 1048608 | tf_op jit(solution)/shard_map/all_to_all | solution.py:30
  102.1 1.0 reshape.112
  103.2 1.2 copy.35
  104.3 0.8 copy.23
  105.1 0.8 reshape.102
  105.9 0.0 copy-start.3
  105.9 0.0 copy-start.5
  105.9 0.0 copy-start.7
  105.9 3.9 %convolution_bitcast_fusion = f32[1024,256]{0,1:T(8,128)S(1)} fusion(bf16[2048,256]{1,0:T(8,128)(2,1)S(1)} %reshape.102, bf16[1024,2048]{1,0:T(8,128)(2,1)} %param.7), kind=kOutput, calls=%fused_computation.7 | convolution fusion | flops 1073741824 | bytes 6291456 | tf_op jit(solution)/shard_map/btd,bdr->btr/dot_general | solution.py:38
  109.8 0.0 copy-start.10
  109.9 1.0 copy-done.10
  110.8 0.0 copy-done.5
  110.8 0.0 copy-done.7
  110.8 1.5 fusion
  112.3 0.5 copy.24
  112.9 0.8 convert_element_type.63
  113.7 0.6 copy.36
  114.3 1.4 reduce.1
  115.7 0.8 reshape.113
  116.5 29.7 %all_to_all.15 = bf16[32,2,8192]{2,1,0:T(2,128)(2,1)S(1)} all-to-all(bf16[32,2,8192]{2,1,0:T(2,128)(2,1)S(1)} %reshape.113), channel_id=1, replica_groups=mesh['pair'=4,'gen'=8] {'pair','gen'}, dimensions={0} | all-to-all | bytes 2097152 | tf_op jit(solution)/shard_map/all_to_all | solution.py:57
  146.2 1.0 reshape.114
  147.3 2.0 convolution_convert_fusion.2
  149.3 0.0 all-gather.2.cloned.1.call-update
  149.3 5.3 %convolution_convert_fusion.3 = bf16[1024,2048]{1,0:T(8,128)(2,1)} fusion(bf16[2048,256]{1,0:T(8,128)(2,1)} %copy-done.3, f32[1024,256]{0,1:T(8,128)} %copy-done.10, bf16[1024,256]{0,1:T(8,128)(2,1)} %copy.21), kind=kOutput, calls=%fused_computation.4 | convolution fusion | flops 1078460416 | bytes 6815744 | tf_op jit(solution)/shard_map/btr,bdr->btd/dot_general | solution.py:44
  154.6 39.8 %all-gather.2.cloned.1.call-done = bf16[16,65536]{1,0:T(8,128)(2,1)} async-done(((bf16[16,16384]{1,0:T(8,128)(2,1)}), bf16[16,65536]{1,0:T(8,128)(2,1)}) %all-gather.2.cloned.1.call-update) | async-done | bytes 2097168 | tf_op jit(solution)/shard_map/all_gather | solution.py:61
  194.4 11.0 %fusion.16 = f32[16,128]{1,0:T(8,128)S(1)} fusion(bf16[16,65536]{1,0:T(8,128)(2,1)} %all-gather.2.cloned.1.call-done, bf16[128,65536]{1,0:T(8,128)(2,1)} %param.13), kind=kOutput, calls=%fused_computation.35 | convolution fusion | flops 268435456 | bytes 18882560 | tf_op jit(solution)/shard_map/pc,ec->pe/dot_general | solution.py:65
  205.4 13.8 %psum.7 = f32[16,128]{1,0:T(8,128)S(1)} all-reduce(f32[16,128]{1,0:T(8,128)S(1)} %fusion.16), channel_id=1, replica_groups=mesh['pair'=4,'gen'=8] {'gen'}, use_global_device_ids=true, to_apply=%region_1.2 | all-reduce | flops 2048 | bytes 16384 | tf_op jit(solution)/shard_map/psum | solution.py:68
  219.2 1.0 fusion.7
  220.2 8.5 %convolution_convert_fusion = bf16[128,65536]{1,0:T(8,128)(2,1)} fusion(bf16[16,128]{1,0:T(8,128)(2,1)S(1)} %convolution_convert_fusion.5, bf16[16,65536]{1,0:T(8,128)(2,1)S(1)} %copy-done.2), kind=kOutput, calls=%fused_computation.1 | convolution fusion | flops 276824064 | bytes 18878464 | tf_op jit(solution)/shard_map/pe,pc->ec/dot_general | solution.py:62
  (12 shorter events, 0.0 us)
Async XLA Ops:
  7.2 0.8 copy-start
  7.2 57.8 %reduce-scatter.2.cloned.1.call-start = ((), (), s32[]{:S(2)}) async-start(), calls=%async_computation.3 | async-start | bytes 2621440 | tf_op jit(solution)/shard_map/reduce_scatter | solution.py:25
  8.8 9.4 %copy-start.6 = (s32[32,1]{0,1:T(1,128)S(1)}, s32[32,1]{0,1:T(1,128)}, u32[]{:S(2)}) copy-start(s32[32,1]{0,1:T(1,128)} %param.9) | copy-start | bytes 388
  68.2 7.9 %copy-start.4 = (bf16[1024,256]{1,0:T(8,128)(2,1)S(1)}, bf16[1024,256]{1,0:T(8,128)(2,1)}, u32[]{:S(2)}) copy-start(bf16[1024,256]{1,0:T(8,128)(2,1)} %param.8) | copy-start | bytes 1572868
  72.0 30.1 %all-to-all-start = ((bf16[32,2,8192]{2,1,0:T(2,128)(2,1)}), bf16[32,2,8192]{2,1,0:T(2,128)(2,1)S(1)}, u32[]{:S(2)}, u32[]{:S(2)}) async-start(bf16[32,2,8192]{2,1,0:T(2,128)(2,1)} %reshape.111), calls=%async_computation.1 | async-start | bytes 2097152 | tf_op jit(solution)/shard_map/all_to_all | solution.py:30
  75.9 118.5 %all-gather.2.cloned.1.call-start = ((), (), s32[]{:S(2)}) async-start(), calls=%async_computation.4 | async-start | bytes 2621440 | tf_op jit(solution)/shard_map/all_gather | solution.py:61
  105.9 6.4 %copy-start.3 = (bf16[2048,256]{1,0:T(8,128)(2,1)}, bf16[2048,256]{1,0:T(8,128)(2,1)S(1)}, u32[]{:S(2)}) copy-start(bf16[2048,256]{1,0:T(8,128)(2,1)S(1)} %reshape.102) | copy-start | bytes 3145732
  105.9 4.9 %copy-start.5 = (bf16[1024,256]{0,1:T(8,128)(2,1)S(1)}, bf16[1024,256]{0,1:T(8,128)(2,1)}, u32[]{:S(2)}) copy-start(bf16[1024,256]{0,1:T(8,128)(2,1)} %copy.21) | copy-start | bytes 1572868
  105.9 4.9 %copy-start.7 = (bf16[1024,2048]{1,0:T(8,128)(2,1)S(1)}, bf16[1024,2048]{1,0:T(8,128)(2,1)}, u32[]{:S(2)}) copy-start(bf16[1024,2048]{1,0:T(8,128)(2,1)} %param.7) | copy-start | bytes 12582916
  109.8 1.0 copy-start.10
  154.6 64.6 %copy-start.8 = (s32[16]{0:T(128)S(1)}, s32[16]{0:T(128)}, u32[]{:S(2)}) copy-start(s32[16]{0:T(128)} %param.11) | copy-start | bytes 196
  154.6 64.6 %copy-start.9 = (s32[16]{0:T(128)S(1)}, s32[16]{0:T(128)}, u32[]{:S(2)}) copy-start(s32[16]{0:T(128)} %param.10) | copy-start | bytes 196
  194.4 25.8 %copy-start.2 = (bf16[16,65536]{1,0:T(8,128)(2,1)S(1)}, bf16[16,65536]{1,0:T(8,128)(2,1)}, u32[]{:S(2)}) copy-start(bf16[16,65536]{1,0:T(8,128)(2,1)} %all-gather.2.cloned.1.call-done) | copy-start | bytes 6291460
  220.2 8.5 %copy-start.1 = (f32[96,128]{1,0:T(8,128)S(1)}, f32[96,128]{1,0:T(8,128)}, u32[]{:S(2)}) copy-start(f32[96,128]{1,0:T(8,128)} %param.12) | copy-start | bytes 147460
Sparse Core Ops, SparseCore 0:
  18.4 46.5 reduce-scatter.1
  149.4 44.9 all-gather.1

commit v3 on v1

--- a/solution.py
+++ b/solution.py
@@ -52,11 +52,12 @@
         outer_grads.reshape(gen_count, pair_count_axis, quarter)
         .transpose(1, 0, 2)
         .reshape(pair_count_axis * gen_count, quarter)
+        .astype(jnp.bfloat16)
     )
     returned = lax.all_to_all(by_owner, ("pair", "gen"), 0, 0, tiled=True)
     pair_ids = jnp.arange(pair_count, dtype=jnp.int32)
     segment_hot = (pair_ids[:, None] == flat_pairs[None, :]).astype(jnp.float32)
-    row_grad = jnp.dot(segment_hot, returned, precision=lax.Precision.HIGHEST).astype(jnp.bfloat16)
+    row_grad = jnp.dot(segment_hot, returned.astype(jnp.float32), precision=lax.Precision.HIGHEST).astype(jnp.bfloat16)
     grad_rounded = lax.all_gather(row_grad, "pair", axis=1, tiled=True)
     grad_generator = jnp.einsum(
         "pe,pc->ec", pair_embed, grad_rounded, preferred_element_type=jnp.float32

time: 298 us -> 270 us (0.906)
  blocking collectives: 65.9 us -> 43.5 us
  local copies, waits for them, and re-layouts: 19.4 us -> 14.2 us
    all_to_all x1, blocking collectives: 52.1 us -> 29.7 us  [shards(): returned = lax.all_to_all(by_owner, ('pair', 'gen'), 0, 0, tiled=True)]
where the time goes in v3:
time: 270 us
  waiting for transfers between devices  144 us (53%)
  matrix products  44.1 us (16%)
  blocking collectives  43.5 us (16%)
  between operations  14.3 us (5%)
  local copies, waits for them, and re-layouts  14.2 us (5%)
  starting transfers between devices  5.19 us (2%)
  other arithmetic  4.35 us (2%)
    reduce_scatter x1, waiting for transfers between devices, shards(): lax.psum_scatter(partial_value, 'pair', scatter_dimension=1, tiled=True)  79 us
    all_gather x1, waiting for transfers between devices, shards(): grad_rounded = lax.all_gather(row_grad, 'pair', axis=1, tiled=True)  39.8 us
    all_to_all x1, blocking collectives, shards(): returned = lax.all_to_all(by_owner, ('pair', 'gen'), 0, 0, tiled=True)  29.7 us
    all_to_all x1, waiting for transfers between devices, shards(): incoming = lax.all_to_all(outgoing, ('pair', 'gen'), 0, 0, tiled=True)  25.2 us
    psum x1, blocking collectives, shards(): grad_pair = lax.psum(partial_pair, 'gen')  13.8 us
    dot_general x1, matrix products, shards(): jnp.einsum('pc,ec->pe', grad_rounded, generator, preferred_element_type=j...  11 us
    dot_general x1, matrix products, shards(): jnp.dot(pair_embed, generator, preferred_element_type=jnp.float32)  10.1 us
    unnamed x28, local copies, waits for them, and re-layouts  9.01 us
  transfers between devices with their start and end apart: 3, of which 3 were waited for; matrix products, arithmetic and copies ran while one was open for 2% of the time, Pallas kernels for 0%

profile of v3, /device:TPU:0, one launch (start us, length us, event | category | flops | bytes accessed | tf_op | source)
XLA Modules:
  0.0 269.5 jit_solution(1686576194820628183)
XLA Ops:
  7.2 0.0 copy-start
  7.2 0.0 reduce-scatter.2.cloned.1.call-start
  7.2 0.7 copy-done
  8.0 0.9 convolution_convert_fusion.4
  8.8 10.1 %fusion.16 = f32[16,65536]{1,0:T(8,128)} fusion(bf16[16,128]{1,0:T(8,128)(2,1)S(1)} %convolution_convert_fusion.4, bf16[128,65536]{1,0:T(8,128)(2,1)} %param.13), kind=kOutput, calls=%fused_computation.34 | convolution fusion | flops 268435456 | bytes 20975616 | tf_op jit(solution)/shard_map/dot_general | solution.py:24
  18.9 0.0 reduce-scatter.2.cloned.1.call-update
  19.0 0.6 copy-done.6
  19.6 79.0 %reduce-scatter.2.cloned.1.call-done = f32[16,16384]{1,0:T(8,128)} async-done(((f32[16,65536]{1,0:T(8,128)}), f32[16,16384]{1,0:T(8,128)}) %reduce-scatter.2.cloned.1.call-update) | async-done | bytes 1048592 | tf_op jit(solution)/shard_map/reduce_scatter | solution.py:25
  98.6 1.3 convert_element_type.58
  99.9 1.2 gather_fusion
  101.1 0.0 copy-start.4
  101.1 0.2 bitcast_select_fusion
  101.3 0.5 broadcast.56
  101.8 1.4 reduce
  103.2 1.6 reshape.111
  104.8 5.1 %all-to-all-start = ((bf16[32,2,8192]{2,1,0:T(2,128)(2,1)}), bf16[32,2,8192]{2,1,0:T(2,128)(2,1)S(1)}, u32[]{:S(2)}, u32[]{:S(2)}) async-start(bf16[32,2,8192]{2,1,0:T(2,128)(2,1)} %reshape.111), calls=%async_computation.1 | async-start | bytes 2097152 | tf_op jit(solution)/shard_map/all_to_all | solution.py:30
  109.9 0.0 all-gather.2.cloned.1.call-start
  110.0 0.0 copy-done.4
  110.0 1.0 copy.21
  111.0 25.2 %all-to-all-done = bf16[32,2,8192]{2,1,0:T(2,128)(2,1)S(1)} async-done(((bf16[32,2,8192]{2,1,0:T(2,128)(2,1)}), bf16[32,2,8192]{2,1,0:T(2,128)(2,1)S(1)}, u32[]{:S(2)}, u32[]{:S(2)}) %all-to-all-start) | async-done | bytes 1048608 | tf_op jit(solution)/shard_map/all_to_all | solution.py:30
  136.2 1.0 reshape.112
  137.2 1.2 copy.35
  138.4 0.8 copy.23
  139.2 0.8 reshape.102
  139.9 0.0 copy-start.3
  140.0 0.0 copy-start.5
  140.0 0.0 copy-start.7
  140.0 3.9 %convolution_bitcast_fusion = f32[1024,256]{0,1:T(8,128)S(1)} fusion(bf16[2048,256]{1,0:T(8,128)(2,1)S(1)} %reshape.102, bf16[1024,2048]{1,0:T(8,128)(2,1)} %param.7), kind=kOutput, calls=%fused_computation.6 | convolution fusion | flops 1073741824 | bytes 6291456 | tf_op jit(solution)/shard_map/btd,bdr->btr/dot_general | solution.py:38
  143.9 0.0 copy-start.10
  143.9 1.0 copy-done.10
  144.9 0.0 copy-done.5
  144.9 0.0 copy-done.7
  144.9 1.5 fusion
  146.4 0.5 copy.24
  146.9 0.8 convert_element_type.63
  147.7 0.6 copy.36
  148.3 1.4 reduce.1
  149.7 0.8 reshape.113
  150.6 29.7 %all_to_all.15 = bf16[32,2,8192]{2,1,0:T(2,128)(2,1)S(1)} all-to-all(bf16[32,2,8192]{2,1,0:T(2,128)(2,1)S(1)} %reshape.113), channel_id=1, replica_groups=mesh['pair'=4,'gen'=8] {'pair','gen'}, dimensions={0} | all-to-all | bytes 2097152 | tf_op jit(solution)/shard_map/all_to_all | solution.py:57
  180.2 1.0 reshape.114
  181.3 2.0 convolution_convert_fusion.1
  183.3 0.0 all-gather.2.cloned.1.call-update
  183.3 5.3 %convolution_convert_fusion.2 = bf16[1024,2048]{1,0:T(8,128)(2,1)} fusion(bf16[2048,256]{1,0:T(8,128)(2,1)} %copy-done.3, f32[1024,256]{0,1:T(8,128)} %copy-done.10, bf16[1024,256]{0,1:T(8,128)(2,1)} %copy.21), kind=kOutput, calls=%fused_computation.3 | convolution fusion | flops 1078460416 | bytes 6815744 | tf_op jit(solution)/shard_map/btr,bdr->btd/dot_general | solution.py:44
  188.6 39.8 %all-gather.2.cloned.1.call-done = bf16[16,65536]{1,0:T(8,128)(2,1)} async-done(((bf16[16,16384]{1,0:T(8,128)(2,1)}), bf16[16,65536]{1,0:T(8,128)(2,1)}) %all-gather.2.cloned.1.call-update) | async-done | bytes 2097168 | tf_op jit(solution)/shard_map/all_gather | solution.py:61
  228.4 11.0 %fusion.17 = f32[16,128]{1,0:T(8,128)S(1)} fusion(bf16[16,65536]{1,0:T(8,128)(2,1)} %all-gather.2.cloned.1.call-done, bf16[128,65536]{1,0:T(8,128)(2,1)} %param.13), kind=kOutput, calls=%fused_computation.35 | convolution fusion | flops 268435456 | bytes 18882560 | tf_op jit(solution)/shard_map/pc,ec->pe/dot_general | solution.py:65
  239.4 13.8 %psum.7 = f32[16,128]{1,0:T(8,128)S(1)} all-reduce(f32[16,128]{1,0:T(8,128)S(1)} %fusion.17), channel_id=1, replica_groups=mesh['pair'=4,'gen'=8] {'gen'}, use_global_device_ids=true, to_apply=%region_1.2 | all-reduce | flops 2048 | bytes 16384 | tf_op jit(solution)/shard_map/psum | solution.py:68
  253.2 1.0 fusion.7
  254.2 8.5 %convolution_convert_fusion = bf16[128,65536]{1,0:T(8,128)(2,1)} fusion(bf16[16,128]{1,0:T(8,128)(2,1)S(1)} %convolution_convert_fusion.4, bf16[16,65536]{1,0:T(8,128)(2,1)S(1)} %copy-done.2), kind=kOutput, calls=%fused_computation.1 | convolution fusion | flops 276824064 | bytes 18878464 | tf_op jit(solution)/shard_map/pe,pc->ec/dot_general | solution.py:62
  (13 shorter events, 0.0 us)
Async XLA Ops:
  7.2 0.8 copy-start
  7.2 91.4 %reduce-scatter.2.cloned.1.call-start = ((), (), s32[]{:S(2)}) async-start(), calls=%async_computation.3 | async-start | bytes 5242880 | tf_op jit(solution)/shard_map/reduce_scatter | solution.py:25
  18.9 0.7 copy-start.6
  101.1 8.9 %copy-start.4 = (bf16[1024,256]{1,0:T(8,128)(2,1)S(1)}, bf16[1024,256]{1,0:T(8,128)(2,1)}, u32[]{:S(2)}) copy-start(bf16[1024,256]{1,0:T(8,128)(2,1)} %param.8) | copy-start | bytes 1572868
  104.8 31.4 %all-to-all-start = ((bf16[32,2,8192]{2,1,0:T(2,128)(2,1)}), bf16[32,2,8192]{2,1,0:T(2,128)(2,1)S(1)}, u32[]{:S(2)}, u32[]{:S(2)}) async-start(bf16[32,2,8192]{2,1,0:T(2,128)(2,1)} %reshape.111), calls=%async_computation.1 | async-start | bytes 2097152 | tf_op jit(solution)/shard_map/all_to_all | solution.py:30
  109.9 118.5 %all-gather.2.cloned.1.call-start = ((), (), s32[]{:S(2)}) async-start(), calls=%async_computation.4 | async-start | bytes 2621440 | tf_op jit(solution)/shard_map/all_gather | solution.py:61
  139.9 6.4 %copy-start.3 = (bf16[2048,256]{1,0:T(8,128)(2,1)}, bf16[2048,256]{1,0:T(8,128)(2,1)S(1)}, u32[]{:S(2)}) copy-start(bf16[2048,256]{1,0:T(8,128)(2,1)S(1)} %reshape.102) | copy-start | bytes 3145732
  140.0 4.9 %copy-start.5 = (bf16[1024,256]{0,1:T(8,128)(2,1)S(1)}, bf16[1024,256]{0,1:T(8,128)(2,1)}, u32[]{:S(2)}) copy-start(bf16[1024,256]{0,1:T(8,128)(2,1)} %copy.21) | copy-start | bytes 1572868
  140.0 4.9 %copy-start.7 = (bf16[1024,2048]{1,0:T(8,128)(2,1)S(1)}, bf16[1024,2048]{1,0:T(8,128)(2,1)}, u32[]{:S(2)}) copy-start(bf16[1024,2048]{1,0:T(8,128)(2,1)} %param.7) | copy-start | bytes 12582916
  143.9 1.0 copy-start.10
  188.6 64.6 %copy-start.8 = (s32[16]{0:T(128)S(1)}, s32[16]{0:T(128)}, u32[]{:S(2)}) copy-start(s32[16]{0:T(128)} %param.11) | copy-start | bytes 196
  188.6 64.6 %copy-start.9 = (s32[16]{0:T(128)S(1)}, s32[16]{0:T(128)}, u32[]{:S(2)}) copy-start(s32[16]{0:T(128)} %param.10) | copy-start | bytes 196
  228.4 25.8 %copy-start.2 = (bf16[16,65536]{1,0:T(8,128)(2,1)S(1)}, bf16[16,65536]{1,0:T(8,128)(2,1)}, u32[]{:S(2)}) copy-start(bf16[16,65536]{1,0:T(8,128)(2,1)} %all-gather.2.cloned.1.call-done) | copy-start | bytes 6291460
  254.2 8.5 %copy-start.1 = (f32[96,128]{1,0:T(8,128)S(1)}, f32[96,128]{1,0:T(8,128)}, u32[]{:S(2)}) copy-start(f32[96,128]{1,0:T(8,128)} %param.12) | copy-start | bytes 147460
Sparse Core Ops, SparseCore 0:
  19.1 79.4 reduce-scatter.1
  183.4 44.9 all-gather.1

commit v4 on v3

--- a/solution.py
+++ b/solution.py
@@ -26,13 +26,10 @@
         partial_value, "pair", scatter_dimension=1, tiled=True
     ).astype(jnp.bfloat16)
     flat_pairs = block_pair[:, 0]
-    outgoing = jnp.take(adapter_part, flat_pairs, axis=0)
-    incoming = lax.all_to_all(outgoing, ("pair", "gen"), 0, 0, tiled=True)
-    adapters = (
-        incoming.reshape(pair_count_axis, gen_count, quarter)
-        .transpose(1, 0, 2)
-        .reshape(blocks_here, model_width, adapter_rank)
-    )
+    gen_major_pairs = flat_pairs.reshape(pair_count_axis, gen_count).T.reshape(-1)
+    outgoing = jnp.take(adapter_part, gen_major_pairs, axis=0)
+    incoming = lax.all_to_all(outgoing, ("gen", "pair"), 0, 0, tiled=True)
+    adapters = incoming.reshape(blocks_here, model_width, adapter_rank)
     token_blocks = tokens.reshape(blocks_here, BLK, model_width)
     cot_blocks = cotangent.reshape(blocks_here, BLK, adapter_rank)
     hidden = jnp.einsum("btd,bdr->btr", token_blocks, adapters, preferred_element_type=jnp.float32)
@@ -48,15 +45,10 @@
     outer_grads = jnp.einsum(
         "btd,btr->bdr", token_blocks, grad_hidden, preferred_element_type=jnp.float32
     )
-    by_owner = (
-        outer_grads.reshape(gen_count, pair_count_axis, quarter)
-        .transpose(1, 0, 2)
-        .reshape(pair_count_axis * gen_count, quarter)
-        .astype(jnp.bfloat16)
-    )
-    returned = lax.all_to_all(by_owner, ("pair", "gen"), 0, 0, tiled=True)
+    by_owner = outer_grads.reshape(gen_count * pair_count_axis, quarter).astype(jnp.bfloat16)
+    returned = lax.all_to_all(by_owner, ("gen", "pair"), 0, 0, tiled=True)
     pair_ids = jnp.arange(pair_count, dtype=jnp.int32)
-    segment_hot = (pair_ids[:, None] == flat_pairs[None, :]).astype(jnp.float32)
+    segment_hot = (pair_ids[:, None] == gen_major_pairs[None, :]).astype(jnp.float32)
     row_grad = jnp.dot(segment_hot, returned.astype(jnp.float32), precision=lax.Precision.HIGHEST).astype(jnp.bfloat16)
     grad_rounded = lax.all_gather(row_grad, "pair", axis=1, tiled=True)
     grad_generator = jnp.einsum(
@@ -65,7 +57,12 @@
     partial_pair = jnp.einsum(
         "pc,ec->pe", grad_rounded, generator, preferred_element_type=jnp.float32
     )
-    grad_pair = lax.psum(partial_pair, "gen")
+    grad_pair = partial_pair
+    span = 1
+    while span < gen_count:
+        swap = [(i, i ^ span) for i in range(gen_count)]
+        grad_pair = grad_pair + lax.ppermute(grad_pair, "gen", swap)
+        span *= 2
     grad_embed = jnp.dot(hot_both.T, grad_pair, precision=lax.Precision.HIGHEST)
     return (grad_tokens, grad_generator, grad_embed)
 

time: 270 us -> 274 us (1.015)
  blocking collectives: 43.5 us -> 29.3 us
  other arithmetic: 4.35 us -> 17 us
  waiting for transfers between devices: 144 us -> 149 us
  starting transfers between devices: 5.19 us -> 8.4 us
    psum x1 -> x0, blocking collectives: 13.8 us -> none  [shards(): grad_pair = lax.psum(partial_pair, 'gen')]
    all_to_all x0 -> x1, other arithmetic: none -> 6.41 us  [shards(): incoming = lax.all_to_all(outgoing, ('gen', 'pair'), 0, 0, tiled=True)]
    all_gather x1, waiting for transfers between devices: 39.8 us -> 45.9 us  [shards(): grad_rounded = lax.all_gather(row_grad, 'pair', axis=1, tiled=True)]
    convert_element_type x1, other arithmetic: 1.45 us -> 7.06 us  [shards(): outer_grads.reshape(gen_count * pair_count_axis, quarter)]
    ppermute x0 -> x3, starting transfers between devices: none -> 3.03 us  [shards(): grad_pair = grad_pair + lax.ppermute(grad_pair, 'gen', swap)]
    unnamed x28 -> x30, local copies, waits for them, and re-layouts: 9.01 us -> 7.87 us
  transfers between devices with their start and end apart: 3 -> 6, of which waited for: 3 -> 4; matrix products, arithmetic and copies ran while one was open for 2% -> 6% of each run, Pallas kernels for 0% -> 0%
where the time goes in v4:
time: 274 us; the launch traced here: 273 us
  waiting for transfers between devices  149 us (54%)
  matrix products  43.7 us (16%)
  blocking collectives  29.3 us (11%)
  other arithmetic  17 us (6%)
  between operations  14.3 us (5%)
  local copies, waits for them, and re-layouts  11.7 us (4%)
  starting transfers between devices  8.4 us (3%)
    reduce_scatter x1, waiting for transfers between devices, shards(): lax.psum_scatter(partial_value, 'pair', scatter_dimension=1, tiled=True)  77.9 us
    all_gather x1, waiting for transfers between devices, shards(): grad_rounded = lax.all_gather(row_grad, 'pair', axis=1, tiled=True)  45.9 us
    all_to_all x1, blocking collectives, shards(): returned = lax.all_to_all(by_owner, ('gen', 'pair'), 0, 0, tiled=True)  29.3 us
    all_to_all x1, waiting for transfers between devices, shards(): incoming = lax.all_to_all(outgoing, ('gen', 'pair'), 0, 0, tiled=True)  23.8 us
    dot_general x1, matrix products, shards(): jnp.einsum('pc,ec->pe', grad_rounded, generator, preferred_element_type=j...  10.8 us
    dot_general x1, matrix products, shards(): jnp.dot(pair_embed, generator, preferred_element_type=jnp.float32)  10.1 us
    dot_general x1, matrix products, shards(): jnp.einsum('pe,pc->ec', pair_embed, grad_rounded, preferred_element_type=...  8.53 us
    unnamed x30, local copies, waits for them, and re-layouts  7.87 us
  transfers between devices with their start and end apart: 6, of which 4 were waited for; matrix products, arithmetic and copies ran while one was open for 6% of the time, Pallas kernels for 0%

profile of v4, /device:TPU:0, one launch (start us, length us, event | category | flops | bytes accessed | tf_op | source)
XLA Modules:
  0.0 273.3 jit_solution(9583500638442482579)
XLA Ops:
  7.2 0.0 copy-start
  7.2 0.0 reduce-scatter.2.cloned.1.call-start
  7.2 0.7 copy-done
  8.0 0.9 convolution_convert_fusion.4
  8.8 10.1 %fusion.17 = f32[16,65536]{1,0:T(8,128)} fusion(bf16[16,128]{1,0:T(8,128)(2,1)S(1)} %convolution_convert_fusion.4, bf16[128,65536]{1,0:T(8,128)(2,1)} %param.13), kind=kOutput, calls=%fused_computation.34 | convolution fusion | flops 268435456 | bytes 20975616 | tf_op jit(solution)/shard_map/dot_general | solution.py:24
  18.9 0.0 reduce-scatter.2.cloned.1.call-update
  19.0 0.5 broadcast.72
  19.5 0.1 copy-done.8
  19.6 0.7 reduce.4
  20.3 0.1 reshape_squeeze.3
  20.4 0.1 copy.24
  20.4 0.1 reshape.125
  20.5 0.1 reshape.124
  20.6 77.9 %reduce-scatter.2.cloned.1.call-done = f32[16,16384]{1,0:T(8,128)} async-done(((f32[16,65536]{1,0:T(8,128)}), f32[16,16384]{1,0:T(8,128)}) %reduce-scatter.2.cloned.1.call-update) | async-done | bytes 1048592 | tf_op jit(solution)/shard_map/reduce_scatter | solution.py:25
  98.6 1.3 convert_element_type.52
  99.9 1.2 gather_fusion
  101.1 0.2 bitcast_select_fusion
  101.3 0.5 broadcast.73
  101.8 1.4 reduce.5
  103.2 1.6 reshape.145
  104.8 5.1 %all-to-all-start = ((bf16[32,2,8192]{2,1,0:T(2,128)(2,1)}), bf16[32,2,8192]{2,1,0:T(2,128)(2,1)S(1)}, u32[]{:S(2)}, u32[]{:S(2)}) async-start(bf16[32,2,8192]{2,1,0:T(2,128)(2,1)} %reshape.145), calls=%async_computation.1 | async-start | bytes 2097152 | tf_op jit(solution)/shard_map/all_to_all | solution.py:31
  109.9 0.2 all-gather.2.cloned.1.call-start
  110.2 1.0 copy.23
  111.2 23.8 %all-to-all-done = bf16[32,2,8192]{2,1,0:T(2,128)(2,1)S(1)} async-done(((bf16[32,2,8192]{2,1,0:T(2,128)(2,1)}), bf16[32,2,8192]{2,1,0:T(2,128)(2,1)S(1)}, u32[]{:S(2)}, u32[]{:S(2)}) %all-to-all-start) | async-done | bytes 1048608 | tf_op jit(solution)/shard_map/all_to_all | solution.py:31
  135.0 1.0 reshape.146
  136.0 6.4 %reduce.1 = bf16[32,16384]{1,0:T(8,128)(2,1)S(1)} reduce(bf16[32,1,16384]{2,1,0:T(2,128)(2,1)S(1)} %reshape.146, bf16[]{:T(256)} %constant.19), dimensions={1}, to_apply=%all_to_all.10.reduce_sub_computation | reduce | bytes 2097154 | tf_op jit(solution)/shard_map/all_to_all | solution.py:31
  142.4 0.5 reshape.126
  143.0 0.0 copy-start.3
  143.0 0.0 copy-start.7
  143.0 3.9 %convolution_bitcast_fusion = f32[1024,256]{0,1:T(8,128)S(1)} fusion(bf16[2048,256]{1,0:T(8,128)(2,1)S(1)} %reshape.126, bf16[1024,2048]{1,0:T(8,128)(2,1)} %param.7), kind=kOutput, calls=%fused_computation.6 | convolution fusion | flops 1073741824 | bytes 6291456 | tf_op jit(solution)/shard_map/btd,bdr->btr/dot_general | solution.py:35
  146.9 1.0 copy-done.11
  147.9 1.6 fusion
  149.5 0.5 copy.27
  150.0 0.7 convert_element_type.60
  150.7 7.1 %reduce.6 = bf16[32,16384]{1,0:T(8,128)(2,1)S(1)} reduce(bf16[32,1,16384]{2,1,0:T(2,128)(2,1)S(1)} %convert_element_type.60, bf16[]{:T(256)} %broadcast.73), dimensions={1}, to_apply=%convert_element_type.60.reduce_sub_computation | reduce | bytes 2097154 | tf_op jit(solution)/shard_map/convert_element_type | solution.py:48
  157.8 0.8 reshape.147
  158.6 29.3 %all_to_all.15 = bf16[32,2,8192]{2,1,0:T(2,128)(2,1)S(1)} all-to-all(bf16[32,2,8192]{2,1,0:T(2,128)(2,1)S(1)} %reshape.147), channel_id=1, replica_groups=mesh['pair'=4,'gen'=8] {'gen','pair'}, dimensions={0} | all-to-all | bytes 2097152 | tf_op jit(solution)/shard_map/all_to_all | solution.py:49
  187.9 1.0 reshape.148
  188.9 2.0 convolution_convert_fusion.1
  191.0 0.0 all-gather.2.cloned.1.call-update
  191.0 45.9 %all-gather.2.cloned.1.call-done = bf16[16,65536]{1,0:T(8,128)(2,1)} async-done(((bf16[16,16384]{1,0:T(8,128)(2,1)}), bf16[16,65536]{1,0:T(8,128)(2,1)}) %all-gather.2.cloned.1.call-update) | async-done | bytes 2097168 | tf_op jit(solution)/shard_map/all_gather | solution.py:53
  236.9 10.8 %fusion.18 = f32[16,128]{1,0:T(8,128)S(1)} fusion(bf16[16,65536]{1,0:T(8,128)(2,1)} %all-gather.2.cloned.1.call-done, bf16[128,65536]{1,0:T(8,128)(2,1)} %param.13), kind=kOutput, calls=%fused_computation.35 | convolution fusion | flops 268435456 | bytes 18882560 | tf_op jit(solution)/shard_map/pc,ec->pe/dot_general | solution.py:57
  247.7 1.2 collective-permute-done
  248.9 1.5 collective-permute-start.1
  250.4 5.0 %convolution_convert_fusion.2 = bf16[1024,2048]{1,0:T(8,128)(2,1)} fusion(bf16[2048,256]{1,0:T(8,128)(2,1)S(1)} %copy-done.4, f32[1024,256]{0,1:T(8,128)} %copy-done.11, bf16[1024,256]{0,1:T(8,128)(2,1)} %copy.23), kind=kOutput, calls=%fused_computation.3 | convolution fusion | flops 1078460416 | bytes 6815744 | tf_op jit(solution)/shard_map/btr,bdr->btd/dot_general | solution.py:41
  255.4 1.5 collective-permute-start.2
  257.0 8.5 %convolution_convert_fusion = bf16[128,65536]{1,0:T(8,128)(2,1)} fusion(bf16[16,128]{1,0:T(8,128)(2,1)S(1)} %convolution_convert_fusion.4, bf16[16,65536]{1,0:T(8,128)(2,1)S(1)} %copy-done.2), kind=kOutput, calls=%fused_computation.1 | convolution fusion | flops 276824064 | bytes 18878464 | tf_op jit(solution)/shard_map/pe,pc->ec/dot_general | solution.py:54
  265.5 1.0 fusion.7
  (26 shorter events, 0.1 us)
Async XLA Ops:
  7.2 0.8 copy-start
  7.2 91.4 %reduce-scatter.2.cloned.1.call-start = ((), (), s32[]{:S(2)}) async-start(), calls=%async_computation.3 | async-start | bytes 5242880 | tf_op jit(solution)/shard_map/reduce_scatter | solution.py:25
  18.9 0.7 copy-start.8
  101.1 9.1 %copy-start.5 = (bf16[1024,256]{1,0:T(8,128)(2,1)S(1)}, bf16[1024,256]{1,0:T(8,128)(2,1)}, u32[]{:S(2)}) copy-start(bf16[1024,256]{1,0:T(8,128)(2,1)} %param.8) | copy-start | bytes 1572868
  104.8 30.2 %all-to-all-start = ((bf16[32,2,8192]{2,1,0:T(2,128)(2,1)}), bf16[32,2,8192]{2,1,0:T(2,128)(2,1)S(1)}, u32[]{:S(2)}, u32[]{:S(2)}) async-start(bf16[32,2,8192]{2,1,0:T(2,128)(2,1)} %reshape.145), calls=%async_computation.1 | async-start | bytes 2097152 | tf_op jit(solution)/shard_map/all_to_all | solution.py:31
  109.9 127.0 %all-gather.2.cloned.1.call-start = ((), (), s32[]{:S(2)}) async-start(), calls=%async_computation.4 | async-start | bytes 2621440 | tf_op jit(solution)/shard_map/all_gather | solution.py:53
  143.0 6.5 %copy-start.3 = (bf16[2048,256]{1,0:T(8,128)(2,1)}, bf16[2048,256]{1,0:T(8,128)(2,1)S(1)}, u32[]{:S(2)}) copy-start(bf16[2048,256]{1,0:T(8,128)(2,1)S(1)} %reshape.126) | copy-start | bytes 3145732
  143.0 4.9 %copy-start.6 = (bf16[1024,256]{0,1:T(8,128)(2,1)S(1)}, bf16[1024,256]{0,1:T(8,128)(2,1)}, u32[]{:S(2)}) copy-start(bf16[1024,256]{0,1:T(8,128)(2,1)} %copy.23) | copy-start | bytes 1572868
  143.0 4.9 %copy-start.7 = (bf16[1024,2048]{1,0:T(8,128)(2,1)S(1)}, bf16[1024,2048]{1,0:T(8,128)(2,1)}, u32[]{:S(2)}) copy-start(bf16[1024,2048]{1,0:T(8,128)(2,1)} %param.7) | copy-start | bytes 12582916
  146.9 1.0 copy-start.11
  191.0 59.4 %copy-start.4 = (bf16[2048,256]{1,0:T(8,128)(2,1)S(1)}, bf16[2048,256]{1,0:T(8,128)(2,1)}, u32[]{:S(2)}) copy-start(bf16[2048,256]{1,0:T(8,128)(2,1)} %copy-done.3) | copy-start | bytes 3145732
  247.7 1.2 collective-permute-start
  248.9 8.0 %copy-start.2 = (bf16[16,65536]{1,0:T(8,128)(2,1)S(1)}, bf16[16,65536]{1,0:T(8,128)(2,1)}, u32[]{:S(2)}) copy-start(bf16[16,65536]{1,0:T(8,128)(2,1)} %all-gather.2.cloned.1.call-done) | copy-start | bytes 6291460
  248.9 6.5 %collective-permute-start.1 = (f32[16,128]{1,0:T(8,128)S(1)}, f32[16,128]{1,0:T(8,128)S(1)}, u32[]{:S(2)}, u32[]{:S(2)}) collective-permute-start(f32[16,128]{1,0:T(8,128)S(1)} %add.50), channel_id=1, source_target_pairs={{0,2},{1,3},{2,0},{3,1},{4,6},{5,7},{6,4},{7,5},{8,10},{9,11},{10,... | collective-permute-start | bytes 24584 | tf_op jit(solution)/shard_map/ppermute | solution.py:64
  255.4 10.1 %copy-start.9 = (s32[16]{0:T(128)S(1)}, s32[16]{0:T(128)}, u32[]{:S(2)}) copy-start(s32[16]{0:T(128)} %param.11) | copy-start | bytes 196
  255.4 10.1 %copy-start.10 = (s32[16]{0:T(128)S(1)}, s32[16]{0:T(128)}, u32[]{:S(2)}) copy-start(s32[16]{0:T(128)} %param.10) | copy-start | bytes 196
  255.4 10.1 %collective-permute-start.2 = (f32[16,128]{1,0:T(8,128)S(1)}, f32[16,128]{1,0:T(8,128)S(1)}, u32[]{:S(2)}, u32[]{:S(2)}) collective-permute-start(f32[16,128]{1,0:T(8,128)S(1)} %add.51), channel_id=1, source_target_pairs={{0,4},{1,5},{2,6},{3,7},{4,0},{5,1},{6,2},{7,3},{8,12},{9,13},{10,... | collective-permute-start | bytes 24584 | tf_op jit(solution)/shard_map/ppermute | solution.py:64
  257.0 9.5 %copy-start.1 = (f32[96,128]{1,0:T(8,128)S(1)}, f32[96,128]{1,0:T(8,128)}, u32[]{:S(2)}) copy-start(f32[96,128]{1,0:T(8,128)} %param.12) | copy-start | bytes 147460
Sparse Core Ops, SparseCore 0:
  19.1 79.4 reduce-scatter.1
  191.1 45.7 all-gather.1

commit v5 on v4

--- a/solution.py
+++ b/solution.py
@@ -27,7 +27,8 @@
     ).astype(jnp.bfloat16)
     flat_pairs = block_pair[:, 0]
     gen_major_pairs = flat_pairs.reshape(pair_count_axis, gen_count).T.reshape(-1)
-    outgoing = jnp.take(adapter_part, gen_major_pairs, axis=0)
+    rows_per = quarter // adapter_rank
+    outgoing = jnp.take(adapter_part.reshape(pair_count, rows_per, adapter_rank), gen_major_pairs, axis=0)
     incoming = lax.all_to_all(outgoing, ("gen", "pair"), 0, 0, tiled=True)
     adapters = incoming.reshape(blocks_here, model_width, adapter_rank)
     token_blocks = tokens.reshape(blocks_here, BLK, model_width)
@@ -45,11 +46,15 @@
     outer_grads = jnp.einsum(
         "btd,btr->bdr", token_blocks, grad_hidden, preferred_element_type=jnp.float32
     )
-    by_owner = outer_grads.reshape(gen_count * pair_count_axis, quarter).astype(jnp.bfloat16)
+    by_owner = outer_grads.reshape(gen_count * pair_count_axis, rows_per, adapter_rank).astype(jnp.bfloat16)
     returned = lax.all_to_all(by_owner, ("gen", "pair"), 0, 0, tiled=True)
     pair_ids = jnp.arange(pair_count, dtype=jnp.int32)
     segment_hot = (pair_ids[:, None] == gen_major_pairs[None, :]).astype(jnp.float32)
-    row_grad = jnp.dot(segment_hot, returned.astype(jnp.float32), precision=lax.Precision.HIGHEST).astype(jnp.bfloat16)
+    row_grad = (
+        jnp.einsum("pb,bxr->pxr", segment_hot, returned.astype(jnp.float32), precision=lax.Precision.HIGHEST)
+        .astype(jnp.bfloat16)
+        .reshape(pair_count, quarter)
+    )
     grad_rounded = lax.all_gather(row_grad, "pair", axis=1, tiled=True)
     grad_generator = jnp.einsum(
         "pe,pc->ec", pair_embed, grad_rounded, preferred_element_type=jnp.float32

time: 274 us -> 252 us (0.920)
  other arithmetic: 17 us -> 3.1 us
  waiting for transfers between devices: 149 us -> 143 us
    convert_element_type x1 -> x0, other arithmetic: 7.06 us -> none  [shards(): outer_grads.reshape(gen_count * pair_count_axis, quarter)]
    all_to_all x1 -> x0, other arithmetic: 6.41 us -> none  [shards(): incoming = lax.all_to_all(outgoing, ('gen', 'pair'), 0, 0, tiled=True)]
    all_to_all x1, waiting for transfers between devices: 23.8 us -> 18.4 us  [shards(): incoming = lax.all_to_all(outgoing, ('gen', 'pair'), 0, 0, tiled=True)]
    unnamed x30 -> x20, local copies, waits for them, and re-layouts: 7.87 us -> 8.13 us
  transfers between devices with their start and end apart: 6 -> 6, of which waited for: 4 -> 4; matrix products, arithmetic and copies ran while one was open for 6% -> 8% of each run, Pallas kernels for 0% -> 0%
where the time goes in v5:
time: 252 us
  waiting for transfers between devices  143 us (57%)
  matrix products  43.2 us (17%)
  blocking collectives  29.3 us (12%)
  between operations  14.2 us (6%)
  local copies, waits for them, and re-layouts  10.5 us (4%)
  starting transfers between devices  8.22 us (3%)
  other arithmetic  3.1 us (1%)
    reduce_scatter x1, waiting for transfers between devices, shards(): lax.psum_scatter(partial_value, 'pair', scatter_dimension=1, tiled=True)  77.9 us
    all_gather x1, waiting for transfers between devices, shards(): grad_rounded = lax.all_gather(row_grad, 'pair', axis=1, tiled=True)  45.9 us
    all_to_all x1, blocking collectives, shards(): returned = lax.all_to_all(by_owner, ('gen', 'pair'), 0, 0, tiled=True)  29.3 us
    all_to_all x1, waiting for transfers between devices, shards(): incoming = lax.all_to_all(outgoing, ('gen', 'pair'), 0, 0, tiled=True)  18.4 us
    dot_general x1, matrix products, shards(): jnp.einsum('pc,ec->pe', grad_rounded, generator, preferred_element_type=j...  10.8 us
    dot_general x1, matrix products, shards(): jnp.dot(pair_embed, generator, preferred_element_type=jnp.float32)  10.1 us
    dot_general x1, matrix products, shards(): jnp.einsum('pe,pc->ec', pair_embed, grad_rounded, preferred_element_type=...  8.52 us
    unnamed x20, local copies, waits for them, and re-layouts  8.13 us
  transfers between devices with their start and end apart: 6, of which 4 were waited for; matrix products, arithmetic and copies ran while one was open for 8% of the time, Pallas kernels for 0%

profile of v5, /device:TPU:0, one launch (start us, length us, event | category | flops | bytes accessed | tf_op | source)
XLA Modules:
  0.0 252.0 jit_solution(17206080016466876757)
XLA Ops:
  7.2 0.0 copy-start
  7.2 0.0 reduce-scatter.2.cloned.1.call-start
  7.2 0.7 copy-done
  8.0 0.9 convolution_convert_fusion.3
  8.8 10.1 %fusion.21 = f32[16,65536]{1,0:T(8,128)} fusion(bf16[16,128]{1,0:T(8,128)(2,1)S(1)} %convolution_convert_fusion.3, bf16[128,65536]{1,0:T(8,128)(2,1)} %param.13), kind=kOutput, calls=%fused_computation.32 | convolution fusion | flops 268435456 | bytes 20975616 | tf_op jit(solution)/shard_map/dot_general | solution.py:24
  18.9 0.0 reduce-scatter.2.cloned.1.call-update
  19.0 0.5 broadcast.42
  19.5 0.1 copy-done.5
  19.6 0.7 reduce.3
  20.3 0.1 reshape_squeeze.3
  20.3 0.1 copy.19
  20.4 0.1 reshape.93
  20.5 0.1 reshape.91
  20.6 0.0 copy-start.4
  20.6 77.9 %reduce-scatter.2.cloned.1.call-done = f32[16,16384]{1,0:T(8,128)} async-done(((f32[16,65536]{1,0:T(8,128)}), f32[16,16384]{1,0:T(8,128)}) %reduce-scatter.2.cloned.1.call-update) | async-done | bytes 1048592 | tf_op jit(solution)/shard_map/reduce_scatter | solution.py:25
  98.6 1.3 convert_element_type.42
  99.9 0.1 copy.30
  100.0 0.6 gather_fusion
  100.6 1.1 broadcast_select_fusion
  101.7 5.1 %all-to-all-start = ((bf16[32,64,256]{2,1,0:T(8,128)(2,1)}), bf16[32,64,256]{2,1,0:T(8,128)(2,1)S(1)}, u32[]{:S(2)}, u32[]{:S(2)}) async-start(bf16[32,64,256]{2,1,0:T(8,128)(2,1)} %broadcast_select_fusion), calls=%async_computation.1 | async-start | bytes 2097152 | tf_op jit(solution)/shard_map/all_to_all | solution.py:32
  106.8 0.0 all-gather.2.cloned.1.call-start
  106.9 0.0 copy-done.4
  106.9 0.2 copy.18
  107.1 6.4 %copy.21 = bf16[1024,2048]{0,1:T(8,128)(2,1)} copy(bf16[1024,2048]{1,0:T(8,128)(2,1)} %param.7) | data formatting | bytes 8388608 | tf_op args[0]
  113.5 18.4 %all-to-all-done = bf16[32,64,256]{2,1,0:T(8,128)(2,1)S(1)} async-done(((bf16[32,64,256]{2,1,0:T(8,128)(2,1)}), bf16[32,64,256]{2,1,0:T(8,128)(2,1)S(1)}, u32[]{:S(2)}, u32[]{:S(2)}) %all-to-all-start) | async-done | bytes 1048608 | tf_op jit(solution)/shard_map/all_to_all | solution.py:32
  131.9 3.9 %multiply_convert_fusion = bf16[1024,256]{0,1:T(8,128)(2,1)S(1)} fusion(bf16[2048,256]{1,0:T(8,128)(2,1)S(1)} %bitcast.37, bf16[1024,2048]{1,0:T(8,128)(2,1)} %param.7, bf16[1024,256]{0,1:T(8,128)(2,1)S(1)} %copy.18), kind=kOutput, calls=%fused_computation.12 | convolution fusion | flops 1076363264 | bytes 6291456 | tf_op jit(solution)/shard_map/btd,bdr->btr/dot_general | solution.py:36
  135.8 0.0 copy-start.3
  135.8 0.0 copy-done.2
  135.8 3.0 %fusion.5 = bf16[32,64,256]{2,0,1:T(8,128)(2,1)S(1)} fusion(bf16[32,64,1024]{2,1,0:T(8,128)(2,1)S(1)} %bitcast.39, bf16[1024,256]{0,1:T(8,128)(2,1)S(1)} %multiply_convert_fusion), kind=kOutput, calls=%fused_computation.6 | convolution fusion | flops 1074266112 | bytes 5767168 | tf_op jit(solution)/shard_map/btd,btr->bdr/dot_general | solution.py:46
  138.8 0.0 copy-done.3
  138.8 0.6 copy.24
  139.4 29.3 %all_to_all.10 = bf16[32,64,256]{2,1,0:T(8,128)(2,1)S(1)} all-to-all(bf16[32,64,256]{2,1,0:T(8,128)(2,1)S(1)} %copy.24), channel_id=1, replica_groups=mesh['pair'=4,'gen'=8] {'gen','pair'}, dimensions={0} | all-to-all | bytes 2097152 | tf_op jit(solution)/shard_map/all_to_all | solution.py:50
  168.7 0.7 fusion.8
  169.4 0.8 copy.29
  170.2 0.0 all-gather.2.cloned.1.call-update
  170.3 45.9 %all-gather.2.cloned.1.call-done = bf16[16,65536]{1,0:T(8,128)(2,1)} async-done(((bf16[16,16384]{1,0:T(8,128)(2,1)}), bf16[16,65536]{1,0:T(8,128)(2,1)}) %all-gather.2.cloned.1.call-update) | async-done | bytes 2097168 | tf_op jit(solution)/shard_map/all_gather | solution.py:58
  216.2 10.8 %fusion.22 = f32[16,128]{1,0:T(8,128)S(1)} fusion(bf16[16,65536]{1,0:T(8,128)(2,1)} %all-gather.2.cloned.1.call-done, bf16[128,65536]{1,0:T(8,128)(2,1)} %param.13), kind=kOutput, calls=%fused_computation.33 | convolution fusion | flops 268435456 | bytes 18882560 | tf_op jit(solution)/shard_map/pc,ec->pe/dot_general | solution.py:62
  227.0 0.0 collective-permute-start
  227.0 1.2 collective-permute-done
  228.2 1.5 collective-permute-start.1
  229.7 4.4 %convolution_convert_fusion.1 = bf16[1024,2048]{1,0:T(8,128)(2,1)} fusion(bf16[1024,256]{0,1:T(8,128)(2,1)} %copy-done.3, bf16[2048,256]{1,0:T(8,128)(2,1)S(1)} %bitcast.38), kind=kOutput, calls=%fused_computation.4 | convolution fusion | flops 1075838976 | bytes 5767168 | tf_op jit(solution)/shard_map/btr,bdr->btd/dot_general | solution.py:42
  234.1 0.0 collective-permute-done.1
  234.1 0.0 copy-start.7
  234.1 1.5 collective-permute-start.2
  235.6 0.0 copy-done.1
  235.6 8.5 %convolution_convert_fusion = bf16[128,65536]{1,0:T(8,128)(2,1)} fusion(bf16[16,128]{1,0:T(8,128)(2,1)S(1)} %convolution_convert_fusion.3, bf16[16,65536]{1,0:T(8,128)(2,1)S(1)} %copy-done.1), kind=kOutput, calls=%fused_computation.1 | convolution fusion | flops 276824064 | bytes 18878464 | tf_op jit(solution)/shard_map/pe,pc->ec/dot_general | solution.py:59
  244.1 0.0 collective-permute-done.2
  244.2 1.0 fusion.11
  (11 shorter events, 0.0 us)
Async XLA Ops:
  7.2 0.8 copy-start
  7.2 91.4 %reduce-scatter.2.cloned.1.call-start = ((), (), s32[]{:S(2)}) async-start(), calls=%async_computation.3 | async-start | bytes 5242880 | tf_op jit(solution)/shard_map/reduce_scatter | solution.py:25
  18.9 0.7 copy-start.5
  20.6 86.3 %copy-start.4 = (bf16[1024,256]{1,0:T(8,128)(2,1)S(1)}, bf16[1024,256]{1,0:T(8,128)(2,1)}, u32[]{:S(2)}) copy-start(bf16[1024,256]{1,0:T(8,128)(2,1)} %param.8) | copy-start | bytes 1572868
  101.7 30.2 %all-to-all-start = ((bf16[32,64,256]{2,1,0:T(8,128)(2,1)}), bf16[32,64,256]{2,1,0:T(8,128)(2,1)S(1)}, u32[]{:S(2)}, u32[]{:S(2)}) async-start(bf16[32,64,256]{2,1,0:T(8,128)(2,1)} %broadcast_select_fusion), calls=%async_computation.1 | async-start | bytes 2097152 | tf_op jit(solution)/shard_map/all_to_all | solution.py:32
  106.8 109.3 %all-gather.2.cloned.1.call-start = ((), (), s32[]{:S(2)}) async-start(), calls=%async_computation.4 | async-start | bytes 2621440 | tf_op jit(solution)/shard_map/all_gather | solution.py:58
  131.9 3.9 %copy-start.2 = (bf16[1024,2048]{0,1:T(8,128)(2,1)S(1)}, bf16[1024,2048]{0,1:T(8,128)(2,1)}, u32[]{:S(2)}) copy-start(bf16[1024,2048]{0,1:T(8,128)(2,1)} %copy.21) | copy-start | bytes 12582916
  135.8 3.0 %copy-start.3 = (bf16[1024,256]{0,1:T(8,128)(2,1)}, bf16[1024,256]{0,1:T(8,128)(2,1)S(1)}, u32[]{:S(2)}) copy-start(bf16[1024,256]{0,1:T(8,128)(2,1)S(1)} %multiply_convert_fusion) | copy-start | bytes 1572868
  227.0 1.2 collective-permute-start
  228.2 7.4 %copy-start.1 = (bf16[16,65536]{1,0:T(8,128)(2,1)S(1)}, bf16[16,65536]{1,0:T(8,128)(2,1)}, u32[]{:S(2)}) copy-start(bf16[16,65536]{1,0:T(8,128)(2,1)} %all-gather.2.cloned.1.call-done) | copy-start | bytes 6291460
  228.2 5.9 %collective-permute-start.1 = (f32[16,128]{1,0:T(8,128)S(1)}, f32[16,128]{1,0:T(8,128)S(1)}, u32[]{:S(2)}, u32[]{:S(2)}) collective-permute-start(f32[16,128]{1,0:T(8,128)S(1)} %add.50), channel_id=1, source_target_pairs={{0,2},{1,3},{2,0},{3,1},{4,6},{5,7},{6,4},{7,5},{8,10},{9,11},{10,... | collective-permute-start | bytes 24584 | tf_op jit(solution)/shard_map/ppermute | solution.py:69
  234.1 10.1 %copy-start.6 = (s32[16]{0:T(128)S(1)}, s32[16]{0:T(128)}, u32[]{:S(2)}) copy-start(s32[16]{0:T(128)} %param.11) | copy-start | bytes 196
  234.1 10.1 %copy-start.7 = (s32[16]{0:T(128)S(1)}, s32[16]{0:T(128)}, u32[]{:S(2)}) copy-start(s32[16]{0:T(128)} %param.10) | copy-start | bytes 196
  234.1 10.1 %collective-permute-start.2 = (f32[16,128]{1,0:T(8,128)S(1)}, f32[16,128]{1,0:T(8,128)S(1)}, u32[]{:S(2)}, u32[]{:S(2)}) collective-permute-start(f32[16,128]{1,0:T(8,128)S(1)} %add.51), channel_id=1, source_target_pairs={{0,4},{1,5},{2,6},{3,7},{4,0},{5,1},{6,2},{7,3},{8,12},{9,13},{10,... | collective-permute-start | bytes 24584 | tf_op jit(solution)/shard_map/ppermute | solution.py:69
Sparse Core Ops, SparseCore 0:
  19.1 79.4 reduce-scatter.1
  170.4 45.7 all-gather.1

commit v6 on v5

--- a/solution.py
+++ b/solution.py
@@ -46,22 +46,37 @@
     outer_grads = jnp.einsum(
         "btd,btr->bdr", token_blocks, grad_hidden, preferred_element_type=jnp.float32
     )
-    by_owner = outer_grads.reshape(gen_count * pair_count_axis, rows_per, adapter_rank).astype(jnp.bfloat16)
+    halves = 2
+    slice_rows = rows_per // halves
+    by_owner = (
+        outer_grads.reshape(gen_count, halves, pair_count_axis, slice_rows, adapter_rank)
+        .transpose(0, 2, 1, 3, 4)
+        .reshape(gen_count * pair_count_axis, rows_per, adapter_rank)
+        .astype(jnp.bfloat16)
+    )
     returned = lax.all_to_all(by_owner, ("gen", "pair"), 0, 0, tiled=True)
     pair_ids = jnp.arange(pair_count, dtype=jnp.int32)
     segment_hot = (pair_ids[:, None] == gen_major_pairs[None, :]).astype(jnp.float32)
     row_grad = (
         jnp.einsum("pb,bxr->pxr", segment_hot, returned.astype(jnp.float32), precision=lax.Precision.HIGHEST)
         .astype(jnp.bfloat16)
-        .reshape(pair_count, quarter)
+        .reshape(pair_count, halves, slice_rows * adapter_rank)
     )
-    grad_rounded = lax.all_gather(row_grad, "pair", axis=1, tiled=True)
+    half_cols = chunk // halves
+    grad_halves = []
+    partial_pair = None
+    for h in range(halves):
+        grad_half = lax.all_gather(row_grad[:, h], "pair", axis=1, tiled=True)
+        grad_halves.append(grad_half)
+        part = jnp.einsum(
+            "pc,ec->pe", grad_half, generator[:, h * half_cols:(h + 1) * half_cols],
+            preferred_element_type=jnp.float32,
+        )
+        partial_pair = part if partial_pair is None else partial_pair + part
+    grad_rounded = jnp.concatenate(grad_halves, axis=1)
     grad_generator = jnp.einsum(
         "pe,pc->ec", pair_embed, grad_rounded, preferred_element_type=jnp.float32
     ).astype(jnp.bfloat16)
-    partial_pair = jnp.einsum(
-        "pc,ec->pe", grad_rounded, generator, preferred_element_type=jnp.float32
-    )
     grad_pair = partial_pair
     span = 1
     while span < gen_count:

time: 252 us -> 295 us (1.17)
  waiting for transfers between devices: 143 us -> 182 us
  local copies, waits for them, and re-layouts: 10.5 us -> 17 us
    all_gather x1 -> x2, waiting for transfers between devices: 45.9 us -> 83.7 us  [shards(): grad_half = lax.all_gather(row_grad[:, h], 'pair', axis=1, tiled=True)]
    unnamed x20 -> x24, local copies, waits for them, and re-layouts: 8.13 us -> 13.6 us
    dot_general x1 -> x2, matrix products: 10.8 us -> 11.4 us  [shards(): jnp.einsum('pc,ec->pe', grad_half, generator[:, h * half_cols:(h + 1) * h...]
  transfers between devices with their start and end apart: 6 -> 7, of which waited for: 4 -> 5; matrix products, arithmetic and copies ran while one was open for 8% -> 10% of each run, Pallas kernels for 0% -> 0%
where the time goes in v6:
time: 295 us
  waiting for transfers between devices  182 us (62%)
  matrix products  41 us (14%)
  blocking collectives  29.3 us (10%)
  local copies, waits for them, and re-layouts  17 us (6%)
  between operations  13.9 us (5%)
  starting transfers between devices  8.45 us (3%)
  other arithmetic  3.1 us (1%)
    all_gather x2, waiting for transfers between devices, shards(): grad_half = lax.all_gather(row_grad[:, h], 'pair', axis=1, tiled=True)  83.7 us
    reduce_scatter x1, waiting for transfers between devices, shards(): lax.psum_scatter(partial_value, 'pair', scatter_dimension=1, tiled=True)  77.9 us
    all_to_all x1, blocking collectives, shards(): returned = lax.all_to_all(by_owner, ('gen', 'pair'), 0, 0, tiled=True)  29.3 us
    all_to_all x1, waiting for transfers between devices, shards(): incoming = lax.all_to_all(outgoing, ('gen', 'pair'), 0, 0, tiled=True)  18.4 us
    unnamed x24, local copies, waits for them, and re-layouts  13.6 us
    dot_general x2, matrix products, shards(): jnp.einsum('pc,ec->pe', grad_half, generator[:, h * half_cols:(h + 1) * h...  11.4 us
    dot_general x1, matrix products, shards(): jnp.dot(pair_embed, generator, preferred_element_type=jnp.float32)  10.1 us
    dot_general x1, matrix products, shards(): jnp.einsum('pe,pc->ec', pair_embed, grad_rounded, preferred_element_type=...  8.54 us
  transfers between devices with their start and end apart: 7, of which 5 were waited for; matrix products, arithmetic and copies ran while one was open for 10% of the time, Pallas kernels for 0%

profile of v6, /device:TPU:0, one launch (start us, length us, event | category | flops | bytes accessed | tf_op | source)
XLA Modules:
  0.0 294.5 jit_solution(5513611299201349321)
XLA Ops:
  7.2 0.0 copy-start
  7.2 0.0 reduce-scatter.2.cloned.1.call-start
  7.2 0.7 copy-done
  8.0 0.9 convolution_convert_fusion.4
  8.8 10.1 %fusion.25 = f32[16,65536]{1,0:T(8,128)} fusion(bf16[16,128]{1,0:T(8,128)(2,1)S(1)} %convolution_convert_fusion.4, bf16[128,65536]{1,0:T(8,128)(2,1)} %param.13), kind=kOutput, calls=%fused_computation.41 | convolution fusion | flops 268435456 | bytes 20975616 | tf_op jit(solution)/shard_map/dot_general | solution.py:24
  19.0 0.0 reduce-scatter.2.cloned.1.call-update
  19.0 0.5 broadcast.42
  19.5 0.1 copy-done.6
  19.6 0.7 reduce.3
  20.3 0.1 reshape_squeeze.3
  20.4 0.1 copy.33
  20.4 0.1 reshape.95
  20.5 0.1 reshape.93
  20.6 0.0 copy-start.5
  20.6 77.9 %reduce-scatter.2.cloned.1.call-done = f32[16,16384]{1,0:T(8,128)} async-done(((f32[16,65536]{1,0:T(8,128)}), f32[16,16384]{1,0:T(8,128)}) %reduce-scatter.2.cloned.1.call-update) | async-done | bytes 1048592 | tf_op jit(solution)/shard_map/reduce_scatter | solution.py:25
  98.6 1.3 convert_element_type.45
  99.9 0.1 copy.44
  100.0 0.6 gather_fusion
  100.6 1.1 broadcast_select_fusion
  101.7 5.1 %all-to-all-start = ((bf16[32,64,256]{2,1,0:T(8,128)(2,1)}), bf16[32,64,256]{2,1,0:T(8,128)(2,1)S(1)}, u32[]{:S(2)}, u32[]{:S(2)}) async-start(bf16[32,64,256]{2,1,0:T(8,128)(2,1)} %broadcast_select_fusion), calls=%async_computation.1 | async-start | bytes 2097152 | tf_op jit(solution)/shard_map/all_to_all | solution.py:32
  106.9 0.0 all-gather.7.cloned.1.call-start
  106.9 0.2 copy.32
  107.1 6.4 %copy.35 = bf16[1024,2048]{0,1:T(8,128)(2,1)} copy(bf16[1024,2048]{1,0:T(8,128)(2,1)} %param.7) | data formatting | bytes 8388608 | tf_op args[0]
  113.5 18.4 %all-to-all-done = bf16[32,64,256]{2,1,0:T(8,128)(2,1)S(1)} async-done(((bf16[32,64,256]{2,1,0:T(8,128)(2,1)}), bf16[32,64,256]{2,1,0:T(8,128)(2,1)S(1)}, u32[]{:S(2)}, u32[]{:S(2)}) %all-to-all-start) | async-done | bytes 1048608 | tf_op jit(solution)/shard_map/all_to_all | solution.py:32
  131.9 3.9 %multiply_convert_fusion = bf16[1024,256]{0,1:T(8,128)(2,1)S(1)} fusion(bf16[2048,256]{1,0:T(8,128)(2,1)S(1)} %bitcast.45, bf16[1024,2048]{1,0:T(8,128)(2,1)} %param.7, bf16[1024,256]{0,1:T(8,128)(2,1)S(1)} %copy.32), kind=kOutput, calls=%fused_computation.19 | convolution fusion | flops 1076363264 | bytes 6291456 | tf_op jit(solution)/shard_map/btd,bdr->btr/dot_general | solution.py:36
  135.8 1.3 fusion.7
  137.1 0.1 copy.37
  137.2 29.3 %all_to_all.10 = bf16[32,64,256]{2,1,0:T(8,128)(2,1)S(1)} all-to-all(bf16[32,64,256]{2,1,0:T(8,128)(2,1)S(1)} %bitcast.48), channel_id=1, replica_groups=mesh['pair'=4,'gen'=8] {'gen','pair'}, dimensions={0} | all-to-all | bytes 2097152 | tf_op jit(solution)/shard_map/all_to_all | solution.py:57
  166.6 0.7 convolution_convert_fusion.3
  167.2 0.2 copy.39
  167.4 0.1 reshape.97
  167.5 2.1 fusion.24
  169.6 0.0 all-gather.7.cloned.1.call-update
  169.6 0.2 all-gather.5.cloned.1.call-start
  169.8 0.5 all-gather.5.cloned.1.call-update
  170.3 45.2 %all-gather.7.cloned.1.call-done = bf16[16,1,32768]{2,1,0:T(2,128)(2,1)} async-done(((bf16[16,1,8192]{2,1,0:T(2,128)(2,1)}), bf16[16,1,32768]{2,1,0:T(2,128)(2,1)}) %all-gather.7.cloned.1.call-update) | async-done | bytes 1048592 | tf_op jit(solution)/shard_map/all_gather | solution.py:69
  215.5 2.7 copy.49
  218.3 5.6 %fusion = f32[16,128]{1,0:T(8,128)S(1)} fusion(bf16[16,32768]{1,0:T(8,128)(2,1)S(1)} %bitcast.42, bf16[128,65536]{1,0:T(8,128)(2,1)} %param.13), kind=kOutput, calls=%fused_computation.2 | convolution fusion | flops 134217728 | bytes 9445376 | tf_op jit(solution)/shard_map/pc,ec->pe/dot_general | solution.py:71
  223.9 38.5 %all-gather.5.cloned.1.call-done = bf16[16,1,32768]{2,1,0:T(2,128)(2,1)} async-done(((bf16[16,1,8192]{2,1,0:T(2,128)(2,1)}), bf16[16,1,32768]{2,1,0:T(2,128)(2,1)}) %all-gather.5.cloned.1.call-update) | async-done | bytes 1048592 | tf_op jit(solution)/shard_map/all_gather | solution.py:69
  262.4 2.7 copy.50
  265.2 5.7 %fusion.8 = f32[16,128]{1,0:T(8,128)S(1)} fusion(f32[16,128]{1,0:T(8,128)S(1)} %fusion, bf16[16,32768]{1,0:T(8,128)(2,1)S(1)} %bitcast.40, bf16[128,65536]{1,0:T(8,128)(2,1)} %param.13), kind=kOutput, calls=%fused_computation.14 | convolution fusion | flops 134219776 | bytes 9453568 | tf_op jit(solution)/shard_map/pc,ec->pe/dot_general | solution.py:71
  270.9 0.0 collective-permute-start
  271.0 1.2 collective-permute-done
  272.1 1.5 collective-permute-start.1
  273.6 3.3 %convolution_convert_fusion.1 = bf16[1024,2048]{1,0:T(8,128)(2,1)} fusion(bf16[1024,256]{0,1:T(8,128)(2,1)S(1)} %copy-done.4, bf16[2048,256]{1,0:T(8,128)(2,1)S(1)} %bitcast.46), kind=kOutput, calls=%fused_computation.6 | convolution fusion | flops 1075838976 | bytes 5767168 | tf_op jit(solution)/shard_map/btr,bdr->btd/dot_general | solution.py:42
  277.0 1.5 collective-permute-start.2
  278.5 8.5 %convolution_convert_fusion = bf16[128,65536]{1,0:T(8,128)(2,1)} fusion(bf16[16,128]{1,0:T(8,128)(2,1)S(1)} %convolution_convert_fusion.4, bf16[16,32768]{1,0:T(8,128)(2,1)S(1)} %bitcast.43, bf16[16,32768]{1,0:T(8,128)(2,1)S(1)} %bitcast.41), kind=kOutput, calls=%fused_computation.1 | convolution fusion | flops 281018368 | bytes 18878464 | tf_op jit(solution)/shard_map/pe,pc->ec/dot_general | solution.py:77
  287.0 1.0 fusion.13
  (21 shorter events, 0.1 us)
Async XLA Ops:
  7.2 0.8 copy-start
  7.2 91.4 %reduce-scatter.2.cloned.1.call-start = ((), (), s32[]{:S(2)}) async-start(), calls=%async_computation.3 | async-start | bytes 5242880 | tf_op jit(solution)/shard_map/reduce_scatter | solution.py:25
  19.0 0.7 copy-start.6
  20.6 86.3 %copy-start.5 = (bf16[1024,256]{1,0:T(8,128)(2,1)S(1)}, bf16[1024,256]{1,0:T(8,128)(2,1)}, u32[]{:S(2)}) copy-start(bf16[1024,256]{1,0:T(8,128)(2,1)} %param.8) | copy-start | bytes 1572868
  101.7 30.2 %all-to-all-start = ((bf16[32,64,256]{2,1,0:T(8,128)(2,1)}), bf16[32,64,256]{2,1,0:T(8,128)(2,1)S(1)}, u32[]{:S(2)}, u32[]{:S(2)}) async-start(bf16[32,64,256]{2,1,0:T(8,128)(2,1)} %broadcast_select_fusion), calls=%async_computation.1 | async-start | bytes 2097152 | tf_op jit(solution)/shard_map/all_to_all | solution.py:32
  106.9 108.7 %all-gather.7.cloned.1.call-start = ((), (), s32[]{:S(2)}) async-start(), calls=%async_computation.5 | async-start | bytes 2621440 | tf_op jit(solution)/shard_map/all_gather | solution.py:69
  131.9 3.9 %copy-start.2 = (bf16[1024,2048]{0,1:T(8,128)(2,1)S(1)}, bf16[1024,2048]{0,1:T(8,128)(2,1)}, u32[]{:S(2)}) copy-start(bf16[1024,2048]{0,1:T(8,128)(2,1)} %copy.35) | copy-start | bytes 12582916
  135.8 1.4 copy-start.3
  169.6 92.8 %all-gather.5.cloned.1.call-start = ((), (), s32[]{:S(2)}) async-start(), calls=%async_computation.4 | async-start | bytes 2621440 | tf_op jit(solution)/shard_map/all_gather | solution.py:69
  265.2 8.4 %copy-start.4 = (bf16[1024,256]{0,1:T(8,128)(2,1)S(1)}, bf16[1024,256]{0,1:T(8,128)(2,1)}, u32[]{:S(2)}) copy-start(bf16[1024,256]{0,1:T(8,128)(2,1)} %copy-done.3) | copy-start | bytes 1572868
  270.9 1.2 collective-permute-start
  272.1 4.8 %collective-permute-start.1 = (f32[16,128]{1,0:T(8,128)S(1)}, f32[16,128]{1,0:T(8,128)S(1)}, u32[]{:S(2)}, u32[]{:S(2)}) collective-permute-start(f32[16,128]{1,0:T(8,128)S(1)} %add.54), channel_id=1, source_target_pairs={{0,2},{1,3},{2,0},{3,1},{4,6},{5,7},{6,4},{7,5},{8,10},{9,11},{10,... | collective-permute-start | bytes 24584 | tf_op jit(solution)/shard_map/ppermute | solution.py:84
  277.0 10.1 %copy-start.7 = (s32[16]{0:T(128)S(1)}, s32[16]{0:T(128)}, u32[]{:S(2)}) copy-start(s32[16]{0:T(128)} %param.11) | copy-start | bytes 196
  277.0 10.1 %copy-start.8 = (s32[16]{0:T(128)S(1)}, s32[16]{0:T(128)}, u32[]{:S(2)}) copy-start(s32[16]{0:T(128)} %param.10) | copy-start | bytes 196
  277.0 10.1 %collective-permute-start.2 = (f32[16,128]{1,0:T(8,128)S(1)}, f32[16,128]{1,0:T(8,128)S(1)}, u32[]{:S(2)}, u32[]{:S(2)}) collective-permute-start(f32[16,128]{1,0:T(8,128)S(1)} %add.55), channel_id=1, source_target_pairs={{0,4},{1,5},{2,6},{3,7},{4,0},{5,1},{6,2},{7,3},{8,12},{9,13},{10,... | collective-permute-start | bytes 24584 | tf_op jit(solution)/shard_map/ppermute | solution.py:84
  278.5 9.5 %copy-start.1 = (f32[96,128]{1,0:T(8,128)S(1)}, f32[96,128]{1,0:T(8,128)}, u32[]{:S(2)}) copy-start(f32[96,128]{1,0:T(8,128)} %param.12) | copy-start | bytes 147460
Sparse Core Ops, SparseCore 0:
  19.1 79.4 reduce-scatter.1
  169.7 45.7 all-gather.6
  217.8 44.6 all-gather.4

commit v7 on v5

--- a/solution.py
+++ b/solution.py
@@ -2,8 +2,59 @@
 import jax.numpy as jnp
 from jax import lax
 from jax.sharding import PartitionSpec as P
+from jax.experimental import pallas as pl
+from jax.experimental.pallas import tpu as pltpu
 
 BLK = 1024
+TAIL_COLS = 4096
+
+
+def _tail_kernel(embed_t_ref, grad_ref, gen_ref, out_ref, pair_ref):
+    step = pl.program_id(0)
+    grad_tile = grad_ref[...]
+    out_ref[...] = jnp.dot(
+        embed_t_ref[...], grad_tile, preferred_element_type=jnp.float32
+    ).astype(out_ref.dtype)
+    part = lax.dot_general(
+        grad_tile, gen_ref[...], (((1,), (1,)), ((), ())), preferred_element_type=jnp.float32
+    )
+
+    @pl.when(step == 0)
+    def _():
+        pair_ref[...] = part
+
+    @pl.when(step > 0)
+    def _():
+        pair_ref[...] += part
+
+
+def grad_tail(embed_t, grad_rounded, generator):
+    feats, cols = generator.shape
+    pairs = grad_rounded.shape[0]
+    tile = min(TAIL_COLS, cols)
+    return pl.pallas_call(
+        _tail_kernel,
+        grid=(cols // tile,),
+        in_specs=[
+            pl.BlockSpec((feats, pairs), lambda i: (0, 0)),
+            pl.BlockSpec((pairs, tile), lambda i: (0, i)),
+            pl.BlockSpec((feats, tile), lambda i: (0, i)),
+        ],
+        out_specs=[
+            pl.BlockSpec((feats, tile), lambda i: (0, i)),
+            pl.BlockSpec((pairs, feats), lambda i: (0, 0)),
+        ],
+        out_shape=[
+            jax.ShapeDtypeStruct((feats, cols), jnp.bfloat16),
+            jax.ShapeDtypeStruct((pairs, feats), jnp.float32),
+        ],
+        compiler_params=pltpu.CompilerParams(dimension_semantics=("arbitrary",)),
+        cost_estimate=pl.CostEstimate(
+            flops=4 * feats * cols * pairs,
+            transcendentals=0,
+            bytes_accessed=2 * (2 * feats * cols + pairs * cols),
+        ),
+    )(embed_t, grad_rounded, generator)
 
 
 def shards(tokens, cotangent, block_pair, src_lang, tgt_lang, lang_embed, generator):
@@ -56,12 +107,7 @@
         .reshape(pair_count, quarter)
     )
     grad_rounded = lax.all_gather(row_grad, "pair", axis=1, tiled=True)
-    grad_generator = jnp.einsum(
-        "pe,pc->ec", pair_embed, grad_rounded, preferred_element_type=jnp.float32
-    ).astype(jnp.bfloat16)
-    partial_pair = jnp.einsum(
-        "pc,ec->pe", grad_rounded, generator, preferred_element_type=jnp.float32
-    )
+    grad_generator, partial_pair = grad_tail(pair_embed.T, grad_rounded, generator)
     grad_pair = partial_pair
     span = 1
     while span < gen_count:

time: 252 us -> 256 us (1.016)
  matrix products: 43.2 us -> 21.8 us
  Pallas kernels: 0 us -> 21.3 us
  waiting for transfers between devices: 143 us -> 146 us
    pallas_call x0 -> x1, Pallas kernels: none -> 21.3 us  [grad_tail(): pl.pallas_call(_tail_kernel, grid=(cols // tile,), in_specs=[pl.BlockSpec...]
    dot_general x2 -> x0, matrix products: 19.3 us -> none  [the longest x1 10.8 us: shards(): jnp.einsum('pc,ec->pe', grad_rounded, generator, preferred_element_type=j...]
    unnamed x20 -> x18, local copies, waits for them, and re-layouts: 8.13 us -> 8.12 us
  transfers between devices with their start and end apart: 6 -> 6, of which waited for: 4 -> 5; matrix products, arithmetic and copies ran while one was open for 8% -> 4% of each run, Pallas kernels for 0% -> 0%
where the time goes in v7:
time: 256 us; the launch traced here: 255 us
  waiting for transfers between devices  146 us (57%)
  blocking collectives  29.3 us (11%)
  matrix products  21.8 us (9%)
  Pallas kernels  21.3 us (8%)
  between operations  14.2 us (6%)
  local copies, waits for them, and re-layouts  10.5 us (4%)
  starting transfers between devices  8.24 us (3%)
  other arithmetic  3.79 us (1%)
    reduce_scatter x1, waiting for transfers between devices, shards(): lax.psum_scatter(partial_value, 'pair', scatter_dimension=1, tiled=True)  77.9 us
    all_gather x1, waiting for transfers between devices, shards(): grad_rounded = lax.all_gather(row_grad, 'pair', axis=1, tiled=True)  45.9 us
    all_to_all x1, blocking collectives, shards(): returned = lax.all_to_all(by_owner, ('gen', 'pair'), 0, 0, tiled=True)  29.3 us
    pallas_call x1, Pallas kernels, grad_tail(): pl.pallas_call(_tail_kernel, grid=(cols // tile,), in_specs=[pl.BlockSpec...  21.3 us
    all_to_all x1, waiting for transfers between devices, shards(): incoming = lax.all_to_all(outgoing, ('gen', 'pair'), 0, 0, tiled=True)  18.4 us
    dot_general x1, matrix products, shards(): jnp.dot(pair_embed, generator, preferred_element_type=jnp.float32)  9.06 us
    unnamed x18, local copies, waits for them, and re-layouts  8.12 us
  transfers between devices with their start and end apart: 6, of which 5 were waited for; matrix products, arithmetic and copies ran while one was open for 4% of the time, Pallas kernels for 0%

profile of v7, /device:TPU:0, one launch (start us, length us, event | category | flops | bytes accessed | tf_op | source)
XLA Modules:
  0.0 255.0 jit_solution(9022794345578497468)
XLA Ops:
  7.2 0.0 copy-start
  7.2 0.0 reduce-scatter.2.cloned.1.call-start
  7.2 0.7 copy-done
  8.0 1.0 convolution_convert_fusion.2
  9.0 0.0 copy-start.3
  9.0 9.1 %fusion.21 = f32[16,65536]{1,0:T(8,128)} fusion(bf16[16,128]{0,1:T(8,128)(2,1)S(1)} %convolution_convert_fusion.2, bf16[128,65536]{1,0:T(8,128)(2,1)} %gen_ref.1), kind=kOutput, calls=%fused_computation.31 | convolution fusion | flops 268435456 | bytes 20975616 | tf_op jit(solution)/shard_map/dot_general | solution.py:75
  18.0 0.0 copy-done.3
  18.0 0.0 reduce-scatter.2.cloned.1.call-update
  18.1 0.5 broadcast.42
  18.6 0.1 copy-done.4
  18.7 0.7 reduce.3
  19.3 0.1 reshape_squeeze.3
  19.4 0.1 copy.22
  19.5 0.1 reshape.93
  19.6 0.1 reshape.91
  19.7 0.0 copy-start.2
  19.7 77.9 %reduce-scatter.2.cloned.1.call-done = f32[16,16384]{1,0:T(8,128)} async-done(((f32[16,65536]{1,0:T(8,128)}), f32[16,16384]{1,0:T(8,128)}) %reduce-scatter.2.cloned.1.call-update) | async-done | bytes 1048592 | tf_op jit(solution)/shard_map/reduce_scatter | solution.py:76
  97.7 1.3 convert_element_type.43
  98.9 0.1 copy.35
  99.1 0.6 gather_fusion
  99.7 1.1 broadcast_select_fusion
  100.8 5.1 %all-to-all-start = ((bf16[32,64,256]{2,1,0:T(8,128)(2,1)}), bf16[32,64,256]{2,1,0:T(8,128)(2,1)S(1)}, u32[]{:S(2)}, u32[]{:S(2)}) async-start(bf16[32,64,256]{2,1,0:T(8,128)(2,1)} %broadcast_select_fusion), calls=%async_computation.1 | async-start | bytes 2097152 | tf_op jit(solution)/shard_map/all_to_all | solution.py:83
  105.9 0.0 all-gather.2.cloned.1.call-start
  106.0 0.0 copy-done.2
  106.0 0.2 copy.21
  106.2 6.4 %copy.25 = bf16[1024,2048]{0,1:T(8,128)(2,1)} copy(bf16[1024,2048]{1,0:T(8,128)(2,1)} %param.7) | data formatting | bytes 8388608 | tf_op args[0]
  112.6 18.4 %all-to-all-done = bf16[32,64,256]{2,1,0:T(8,128)(2,1)S(1)} async-done(((bf16[32,64,256]{2,1,0:T(8,128)(2,1)}), bf16[32,64,256]{2,1,0:T(8,128)(2,1)S(1)}, u32[]{:S(2)}, u32[]{:S(2)}) %all-to-all-start) | async-done | bytes 1048608 | tf_op jit(solution)/shard_map/all_to_all | solution.py:83
  131.0 3.9 %multiply_convert_fusion = bf16[1024,256]{0,1:T(8,128)(2,1)S(1)} fusion(bf16[2048,256]{1,0:T(8,128)(2,1)S(1)} %bitcast.34, bf16[1024,2048]{1,0:T(8,128)(2,1)} %param.7, bf16[1024,256]{0,1:T(8,128)(2,1)S(1)} %copy.21), kind=kOutput, calls=%fused_computation.11 | convolution fusion | flops 1076363264 | bytes 6291456 | tf_op jit(solution)/shard_map/btd,bdr->btr/dot_general | solution.py:87
  134.9 0.0 copy-done.1
  134.9 3.0 %fusion.5 = bf16[32,64,256]{2,0,1:T(8,128)(2,1)S(1)} fusion(bf16[32,64,1024]{2,1,0:T(8,128)(2,1)S(1)} %bitcast.36, bf16[1024,256]{0,1:T(8,128)(2,1)S(1)} %multiply_convert_fusion), kind=kOutput, calls=%fused_computation.5 | convolution fusion | flops 1074266112 | bytes 5767168 | tf_op jit(solution)/shard_map/btd,btr->bdr/dot_general | solution.py:97
  137.9 0.6 copy.28
  138.5 29.3 %all_to_all.10 = bf16[32,64,256]{2,1,0:T(8,128)(2,1)S(1)} all-to-all(bf16[32,64,256]{2,1,0:T(8,128)(2,1)S(1)} %copy.28), channel_id=1, replica_groups=mesh['pair'=4,'gen'=8] {'gen','pair'}, dimensions={0} | all-to-all | bytes 2097152 | tf_op jit(solution)/shard_map/all_to_all | solution.py:101
  167.8 0.7 fusion.8
  168.5 0.8 copy.34
  169.3 0.0 all-gather.2.cloned.1.call-update
  169.3 45.9 %all-gather.2.cloned.1.call-done.grad_ref = bf16[16,65536]{1,0:T(8,128)(2,1)} async-done(((bf16[16,16384]{1,0:T(8,128)(2,1)}), bf16[16,65536]{1,0:T(8,128)(2,1)}) %all-gather.2.cloned.1.call-update) | async-done | bytes 2097168 | tf_op jit(solution)/shard_map/all_gather | solution.py:109
  215.2 21.3 %shard_map.94 = (bf16[128,65536]{1,0:T(8,128)(2,1)}, f32[16,128]{1,0:T(8,128)}) custom-call(bf16[128,16]{1,0:T(8,128)(2,1)} %bitcast.39, bf16[16,65536]{1,0:T(8,128)(2,1)} %all-gather.2.cloned.1.call-done.grad_ref, bf16[128,65536]{1,0:T(8,128)(2,1)} %gen_ref.1), custom_call_target="tpu_custom_call" | custom-call | flops 536870912 | bytes 35651584 | tf_op jit(solution)/shard_map/pallas_call | solution.py:35
  236.5 0.0 collective-permute-start
  236.5 1.4 collective-permute-done
  237.9 0.7 add.50
  238.6 1.5 collective-permute-start.1
  240.1 2.2 collective-permute-done.1
  242.3 1.6 collective-permute-start.2
  243.8 3.3 %convolution_convert_fusion = bf16[1024,2048]{1,0:T(8,128)(2,1)} fusion(bf16[1024,256]{0,1:T(8,128)(2,1)S(1)} %multiply_convert_fusion, bf16[2048,256]{1,0:T(8,128)(2,1)S(1)} %bitcast.35), kind=kOutput, calls=%fused_computation.3 | convolution fusion | flops 1075838976 | bytes 5767168 | tf_op jit(solution)/shard_map/btr,bdr->btd/dot_general | solution.py:93
  247.2 0.0 collective-permute-done.2
  247.2 0.0 copy-done.5
  247.2 0.0 copy-done.6
  247.2 1.0 fusion.11
  (8 shorter events, 0.0 us)
Async XLA Ops:
  7.2 0.8 copy-start
  7.2 90.5 %reduce-scatter.2.cloned.1.call-start = ((), (), s32[]{:S(2)}) async-start(), calls=%async_computation.3 | async-start | bytes 5242880 | tf_op jit(solution)/shard_map/reduce_scatter | solution.py:76
  9.0 9.1 %copy-start.3 = (bf16[16,128]{0,1:T(8,128)(2,1)}, bf16[16,128]{0,1:T(8,128)(2,1)S(1)}, u32[]{:S(2)}) copy-start(bf16[16,128]{0,1:T(8,128)(2,1)S(1)} %convolution_convert_fusion.2) | copy-start | bytes 12292
  18.0 0.7 copy-start.4
  19.7 86.3 %copy-start.2 = (bf16[1024,256]{1,0:T(8,128)(2,1)S(1)}, bf16[1024,256]{1,0:T(8,128)(2,1)}, u32[]{:S(2)}) copy-start(bf16[1024,256]{1,0:T(8,128)(2,1)} %param.8) | copy-start | bytes 1572868
  100.8 30.2 %all-to-all-start = ((bf16[32,64,256]{2,1,0:T(8,128)(2,1)}), bf16[32,64,256]{2,1,0:T(8,128)(2,1)S(1)}, u32[]{:S(2)}, u32[]{:S(2)}) async-start(bf16[32,64,256]{2,1,0:T(8,128)(2,1)} %broadcast_select_fusion), calls=%async_computation.1 | async-start | bytes 2097152 | tf_op jit(solution)/shard_map/all_to_all | solution.py:83
  105.9 109.3 %all-gather.2.cloned.1.call-start = ((), (), s32[]{:S(2)}) async-start(), calls=%async_computation.4 | async-start | bytes 2621440 | tf_op jit(solution)/shard_map/all_gather | solution.py:109
  131.0 3.9 %copy-start.1 = (bf16[1024,2048]{0,1:T(8,128)(2,1)S(1)}, bf16[1024,2048]{0,1:T(8,128)(2,1)}, u32[]{:S(2)}) copy-start(bf16[1024,2048]{0,1:T(8,128)(2,1)} %copy.25) | copy-start | bytes 12582916
  236.5 1.4 collective-permute-start
  238.6 3.7 %collective-permute-start.1 = (f32[16,128]{1,0:T(8,128)S(1)}, f32[16,128]{1,0:T(8,128)S(1)}, u32[]{:S(2)}, u32[]{:S(2)}) collective-permute-start(f32[16,128]{1,0:T(8,128)S(1)} %add.50), channel_id=1, source_target_pairs={{0,2},{1,3},{2,0},{3,1},{4,6},{5,7},{6,4},{7,5},{8,10},{9,11},{10,... | collective-permute-start | bytes 24584 | tf_op jit(solution)/shard_map/ppermute | solution.py:115
  242.3 4.9 %copy-start.5 = (s32[16]{0:T(128)S(1)}, s32[16]{0:T(128)}, u32[]{:S(2)}) copy-start(s32[16]{0:T(128)} %param.11) | copy-start | bytes 196
  242.3 4.9 %copy-start.6 = (s32[16]{0:T(128)S(1)}, s32[16]{0:T(128)}, u32[]{:S(2)}) copy-start(s32[16]{0:T(128)} %param.10) | copy-start | bytes 196
  242.3 4.9 %collective-permute-start.2 = (f32[16,128]{1,0:T(8,128)S(1)}, f32[16,128]{1,0:T(8,128)S(1)}, u32[]{:S(2)}, u32[]{:S(2)}) collective-permute-start(f32[16,128]{1,0:T(8,128)S(1)} %add.51), channel_id=1, source_target_pairs={{0,4},{1,5},{2,6},{3,7},{4,0},{5,1},{6,2},{7,3},{8,12},{9,13},{10,... | collective-permute-start | bytes 24584 | tf_op jit(solution)/shard_map/ppermute | solution.py:115
Sparse Core Ops, SparseCore 0:
  18.2 79.4 reduce-scatter.1
  169.4 45.7 all-gather.1

commit v8 on v7

--- a/solution.py
+++ b/solution.py
@@ -6,7 +6,7 @@
 from jax.experimental.pallas import tpu as pltpu
 
 BLK = 1024
-TAIL_COLS = 4096
+TAIL_COLS = 8192
 
 
 def _tail_kernel(embed_t_ref, grad_ref, gen_ref, out_ref, pair_ref):
@@ -16,7 +16,7 @@
         embed_t_ref[...], grad_tile, preferred_element_type=jnp.float32
     ).astype(out_ref.dtype)
     part = lax.dot_general(
-        grad_tile, gen_ref[...], (((1,), (1,)), ((), ())), preferred_element_type=jnp.float32
+        gen_ref[...], grad_tile, (((1,), (1,)), ((), ())), preferred_element_type=jnp.float32
     )
 
     @pl.when(step == 0)
@@ -42,11 +42,11 @@
         ],
         out_specs=[
             pl.BlockSpec((feats, tile), lambda i: (0, i)),
-            pl.BlockSpec((pairs, feats), lambda i: (0, 0)),
+            pl.BlockSpec((feats, pairs), lambda i: (0, 0)),
         ],
         out_shape=[
             jax.ShapeDtypeStruct((feats, cols), jnp.bfloat16),
-            jax.ShapeDtypeStruct((pairs, feats), jnp.float32),
+            jax.ShapeDtypeStruct((feats, pairs), jnp.float32),
         ],
         compiler_params=pltpu.CompilerParams(dimension_semantics=("arbitrary",)),
         cost_estimate=pl.CostEstimate(
@@ -107,7 +107,8 @@
         .reshape(pair_count, quarter)
     )
     grad_rounded = lax.all_gather(row_grad, "pair", axis=1, tiled=True)
-    grad_generator, partial_pair = grad_tail(pair_embed.T, grad_rounded, generator)
+    grad_generator, pair_part_t = grad_tail(pair_embed.T, grad_rounded, generator)
+    partial_pair = pair_part_t.T
     grad_pair = partial_pair
     span = 1
     while span < gen_count:

time: 256 us -> 253 us (0.988)
  Pallas kernels: 21.3 us -> 18.1 us
    pallas_call x1, Pallas kernels: 21.3 us -> 18.1 us  [grad_tail(): pl.pallas_call(_tail_kernel, grid=(cols // tile,), in_specs=[pl.BlockSpec...]
  transfers between devices with their start and end apart: 6 -> 6, of which waited for: 5 -> 5; matrix products, arithmetic and copies ran while one was open for 4% -> 5% of each run, Pallas kernels for 0% -> 0%
where the time goes in v8:
time: 253 us
  waiting for transfers between devices  147 us (58%)
  blocking collectives  29.3 us (12%)
  matrix products  21.9 us (9%)
  Pallas kernels  18.1 us (7%)
  between operations  14.2 us (6%)
  local copies, waits for them, and re-layouts  10.5 us (4%)
  starting transfers between devices  8.25 us (3%)
  other arithmetic  3.95 us (2%)
    reduce_scatter x1, waiting for transfers between devices, shards(): lax.psum_scatter(partial_value, 'pair', scatter_dimension=1, tiled=True)  77.9 us
    all_gather x1, waiting for transfers between devices, shards(): grad_rounded = lax.all_gather(row_grad, 'pair', axis=1, tiled=True)  45.9 us
    all_to_all x1, blocking collectives, shards(): returned = lax.all_to_all(by_owner, ('gen', 'pair'), 0, 0, tiled=True)  29.3 us
    all_to_all x1, waiting for transfers between devices, shards(): incoming = lax.all_to_all(outgoing, ('gen', 'pair'), 0, 0, tiled=True)  18.4 us
    pallas_call x1, Pallas kernels, grad_tail(): pl.pallas_call(_tail_kernel, grid=(cols // tile,), in_specs=[pl.BlockSpec...  18.1 us
    dot_general x1, matrix products, shards(): jnp.dot(pair_embed, generator, preferred_element_type=jnp.float32)  9.06 us
    unnamed x18, local copies, waits for them, and re-layouts  8.13 us
    all_to_all x1, starting transfers between devices, shards(): incoming = lax.all_to_all(outgoing, ('gen', 'pair'), 0, 0, tiled=True)  5.11 us
  transfers between devices with their start and end apart: 6, of which 5 were waited for; matrix products, arithmetic and copies ran while one was open for 5% of the time, Pallas kernels for 0%

profile of v8, /device:TPU:0, one launch (start us, length us, event | category | flops | bytes accessed | tf_op | source)
XLA Modules:
  0.0 252.7 jit_solution(7670876374737210803)
XLA Ops:
  7.2 0.0 copy-start
  7.2 0.0 reduce-scatter.2.cloned.1.call-start
  7.2 0.7 copy-done
  8.0 1.0 convolution_convert_fusion.2
  9.0 0.0 copy-start.3
  9.0 9.1 %fusion.21 = f32[16,65536]{1,0:T(8,128)} fusion(bf16[16,128]{0,1:T(8,128)(2,1)S(1)} %convolution_convert_fusion.2, bf16[128,65536]{1,0:T(8,128)(2,1)} %gen_ref.1), kind=kOutput, calls=%fused_computation.32 | convolution fusion | flops 268435456 | bytes 20975616 | tf_op jit(solution)/shard_map/dot_general | solution.py:75
  18.0 0.0 copy-done.3
  18.0 0.0 reduce-scatter.2.cloned.1.call-update
  18.1 0.5 broadcast.42
  18.6 0.1 copy-done.6
  18.7 0.7 reduce.3
  19.3 0.1 reshape_squeeze.3
  19.4 0.1 copy.22
  19.5 0.1 reshape.93
  19.6 0.1 reshape.91
  19.7 0.0 copy-start.2
  19.7 77.9 %reduce-scatter.2.cloned.1.call-done = f32[16,16384]{1,0:T(8,128)} async-done(((f32[16,65536]{1,0:T(8,128)}), f32[16,16384]{1,0:T(8,128)}) %reduce-scatter.2.cloned.1.call-update) | async-done | bytes 1048592 | tf_op jit(solution)/shard_map/reduce_scatter | solution.py:76
  97.7 1.3 convert_element_type.43
  98.9 0.1 copy.35
  99.1 0.6 gather_fusion
  99.7 1.1 broadcast_select_fusion
  100.8 5.1 %all-to-all-start = ((bf16[32,64,256]{2,1,0:T(8,128)(2,1)}), bf16[32,64,256]{2,1,0:T(8,128)(2,1)S(1)}, u32[]{:S(2)}, u32[]{:S(2)}) async-start(bf16[32,64,256]{2,1,0:T(8,128)(2,1)} %broadcast_select_fusion), calls=%async_computation.1 | async-start | bytes 2097152 | tf_op jit(solution)/shard_map/all_to_all | solution.py:83
  105.9 0.0 all-gather.2.cloned.1.call-start
  106.0 0.0 copy-done.2
  106.0 0.2 copy.21
  106.2 6.4 %copy.25 = bf16[1024,2048]{0,1:T(8,128)(2,1)} copy(bf16[1024,2048]{1,0:T(8,128)(2,1)} %param.7) | data formatting | bytes 8388608 | tf_op args[0]
  112.6 18.4 %all-to-all-done = bf16[32,64,256]{2,1,0:T(8,128)(2,1)S(1)} async-done(((bf16[32,64,256]{2,1,0:T(8,128)(2,1)}), bf16[32,64,256]{2,1,0:T(8,128)(2,1)S(1)}, u32[]{:S(2)}, u32[]{:S(2)}) %all-to-all-start) | async-done | bytes 1048608 | tf_op jit(solution)/shard_map/all_to_all | solution.py:83
  131.0 3.9 %multiply_convert_fusion = bf16[1024,256]{0,1:T(8,128)(2,1)S(1)} fusion(bf16[2048,256]{1,0:T(8,128)(2,1)S(1)} %bitcast.36, bf16[1024,2048]{1,0:T(8,128)(2,1)} %param.7, bf16[1024,256]{0,1:T(8,128)(2,1)S(1)} %copy.21), kind=kOutput, calls=%fused_computation.11 | convolution fusion | flops 1076363264 | bytes 6291456 | tf_op jit(solution)/shard_map/btd,bdr->btr/dot_general | solution.py:87
  134.9 3.0 %fusion.5 = bf16[32,64,256]{2,0,1:T(8,128)(2,1)S(1)} fusion(bf16[32,64,1024]{2,1,0:T(8,128)(2,1)S(1)} %bitcast.38, bf16[1024,256]{0,1:T(8,128)(2,1)S(1)} %multiply_convert_fusion), kind=kOutput, calls=%fused_computation.5 | convolution fusion | flops 1074266112 | bytes 5767168 | tf_op jit(solution)/shard_map/btd,btr->bdr/dot_general | solution.py:97
  137.9 0.6 copy.28
  138.5 29.3 %all_to_all.10 = bf16[32,64,256]{2,1,0:T(8,128)(2,1)S(1)} all-to-all(bf16[32,64,256]{2,1,0:T(8,128)(2,1)S(1)} %copy.28), channel_id=1, replica_groups=mesh['pair'=4,'gen'=8] {'gen','pair'}, dimensions={0} | all-to-all | bytes 2097152 | tf_op jit(solution)/shard_map/all_to_all | solution.py:101
  167.8 0.7 fusion.8
  168.5 0.8 copy.34
  169.3 0.0 all-gather.2.cloned.1.call-update
  169.3 45.9 %all-gather.2.cloned.1.call-done.grad_ref = bf16[16,65536]{1,0:T(8,128)(2,1)} async-done(((bf16[16,16384]{1,0:T(8,128)(2,1)}), bf16[16,65536]{1,0:T(8,128)(2,1)}) %all-gather.2.cloned.1.call-update) | async-done | bytes 2097168 | tf_op jit(solution)/shard_map/all_gather | solution.py:109
  215.2 18.1 %shard_map.94 = (bf16[128,65536]{1,0:T(8,128)(2,1)}, f32[128,16]{1,0:T(8,128)}) custom-call(bf16[128,16]{1,0:T(8,128)(2,1)} %bitcast.41, bf16[16,65536]{1,0:T(8,128)(2,1)} %all-gather.2.cloned.1.call-done.grad_ref, bf16[128,65536]{1,0:T(8,128)(2,1)} %gen_ref.1), custom_call_target="tpu_custom_call" | custom-call | flops 536870912 | bytes 35651584 | tf_op jit(solution)/shard_map/pallas_call | solution.py:35
  233.4 0.0 collective-permute-start
  233.4 1.5 collective-permute-done
  234.8 0.9 bitcast_add_fusion
  235.7 1.5 collective-permute-start.1
  237.2 2.8 %collective-permute-done.1 = f32[16,128]{0,1:T(8,128)S(1)} collective-permute-done((f32[16,128]{0,1:T(8,128)S(1)}, f32[16,128]{0,1:T(8,128)S(1)}, u32[]{:S(2)}, u32[]{:S(2)}) %collective-permute-start.1) | collective-permute-done | bytes 8224 | tf_op jit(solution)/shard_map/ppermute | solution.py:116
  240.0 0.0 copy-start.4
  240.0 0.0 copy-start.5
  240.0 1.5 collective-permute-start.2
  241.6 3.3 %convolution_convert_fusion = bf16[1024,2048]{1,0:T(8,128)(2,1)} fusion(bf16[1024,256]{0,1:T(8,128)(2,1)S(1)} %multiply_convert_fusion, bf16[2048,256]{1,0:T(8,128)(2,1)S(1)} %bitcast.37), kind=kOutput, calls=%fused_computation.3 | convolution fusion | flops 1075838976 | bytes 5767168 | tf_op jit(solution)/shard_map/btr,bdr->btd/dot_general | solution.py:93
  244.9 0.0 collective-permute-done.2
  244.9 0.0 copy-done.5
  244.9 1.0 fusion.11
  (8 shorter events, 0.0 us)
Async XLA Ops:
  7.2 0.8 copy-start
  7.2 90.5 %reduce-scatter.2.cloned.1.call-start = ((), (), s32[]{:S(2)}) async-start(), calls=%async_computation.3 | async-start | bytes 5242880 | tf_op jit(solution)/shard_map/reduce_scatter | solution.py:76
  9.0 9.1 %copy-start.3 = (bf16[16,128]{0,1:T(8,128)(2,1)}, bf16[16,128]{0,1:T(8,128)(2,1)S(1)}, u32[]{:S(2)}) copy-start(bf16[16,128]{0,1:T(8,128)(2,1)S(1)} %convolution_convert_fusion.2) | copy-start | bytes 12292
  18.0 0.7 copy-start.6
  19.7 86.3 %copy-start.2 = (bf16[1024,256]{1,0:T(8,128)(2,1)S(1)}, bf16[1024,256]{1,0:T(8,128)(2,1)}, u32[]{:S(2)}) copy-start(bf16[1024,256]{1,0:T(8,128)(2,1)} %param.8) | copy-start | bytes 1572868
  100.8 30.2 %all-to-all-start = ((bf16[32,64,256]{2,1,0:T(8,128)(2,1)}), bf16[32,64,256]{2,1,0:T(8,128)(2,1)S(1)}, u32[]{:S(2)}, u32[]{:S(2)}) async-start(bf16[32,64,256]{2,1,0:T(8,128)(2,1)} %broadcast_select_fusion), calls=%async_computation.1 | async-start | bytes 2097152 | tf_op jit(solution)/shard_map/all_to_all | solution.py:83
  105.9 109.3 %all-gather.2.cloned.1.call-start = ((), (), s32[]{:S(2)}) async-start(), calls=%async_computation.4 | async-start | bytes 2621440 | tf_op jit(solution)/shard_map/all_gather | solution.py:109
  131.0 3.9 %copy-start.1 = (bf16[1024,2048]{0,1:T(8,128)(2,1)S(1)}, bf16[1024,2048]{0,1:T(8,128)(2,1)}, u32[]{:S(2)}) copy-start(bf16[1024,2048]{0,1:T(8,128)(2,1)} %copy.25) | copy-start | bytes 12582916
  233.4 1.5 collective-permute-start
  235.7 4.3 %collective-permute-start.1 = (f32[16,128]{0,1:T(8,128)S(1)}, f32[16,128]{0,1:T(8,128)S(1)}, u32[]{:S(2)}, u32[]{:S(2)}) collective-permute-start(f32[16,128]{0,1:T(8,128)S(1)} %bitcast_add_fusion), channel_id=1, source_target_pairs={{0,2},{1,3},{2,0},{3,1},{4,6},{5,7},{6,4},{7,5},{8,10},{9,11},{10,... | collective-permute-start | bytes 24584 | tf_op jit(solution)/shard_map/ppermute | solution.py:116
  240.0 4.9 %copy-start.4 = (s32[16]{0:T(128)S(1)}, s32[16]{0:T(128)}, u32[]{:S(2)}) copy-start(s32[16]{0:T(128)} %param.11) | copy-start | bytes 196
  240.0 4.9 %copy-start.5 = (s32[16]{0:T(128)S(1)}, s32[16]{0:T(128)}, u32[]{:S(2)}) copy-start(s32[16]{0:T(128)} %param.10) | copy-start | bytes 196
  240.0 4.9 %collective-permute-start.2 = (f32[16,128]{0,1:T(8,128)S(1)}, f32[16,128]{0,1:T(8,128)S(1)}, u32[]{:S(2)}, u32[]{:S(2)}) collective-permute-start(f32[16,128]{0,1:T(8,128)S(1)} %add.51), channel_id=1, source_target_pairs={{0,4},{1,5},{2,6},{3,7},{4,0},{5,1},{6,2},{7,3},{8,12},{9,13},{10,... | collective-permute-start | bytes 24584 | tf_op jit(solution)/shard_map/ppermute | solution.py:116
Sparse Core Ops, SparseCore 0:
  18.2 79.4 reduce-scatter.1
  169.4 45.7 all-gather.1

commit v9 on v8

--- a/solution.py
+++ b/solution.py
@@ -110,11 +110,16 @@
     grad_generator, pair_part_t = grad_tail(pair_embed.T, grad_rounded, generator)
     partial_pair = pair_part_t.T
     grad_pair = partial_pair
-    span = 1
-    while span < gen_count:
-        swap = [(i, i ^ span) for i in range(gen_count)]
-        grad_pair = grad_pair + lax.ppermute(grad_pair, "gen", swap)
-        span *= 2
+    if gen_count <= 8:
+        for shift in range(1, gen_count):
+            ring = [(i, (i + shift) % gen_count) for i in range(gen_count)]
+            grad_pair = grad_pair + lax.ppermute(partial_pair, "gen", ring)
+    else:
+        span = 1
+        while span < gen_count:
+            swap = [(i, i ^ span) for i in range(gen_count)]
+            grad_pair = grad_pair + lax.ppermute(grad_pair, "gen", swap)
+            span *= 2
     grad_embed = jnp.dot(hot_both.T, grad_pair, precision=lax.Precision.HIGHEST)
     return (grad_tokens, grad_generator, grad_embed)
 

time: 253 us -> 253 us (level)
  starting transfers between devices: 8.25 us -> 13 us
  waiting for transfers between devices: 147 us -> 143 us
    ppermute x3 -> x7, starting transfers between devices: 3.06 us -> 7.79 us  [shards(): grad_pair = grad_pair + lax.ppermute(partial_pair, 'gen', ring)]
    ppermute x3 -> x7, waiting for transfers between devices: 4.26 us -> 0.5 us  [shards(): grad_pair = grad_pair + lax.ppermute(partial_pair, 'gen', ring)]
    unnamed x18 -> x20, local copies, waits for them, and re-layouts: 8.13 us -> 8.13 us
  transfers between devices with their start and end apart: 6 -> 10, of which waited for: 5 -> 4; matrix products, arithmetic and copies ran while one was open for 5% -> 5% of each run, Pallas kernels for 0% -> 0%
where the time goes in v9:
time: 253 us
  waiting for transfers between devices  143 us (57%)
  blocking collectives  29.3 us (12%)
  matrix products  21.9 us (9%)
  Pallas kernels  18.1 us (7%)
  between operations  14.2 us (6%)
  starting transfers between devices  13 us (5%)
  local copies, waits for them, and re-layouts  10.5 us (4%)
  other arithmetic  3.09 us (1%)
    reduce_scatter x1, waiting for transfers between devices, shards(): lax.psum_scatter(partial_value, 'pair', scatter_dimension=1, tiled=True)  77.9 us
    all_gather x1, waiting for transfers between devices, shards(): grad_rounded = lax.all_gather(row_grad, 'pair', axis=1, tiled=True)  45.9 us
    all_to_all x1, blocking collectives, shards(): returned = lax.all_to_all(by_owner, ('gen', 'pair'), 0, 0, tiled=True)  29.3 us
    all_to_all x1, waiting for transfers between devices, shards(): incoming = lax.all_to_all(outgoing, ('gen', 'pair'), 0, 0, tiled=True)  18.4 us
    pallas_call x1, Pallas kernels, grad_tail(): pl.pallas_call(_tail_kernel, grid=(cols // tile,), in_specs=[pl.BlockSpec...  18.1 us
    dot_general x1, matrix products, shards(): jnp.dot(pair_embed, generator, preferred_element_type=jnp.float32)  9.06 us
    unnamed x20, local copies, waits for them, and re-layouts  8.13 us
    ppermute x7, starting transfers between devices, shards(): grad_pair = grad_pair + lax.ppermute(partial_pair, 'gen', ring)  7.79 us
  transfers between devices with their start and end apart: 10, of which 4 were waited for; matrix products, arithmetic and copies ran while one was open for 5% of the time, Pallas kernels for 0%

profile of v9, /device:TPU:0, one launch (start us, length us, event | category | flops | bytes accessed | tf_op | source)
XLA Modules:
  0.0 252.9 jit_solution(12552873692835616810)
XLA Ops:
  7.2 0.0 copy-start
  7.2 0.0 reduce-scatter.2.cloned.1.call-start
  7.2 0.7 copy-done
  8.0 1.0 convolution_convert_fusion.2
  9.0 0.0 copy-start.3
  9.0 9.1 %fusion.28 = f32[16,65536]{1,0:T(8,128)} fusion(bf16[16,128]{0,1:T(8,128)(2,1)S(1)} %convolution_convert_fusion.2, bf16[128,65536]{1,0:T(8,128)(2,1)} %gen_ref.1), kind=kOutput, calls=%fused_computation.38 | convolution fusion | flops 268435456 | bytes 20975616 | tf_op jit(solution)/shard_map/dot_general | solution.py:75
  18.0 0.0 reduce-scatter.2.cloned.1.call-update
  18.1 0.5 broadcast.42
  18.6 0.1 copy-done.7
  18.7 0.7 reduce.3
  19.3 0.1 reshape_squeeze.3
  19.4 0.1 copy.22
  19.5 0.1 reshape.93
  19.6 0.1 reshape.91
  19.7 0.0 copy-start.2
  19.7 77.9 %reduce-scatter.2.cloned.1.call-done = f32[16,16384]{1,0:T(8,128)} async-done(((f32[16,65536]{1,0:T(8,128)}), f32[16,16384]{1,0:T(8,128)}) %reduce-scatter.2.cloned.1.call-update) | async-done | bytes 1048592 | tf_op jit(solution)/shard_map/reduce_scatter | solution.py:76
  97.7 1.3 convert_element_type.43
  98.9 0.1 copy.35
  99.1 0.6 gather_fusion
  99.7 1.1 broadcast_select_fusion
  100.8 5.1 %all-to-all-start = ((bf16[32,64,256]{2,1,0:T(8,128)(2,1)}), bf16[32,64,256]{2,1,0:T(8,128)(2,1)S(1)}, u32[]{:S(2)}, u32[]{:S(2)}) async-start(bf16[32,64,256]{2,1,0:T(8,128)(2,1)} %broadcast_select_fusion), calls=%async_computation.1 | async-start | bytes 2097152 | tf_op jit(solution)/shard_map/all_to_all | solution.py:83
  105.9 0.0 all-gather.2.cloned.1.call-start
  106.0 0.2 copy.21
  106.2 6.4 %copy.25 = bf16[1024,2048]{0,1:T(8,128)(2,1)} copy(bf16[1024,2048]{1,0:T(8,128)(2,1)} %param.7) | data formatting | bytes 8388608 | tf_op args[0]
  112.6 18.4 %all-to-all-done = bf16[32,64,256]{2,1,0:T(8,128)(2,1)S(1)} async-done(((bf16[32,64,256]{2,1,0:T(8,128)(2,1)}), bf16[32,64,256]{2,1,0:T(8,128)(2,1)S(1)}, u32[]{:S(2)}, u32[]{:S(2)}) %all-to-all-start) | async-done | bytes 1048608 | tf_op jit(solution)/shard_map/all_to_all | solution.py:83
  131.0 3.9 %multiply_convert_fusion = bf16[1024,256]{0,1:T(8,128)(2,1)S(1)} fusion(bf16[2048,256]{1,0:T(8,128)(2,1)S(1)} %bitcast.39, bf16[1024,2048]{1,0:T(8,128)(2,1)} %param.7, bf16[1024,256]{0,1:T(8,128)(2,1)S(1)} %copy.21), kind=kOutput, calls=%fused_computation.11 | convolution fusion | flops 1076363264 | bytes 6291456 | tf_op jit(solution)/shard_map/btd,bdr->btr/dot_general | solution.py:87
  134.9 3.0 %fusion.5 = bf16[32,64,256]{2,0,1:T(8,128)(2,1)S(1)} fusion(bf16[32,64,1024]{2,1,0:T(8,128)(2,1)S(1)} %bitcast.41, bf16[1024,256]{0,1:T(8,128)(2,1)S(1)} %multiply_convert_fusion), kind=kOutput, calls=%fused_computation.5 | convolution fusion | flops 1074266112 | bytes 5767168 | tf_op jit(solution)/shard_map/btd,btr->bdr/dot_general | solution.py:97
  137.9 0.6 copy.28
  138.5 29.3 %all_to_all.10 = bf16[32,64,256]{2,1,0:T(8,128)(2,1)S(1)} all-to-all(bf16[32,64,256]{2,1,0:T(8,128)(2,1)S(1)} %copy.28), channel_id=1, replica_groups=mesh['pair'=4,'gen'=8] {'gen','pair'}, dimensions={0} | all-to-all | bytes 2097152 | tf_op jit(solution)/shard_map/all_to_all | solution.py:101
  167.8 0.7 fusion.8
  168.5 0.8 copy.34
  169.3 0.0 all-gather.2.cloned.1.call-update
  169.3 45.9 %all-gather.2.cloned.1.call-done.grad_ref = bf16[16,65536]{1,0:T(8,128)(2,1)} async-done(((bf16[16,16384]{1,0:T(8,128)(2,1)}), bf16[16,65536]{1,0:T(8,128)(2,1)}) %all-gather.2.cloned.1.call-update) | async-done | bytes 2097168 | tf_op jit(solution)/shard_map/all_gather | solution.py:109
  215.2 18.1 %shard_map.94 = (bf16[128,65536]{1,0:T(8,128)(2,1)}, f32[128,16]{1,0:T(8,128)}) custom-call(bf16[128,16]{1,0:T(8,128)(2,1)} %bitcast.44, bf16[16,65536]{1,0:T(8,128)(2,1)} %all-gather.2.cloned.1.call-done.grad_ref, bf16[128,65536]{1,0:T(8,128)(2,1)} %gen_ref.1), custom_call_target="tpu_custom_call" | custom-call | flops 536870912 | bytes 35651584 | tf_op jit(solution)/shard_map/pallas_call | solution.py:35
  233.4 0.0 copy-start.6
  233.4 0.1 collective-permute-start
  233.5 1.5 collective-permute-start.1
  235.0 2.3 collective-permute-start.2
  237.3 0.6 collective-permute-start.3
  237.8 0.1 collective-permute-start.4
  237.9 0.5 collective-permute-done
  238.4 1.4 collective-permute-start.5
  239.8 0.0 collective-permute-done.1
  239.8 1.9 collective-permute-start.6
  241.7 3.3 %convolution_convert_fusion = bf16[1024,2048]{1,0:T(8,128)(2,1)} fusion(bf16[1024,256]{0,1:T(8,128)(2,1)S(1)} %multiply_convert_fusion, bf16[2048,256]{1,0:T(8,128)(2,1)S(1)} %bitcast.40), kind=kOutput, calls=%fused_computation.3 | convolution fusion | flops 1075838976 | bytes 5767168 | tf_op jit(solution)/shard_map/btr,bdr->btd/dot_general | solution.py:93
  245.0 0.0 collective-permute-done.2
  245.0 0.0 collective-permute-done.3
  245.1 1.0 fusion.11
  (16 shorter events, 0.0 us)
Async XLA Ops:
  7.2 0.8 copy-start
  7.2 90.5 %reduce-scatter.2.cloned.1.call-start = ((), (), s32[]{:S(2)}) async-start(), calls=%async_computation.3 | async-start | bytes 5242880 | tf_op jit(solution)/shard_map/reduce_scatter | solution.py:76
  9.0 9.1 %copy-start.3 = (bf16[16,128]{0,1:T(8,128)(2,1)}, bf16[16,128]{0,1:T(8,128)(2,1)S(1)}, u32[]{:S(2)}) copy-start(bf16[16,128]{0,1:T(8,128)(2,1)S(1)} %convolution_convert_fusion.2) | copy-start | bytes 12292
  18.0 0.7 copy-start.7
  19.7 86.3 %copy-start.2 = (bf16[1024,256]{1,0:T(8,128)(2,1)S(1)}, bf16[1024,256]{1,0:T(8,128)(2,1)}, u32[]{:S(2)}) copy-start(bf16[1024,256]{1,0:T(8,128)(2,1)} %param.8) | copy-start | bytes 1572868
  100.8 30.2 %all-to-all-start = ((bf16[32,64,256]{2,1,0:T(8,128)(2,1)}), bf16[32,64,256]{2,1,0:T(8,128)(2,1)S(1)}, u32[]{:S(2)}, u32[]{:S(2)}) async-start(bf16[32,64,256]{2,1,0:T(8,128)(2,1)} %broadcast_select_fusion), calls=%async_computation.1 | async-start | bytes 2097152 | tf_op jit(solution)/shard_map/all_to_all | solution.py:83
  105.9 109.3 %all-gather.2.cloned.1.call-start = ((), (), s32[]{:S(2)}) async-start(), calls=%async_computation.4 | async-start | bytes 2621440 | tf_op jit(solution)/shard_map/all_gather | solution.py:109
  131.0 3.9 %copy-start.1 = (bf16[1024,2048]{0,1:T(8,128)(2,1)S(1)}, bf16[1024,2048]{0,1:T(8,128)(2,1)}, u32[]{:S(2)}) copy-start(bf16[1024,2048]{0,1:T(8,128)(2,1)} %copy.25) | copy-start | bytes 12582916
  233.4 11.7 %copy-start.4 = (f32[128,16]{1,0:T(8,128)S(1)}, f32[128,16]{1,0:T(8,128)}, u32[]{:S(2)}) copy-start(f32[128,16]{1,0:T(8,128)} %get-tuple-element.6) | copy-start | bytes 24580
  233.4 11.7 %copy-start.5 = (s32[16]{0:T(128)S(1)}, s32[16]{0:T(128)}, u32[]{:S(2)}) copy-start(s32[16]{0:T(128)} %param.11) | copy-start | bytes 196
  233.4 11.7 %copy-start.6 = (s32[16]{0:T(128)S(1)}, s32[16]{0:T(128)}, u32[]{:S(2)}) copy-start(s32[16]{0:T(128)} %param.10) | copy-start | bytes 196
  233.4 5.0 %collective-permute-start = (f32[16,128]{0,1:T(8,128)}, f32[16,128]{0,1:T(8,128)S(1)}, u32[]{:S(2)}, u32[]{:S(2)}) collective-permute-start(f32[16,128]{0,1:T(8,128)} %bitcast.45), channel_id=1, source_target_pairs={{0,1},{1,2},{2,3},{3,4},{4,5},{5,6},{6,7},{7,0},{8,9},{9,10},{10,1... | collective-permute-start | bytes 24584 | tf_op jit(solution)/shard_map/ppermute | solution.py:116
  233.5 6.4 %collective-permute-start.1 = (f32[16,128]{0,1:T(8,128)}, f32[16,128]{0,1:T(8,128)S(1)}, u32[]{:S(2)}, u32[]{:S(2)}) collective-permute-start(f32[16,128]{0,1:T(8,128)} %bitcast.46), channel_id=1, source_target_pairs={{0,2},{1,3},{2,4},{3,5},{4,6},{5,7},{6,0},{7,1},{8,10},{9,11},{10,... | collective-permute-start | bytes 24584 | tf_op jit(solution)/shard_map/ppermute | solution.py:116
  235.0 10.0 %collective-permute-start.2 = (f32[16,128]{0,1:T(8,128)}, f32[16,128]{0,1:T(8,128)S(1)}, u32[]{:S(2)}, u32[]{:S(2)}) collective-permute-start(f32[16,128]{0,1:T(8,128)} %bitcast.47), channel_id=1, source_target_pairs={{0,3},{1,4},{2,5},{3,6},{4,7},{5,0},{6,1},{7,2},{8,11},{9,12},{10,... | collective-permute-start | bytes 24584 | tf_op jit(solution)/shard_map/ppermute | solution.py:116
  237.3 7.7 %collective-permute-start.3 = (f32[16,128]{0,1:T(8,128)}, f32[16,128]{0,1:T(8,128)S(1)}, u32[]{:S(2)}, u32[]{:S(2)}) collective-permute-start(f32[16,128]{0,1:T(8,128)} %bitcast.48), channel_id=1, source_target_pairs={{0,4},{1,5},{2,6},{3,7},{4,0},{5,1},{6,2},{7,3},{8,12},{9,13},{10,... | collective-permute-start | bytes 24584 | tf_op jit(solution)/shard_map/ppermute | solution.py:116
  237.8 7.2 %collective-permute-start.4 = (f32[16,128]{0,1:T(8,128)}, f32[16,128]{0,1:T(8,128)S(1)}, u32[]{:S(2)}, u32[]{:S(2)}) collective-permute-start(f32[16,128]{0,1:T(8,128)} %bitcast.49), channel_id=1, source_target_pairs={{0,5},{1,6},{2,7},{3,0},{4,1},{5,2},{6,3},{7,4},{8,13},{9,14},{10,... | collective-permute-start | bytes 24584 | tf_op jit(solution)/shard_map/ppermute | solution.py:116
  238.4 6.6 %collective-permute-start.5 = (f32[16,128]{0,1:T(8,128)}, f32[16,128]{0,1:T(8,128)S(1)}, u32[]{:S(2)}, u32[]{:S(2)}) collective-permute-start(f32[16,128]{0,1:T(8,128)} %bitcast.50), channel_id=1, source_target_pairs={{0,6},{1,7},{2,0},{3,1},{4,2},{5,3},{6,4},{7,5},{8,14},{9,15},{10,... | collective-permute-start | bytes 24584 | tf_op jit(solution)/shard_map/ppermute | solution.py:116
  239.8 5.2 %collective-permute-start.6 = (f32[16,128]{0,1:T(8,128)}, f32[16,128]{0,1:T(8,128)S(1)}, u32[]{:S(2)}, u32[]{:S(2)}) collective-permute-start(f32[16,128]{0,1:T(8,128)} %bitcast.51), channel_id=1, source_target_pairs={{0,7},{1,0},{2,1},{3,2},{4,3},{5,4},{6,5},{7,6},{8,15},{9,8},{10,9... | collective-permute-start | bytes 24584 | tf_op jit(solution)/shard_map/ppermute | solution.py:116
Sparse Core Ops, SparseCore 0:
  18.2 79.4 reduce-scatter.1
  169.4 45.7 all-gather.1

commit v10 on v5

--- a/solution.py
+++ b/solution.py
@@ -28,7 +28,9 @@
     flat_pairs = block_pair[:, 0]
     gen_major_pairs = flat_pairs.reshape(pair_count_axis, gen_count).T.reshape(-1)
     rows_per = quarter // adapter_rank
-    outgoing = jnp.take(adapter_part.reshape(pair_count, rows_per, adapter_rank), gen_major_pairs, axis=0)
+    outgoing = jnp.take(
+        adapter_part.reshape(pair_count, rows_per, adapter_rank), gen_major_pairs, axis=0, mode="clip"
+    )
     incoming = lax.all_to_all(outgoing, ("gen", "pair"), 0, 0, tiled=True)
     adapters = incoming.reshape(blocks_here, model_width, adapter_rank)
     token_blocks = tokens.reshape(blocks_here, BLK, model_width)

time: 252 us -> 252 us (level)
  no operation moved by 1% of the time
where the time goes in v10:
time: 252 us
  waiting for transfers between devices  144 us (57%)
  matrix products  43.2 us (17%)
  blocking collectives  29.3 us (12%)
  between operations  14.2 us (6%)
  local copies, waits for them, and re-layouts  11.4 us (5%)
  starting transfers between devices  8.22 us (3%)
    reduce_scatter x1, waiting for transfers between devices, shards(): lax.psum_scatter(partial_value, 'pair', scatter_dimension=1, tiled=True)  78.1 us
    all_gather x1, waiting for transfers between devices, shards(): grad_rounded = lax.all_gather(row_grad, 'pair', axis=1, tiled=True)  45.9 us
    all_to_all x1, blocking collectives, shards(): returned = lax.all_to_all(by_owner, ('gen', 'pair'), 0, 0, tiled=True)  29.3 us
    all_to_all x1, waiting for transfers between devices, shards(): incoming = lax.all_to_all(outgoing, ('gen', 'pair'), 0, 0, tiled=True)  18.4 us
    dot_general x1, matrix products, shards(): jnp.einsum('pc,ec->pe', grad_rounded, generator, preferred_element_type=j...  10.8 us
    dot_general x1, matrix products, shards(): jnp.dot(pair_embed, generator, preferred_element_type=jnp.float32)  10.1 us
    dot_general x1, matrix products, shards(): jnp.einsum('pe,pc->ec', pair_embed, grad_rounded, preferred_element_type=...  8.53 us
    unnamed x20, local copies, waits for them, and re-layouts  8.12 us
  transfers between devices with their start and end apart: 6, of which 4 were waited for; matrix products, arithmetic and copies ran while one was open for 8% of the time, Pallas kernels for 0%

profile of v10, /device:TPU:0, one launch (start us, length us, event | category | flops | bytes accessed | tf_op | source)
XLA Modules:
  0.0 251.8 jit_solution(16631792855333854261)
XLA Ops:
  7.2 0.0 copy-start
  7.2 0.0 reduce-scatter.2.cloned.1.call-start
  7.2 0.7 copy-done
  8.0 0.9 convolution_convert_fusion.3
  8.8 10.1 %fusion.20 = f32[16,65536]{1,0:T(8,128)} fusion(bf16[16,128]{1,0:T(8,128)(2,1)S(1)} %convolution_convert_fusion.3, bf16[128,65536]{1,0:T(8,128)(2,1)} %param.13), kind=kOutput, calls=%fused_computation.27 | convolution fusion | flops 268435456 | bytes 20975616 | tf_op jit(solution)/shard_map/dot_general | solution.py:24
  18.9 0.0 reduce-scatter.2.cloned.1.call-update
  19.0 0.0 copy-start.4
  19.0 0.5 broadcast.18
  19.5 0.1 copy-done.5
  19.6 0.7 reduce.3
  20.3 0.1 reshape_squeeze.3
  20.3 0.1 copy.17
  20.4 0.1 reshape.59
  20.5 78.1 %reduce-scatter.2.cloned.1.call-done = f32[16,16384]{1,0:T(8,128)} async-done(((f32[16,65536]{1,0:T(8,128)}), f32[16,16384]{1,0:T(8,128)}) %reduce-scatter.2.cloned.1.call-update) | async-done | bytes 1048592 | tf_op jit(solution)/shard_map/reduce_scatter | solution.py:25
  98.6 1.3 convert_element_type.42
  99.9 0.1 copy.27
  100.0 1.6 gather_fusion
  101.6 5.1 %all-to-all-start = ((bf16[32,64,256]{2,1,0:T(8,128)(2,1)}), bf16[32,64,256]{2,1,0:T(8,128)(2,1)S(1)}, u32[]{:S(2)}, u32[]{:S(2)}) async-start(bf16[32,64,256]{2,1,0:T(8,128)(2,1)} %gather_fusion), calls=%async_computation.1 | async-start | bytes 2097152 | tf_op jit(solution)/shard_map/all_to_all | solution.py:34
  106.7 0.0 all-gather.2.cloned.1.call-start
  106.7 0.0 copy-done.4
  106.7 0.2 copy.16
  107.0 6.4 %copy.18 = bf16[1024,2048]{0,1:T(8,128)(2,1)} copy(bf16[1024,2048]{1,0:T(8,128)(2,1)} %param.7) | data formatting | bytes 8388608 | tf_op args[0]
  113.4 18.4 %all-to-all-done = bf16[32,64,256]{2,1,0:T(8,128)(2,1)S(1)} async-done(((bf16[32,64,256]{2,1,0:T(8,128)(2,1)}), bf16[32,64,256]{2,1,0:T(8,128)(2,1)S(1)}, u32[]{:S(2)}, u32[]{:S(2)}) %all-to-all-start) | async-done | bytes 1048608 | tf_op jit(solution)/shard_map/all_to_all | solution.py:34
  131.7 3.9 %multiply_convert_fusion = bf16[1024,256]{0,1:T(8,128)(2,1)S(1)} fusion(bf16[2048,256]{1,0:T(8,128)(2,1)S(1)} %bitcast.35, bf16[1024,2048]{1,0:T(8,128)(2,1)} %param.7, bf16[1024,256]{0,1:T(8,128)(2,1)S(1)} %copy.16), kind=kOutput, calls=%fused_computation.12 | convolution fusion | flops 1076363264 | bytes 6291456 | tf_op jit(solution)/shard_map/btd,bdr->btr/dot_general | solution.py:38
  135.6 0.0 copy-start.3
  135.7 0.0 copy-done.2
  135.7 3.0 %fusion.5 = bf16[32,64,256]{2,0,1:T(8,128)(2,1)S(1)} fusion(bf16[32,64,1024]{2,1,0:T(8,128)(2,1)S(1)} %bitcast.37, bf16[1024,256]{0,1:T(8,128)(2,1)S(1)} %multiply_convert_fusion), kind=kOutput, calls=%fused_computation.6 | convolution fusion | flops 1074266112 | bytes 5767168 | tf_op jit(solution)/shard_map/btd,btr->bdr/dot_general | solution.py:48
  138.6 0.0 copy-done.3
  138.7 0.6 copy.21
  139.2 29.3 %all_to_all.10 = bf16[32,64,256]{2,1,0:T(8,128)(2,1)S(1)} all-to-all(bf16[32,64,256]{2,1,0:T(8,128)(2,1)S(1)} %copy.21), channel_id=1, replica_groups=mesh['pair'=4,'gen'=8] {'gen','pair'}, dimensions={0} | all-to-all | bytes 2097152 | tf_op jit(solution)/shard_map/all_to_all | solution.py:52
  168.6 0.7 fusion.8
  169.2 0.8 copy.26
  170.1 0.0 all-gather.2.cloned.1.call-update
  170.1 45.9 %all-gather.2.cloned.1.call-done = bf16[16,65536]{1,0:T(8,128)(2,1)} async-done(((bf16[16,16384]{1,0:T(8,128)(2,1)}), bf16[16,65536]{1,0:T(8,128)(2,1)}) %all-gather.2.cloned.1.call-update) | async-done | bytes 2097168 | tf_op jit(solution)/shard_map/all_gather | solution.py:60
  216.0 10.8 %fusion.21 = f32[16,128]{1,0:T(8,128)S(1)} fusion(bf16[16,65536]{1,0:T(8,128)(2,1)} %all-gather.2.cloned.1.call-done, bf16[128,65536]{1,0:T(8,128)(2,1)} %param.13), kind=kOutput, calls=%fused_computation.28 | convolution fusion | flops 268435456 | bytes 18882560 | tf_op jit(solution)/shard_map/pc,ec->pe/dot_general | solution.py:64
  226.8 0.0 collective-permute-start
  226.8 1.2 collective-permute-done
  228.0 1.5 collective-permute-start.1
  229.5 4.4 %convolution_convert_fusion.1 = bf16[1024,2048]{1,0:T(8,128)(2,1)} fusion(bf16[1024,256]{0,1:T(8,128)(2,1)} %copy-done.3, bf16[2048,256]{1,0:T(8,128)(2,1)S(1)} %bitcast.36), kind=kOutput, calls=%fused_computation.4 | convolution fusion | flops 1075838976 | bytes 5767168 | tf_op jit(solution)/shard_map/btr,bdr->btd/dot_general | solution.py:44
  233.9 0.0 collective-permute-done.1
  233.9 0.0 copy-start.7
  233.9 1.5 collective-permute-start.2
  235.4 0.0 copy-done.1
  235.5 8.5 %convolution_convert_fusion = bf16[128,65536]{1,0:T(8,128)(2,1)} fusion(bf16[16,128]{1,0:T(8,128)(2,1)S(1)} %convolution_convert_fusion.3, bf16[16,65536]{1,0:T(8,128)(2,1)S(1)} %copy-done.1), kind=kOutput, calls=%fused_computation.1 | convolution fusion | flops 276824064 | bytes 18878464 | tf_op jit(solution)/shard_map/pe,pc->ec/dot_general | solution.py:61
  244.0 0.0 collective-permute-done.2
  244.0 0.0 copy-done.6
  244.0 0.0 copy-done.7
  244.0 1.0 fusion.11
  (7 shorter events, 0.0 us)
Async XLA Ops:
  7.2 0.8 copy-start
  7.2 91.4 %reduce-scatter.2.cloned.1.call-start = ((), (), s32[]{:S(2)}) async-start(), calls=%async_computation.3 | async-start | bytes 5242880 | tf_op jit(solution)/shard_map/reduce_scatter | solution.py:25
  18.9 0.7 copy-start.5
  19.0 87.8 %copy-start.4 = (bf16[1024,256]{1,0:T(8,128)(2,1)S(1)}, bf16[1024,256]{1,0:T(8,128)(2,1)}, u32[]{:S(2)}) copy-start(bf16[1024,256]{1,0:T(8,128)(2,1)} %param.8) | copy-start | bytes 1572868
  101.6 30.2 %all-to-all-start = ((bf16[32,64,256]{2,1,0:T(8,128)(2,1)}), bf16[32,64,256]{2,1,0:T(8,128)(2,1)S(1)}, u32[]{:S(2)}, u32[]{:S(2)}) async-start(bf16[32,64,256]{2,1,0:T(8,128)(2,1)} %gather_fusion), calls=%async_computation.1 | async-start | bytes 2097152 | tf_op jit(solution)/shard_map/all_to_all | solution.py:34
  106.7 109.3 %all-gather.2.cloned.1.call-start = ((), (), s32[]{:S(2)}) async-start(), calls=%async_computation.4 | async-start | bytes 2621440 | tf_op jit(solution)/shard_map/all_gather | solution.py:60
  131.7 3.9 %copy-start.2 = (bf16[1024,2048]{0,1:T(8,128)(2,1)S(1)}, bf16[1024,2048]{0,1:T(8,128)(2,1)}, u32[]{:S(2)}) copy-start(bf16[1024,2048]{0,1:T(8,128)(2,1)} %copy.18) | copy-start | bytes 12582916
  135.6 3.0 %copy-start.3 = (bf16[1024,256]{0,1:T(8,128)(2,1)}, bf16[1024,256]{0,1:T(8,128)(2,1)S(1)}, u32[]{:S(2)}) copy-start(bf16[1024,256]{0,1:T(8,128)(2,1)S(1)} %multiply_convert_fusion) | copy-start | bytes 1572868
  226.8 1.2 collective-permute-start
  228.0 7.4 %copy-start.1 = (bf16[16,65536]{1,0:T(8,128)(2,1)S(1)}, bf16[16,65536]{1,0:T(8,128)(2,1)}, u32[]{:S(2)}) copy-start(bf16[16,65536]{1,0:T(8,128)(2,1)} %all-gather.2.cloned.1.call-done) | copy-start | bytes 6291460
  228.0 5.9 %collective-permute-start.1 = (f32[16,128]{1,0:T(8,128)S(1)}, f32[16,128]{1,0:T(8,128)S(1)}, u32[]{:S(2)}, u32[]{:S(2)}) collective-permute-start(f32[16,128]{1,0:T(8,128)S(1)} %add.25), channel_id=1, source_target_pairs={{0,2},{1,3},{2,0},{3,1},{4,6},{5,7},{6,4},{7,5},{8,10},{9,11},{10,... | collective-permute-start | bytes 24584 | tf_op jit(solution)/shard_map/ppermute | solution.py:71
  233.9 10.1 %copy-start.6 = (s32[16]{0:T(128)S(1)}, s32[16]{0:T(128)}, u32[]{:S(2)}) copy-start(s32[16]{0:T(128)} %param.11) | copy-start | bytes 196
  233.9 10.1 %copy-start.7 = (s32[16]{0:T(128)S(1)}, s32[16]{0:T(128)}, u32[]{:S(2)}) copy-start(s32[16]{0:T(128)} %param.10) | copy-start | bytes 196
  233.9 10.1 %collective-permute-start.2 = (f32[16,128]{1,0:T(8,128)S(1)}, f32[16,128]{1,0:T(8,128)S(1)}, u32[]{:S(2)}, u32[]{:S(2)}) collective-permute-start(f32[16,128]{1,0:T(8,128)S(1)} %add.26), channel_id=1, source_target_pairs={{0,4},{1,5},{2,6},{3,7},{4,0},{5,1},{6,2},{7,3},{8,12},{9,13},{10,... | collective-permute-start | bytes 24584 | tf_op jit(solution)/shard_map/ppermute | solution.py:71
Sparse Core Ops, SparseCore 0:
  19.1 79.4 reduce-scatter.1
  170.2 45.7 all-gather.1

commit v11 on v10

--- a/solution.py
+++ b/solution.py
@@ -57,6 +57,7 @@
         .astype(jnp.bfloat16)
         .reshape(pair_count, quarter)
     )
+    grad_tokens, row_grad = lax.optimization_barrier((grad_tokens, row_grad))
     grad_rounded = lax.all_gather(row_grad, "pair", axis=1, tiled=True)
     grad_generator = jnp.einsum(
         "pe,pc->ec", pair_embed, grad_rounded, preferred_element_type=jnp.float32

time: 252 us -> 251 us (level)
  blocking collectives: 29.3 us -> 0 us
  waiting for transfers between devices: 144 us -> 167 us
  starting transfers between devices: 8.22 us -> 12.9 us
    all_to_all x1 -> x0, blocking collectives: 29.3 us -> none  [shards(): returned = lax.all_to_all(by_owner, ('gen', 'pair'), 0, 0, tiled=True)]
    all_to_all x0 -> x1, waiting for transfers between devices: none -> 21.5 us  [shards(): returned = lax.all_to_all(by_owner, ('gen', 'pair'), 0, 0, tiled=True)]
    all_to_all x0 -> x1, starting transfers between devices: none -> 4.45 us  [shards(): returned = lax.all_to_all(by_owner, ('gen', 'pair'), 0, 0, tiled=True)]
    unnamed x20 -> x18, local copies, waits for them, and re-layouts: 8.12 us -> 8.11 us
  transfers between devices with their start and end apart: 6 -> 7, of which waited for: 4 -> 6; matrix products, arithmetic and copies ran while one was open for 8% -> 8% of each run, Pallas kernels for 0% -> 0%
where the time goes in v11:
time: 251 us
  waiting for transfers between devices  167 us (67%)
  matrix products  42.3 us (17%)
  between operations  14.1 us (6%)
  starting transfers between devices  12.9 us (5%)
  local copies, waits for them, and re-layouts  12.3 us (5%)
    reduce_scatter x1, waiting for transfers between devices, shards(): lax.psum_scatter(partial_value, 'pair', scatter_dimension=1, tiled=True)  78.1 us
    all_gather x1, waiting for transfers between devices, shards(): grad_rounded = lax.all_gather(row_grad, 'pair', axis=1, tiled=True)  45.9 us
    all_to_all x1, waiting for transfers between devices, shards(): returned = lax.all_to_all(by_owner, ('gen', 'pair'), 0, 0, tiled=True)  21.5 us
    all_to_all x1, waiting for transfers between devices, shards(): incoming = lax.all_to_all(outgoing, ('gen', 'pair'), 0, 0, tiled=True)  18.4 us
    dot_general x1, matrix products, shards(): jnp.einsum('pc,ec->pe', grad_rounded, generator, preferred_element_type=j...  11 us
    dot_general x1, matrix products, shards(): jnp.dot(pair_embed, generator, preferred_element_type=jnp.float32)  10.1 us
    dot_general x1, matrix products, shards(): jnp.einsum('pe,pc->ec', pair_embed, grad_rounded, preferred_element_type=...  8.53 us
    unnamed x18, local copies, waits for them, and re-layouts  8.11 us
  transfers between devices with their start and end apart: 7, of which 6 were waited for; matrix products, arithmetic and copies ran while one was open for 8% of the time, Pallas kernels for 0%

profile of v11, /device:TPU:0, one launch (start us, length us, event | category | flops | bytes accessed | tf_op | source)
XLA Modules:
  0.0 250.9 jit_solution(4040114924178040575)
XLA Ops:
  7.2 0.0 copy-start
  7.2 0.0 reduce-scatter.2.cloned.1.call-start
  7.2 0.7 copy-done
  8.0 0.9 convolution_convert_fusion.3
  8.8 10.1 %fusion.20 = f32[16,65536]{1,0:T(8,128)} fusion(bf16[16,128]{1,0:T(8,128)(2,1)S(1)} %convolution_convert_fusion.3, bf16[128,65536]{1,0:T(8,128)(2,1)} %param.13), kind=kOutput, calls=%fused_computation.27 | convolution fusion | flops 268435456 | bytes 20975616 | tf_op jit(solution)/shard_map/dot_general | solution.py:24
  18.9 0.0 copy-start.4
  18.9 0.0 reduce-scatter.2.cloned.1.call-update
  19.0 0.0 copy-start.3
  19.0 0.5 broadcast.18
  19.5 0.1 copy-done.4
  19.6 0.7 reduce.3
  20.3 0.1 reshape_squeeze.3
  20.3 0.1 copy.17
  20.4 0.1 reshape.59
  20.5 78.1 %reduce-scatter.2.cloned.1.call-done = f32[16,16384]{1,0:T(8,128)} async-done(((f32[16,65536]{1,0:T(8,128)}), f32[16,16384]{1,0:T(8,128)}) %reduce-scatter.2.cloned.1.call-update) | async-done | bytes 1048592 | tf_op jit(solution)/shard_map/reduce_scatter | solution.py:25
  98.6 1.3 convert_element_type.42
  99.9 0.1 copy.27
  100.0 1.6 gather_fusion
  101.6 5.1 %all-to-all-start = ((bf16[32,64,256]{2,1,0:T(8,128)(2,1)}), bf16[32,64,256]{2,1,0:T(8,128)(2,1)S(1)}, u32[]{:S(2)}, u32[]{:S(2)}) async-start(bf16[32,64,256]{2,1,0:T(8,128)(2,1)} %gather_fusion), calls=%async_computation.1 | async-start | bytes 2097152 | tf_op jit(solution)/shard_map/all_to_all | solution.py:34
  106.7 0.0 copy-done.3
  106.7 0.2 copy.16
  106.9 6.4 %copy.18 = bf16[1024,2048]{0,1:T(8,128)(2,1)} copy(bf16[1024,2048]{1,0:T(8,128)(2,1)} %param.7) | data formatting | bytes 8388608 | tf_op args[0]
  113.3 18.4 %all-to-all-done = bf16[32,64,256]{2,1,0:T(8,128)(2,1)S(1)} async-done(((bf16[32,64,256]{2,1,0:T(8,128)(2,1)}), bf16[32,64,256]{2,1,0:T(8,128)(2,1)S(1)}, u32[]{:S(2)}, u32[]{:S(2)}) %all-to-all-start) | async-done | bytes 1048608 | tf_op jit(solution)/shard_map/all_to_all | solution.py:34
  131.7 0.0 copy-start.2
  131.7 3.9 %multiply_convert_fusion = bf16[1024,256]{0,1:T(8,128)(2,1)S(1)} fusion(bf16[2048,256]{1,0:T(8,128)(2,1)S(1)} %bitcast.35, bf16[1024,2048]{1,0:T(8,128)(2,1)} %param.7, bf16[1024,256]{0,1:T(8,128)(2,1)S(1)} %copy.16), kind=kOutput, calls=%fused_computation.12 | convolution fusion | flops 1076363264 | bytes 6291456 | tf_op jit(solution)/shard_map/btd,bdr->btr/dot_general | solution.py:38
  135.6 0.0 copy-done.2
  135.7 3.0 %fusion.5 = bf16[32,64,256]{2,0,1:T(8,128)(2,1)S(1)} fusion(bf16[32,64,1024]{2,1,0:T(8,128)(2,1)S(1)} %bitcast.37, bf16[1024,256]{0,1:T(8,128)(2,1)S(1)} %multiply_convert_fusion), kind=kOutput, calls=%fused_computation.6 | convolution fusion | flops 1074266112 | bytes 5767168 | tf_op jit(solution)/shard_map/btd,btr->bdr/dot_general | solution.py:48
  138.6 1.6 copy.21
  140.2 4.5 %all-to-all-start.1 = ((bf16[32,64,256]{2,1,0:T(8,128)(2,1)}), bf16[32,64,256]{2,1,0:T(8,128)(2,1)S(1)}, u32[]{:S(2)}, u32[]{:S(2)}) async-start(bf16[32,64,256]{2,1,0:T(8,128)(2,1)} %copy.21), calls=%async_computation.2 | async-start | bytes 2097152 | tf_op jit(solution)/shard_map/all_to_all | solution.py:52
  144.6 0.2 all-gather.2.cloned.1.call-start
  144.9 3.3 %convolution_convert_fusion.1 = bf16[1024,2048]{1,0:T(8,128)(2,1)} fusion(bf16[1024,256]{0,1:T(8,128)(2,1)S(1)} %multiply_convert_fusion, bf16[2048,256]{1,0:T(8,128)(2,1)S(1)} %bitcast.36), kind=kOutput, calls=%fused_computation.4 | convolution fusion | flops 1075838976 | bytes 5767168 | tf_op jit(solution)/shard_map/btr,bdr->btd/dot_general | solution.py:44
  148.2 21.5 %all-to-all-done.1 = bf16[32,64,256]{2,1,0:T(8,128)(2,1)S(1)} async-done(((bf16[32,64,256]{2,1,0:T(8,128)(2,1)}), bf16[32,64,256]{2,1,0:T(8,128)(2,1)S(1)}, u32[]{:S(2)}, u32[]{:S(2)}) %all-to-all-start.1) | async-done | bytes 1048608 | tf_op jit(solution)/shard_map/all_to_all | solution.py:52
  169.7 0.7 fusion.8
  170.4 0.8 copy.26
  171.2 0.0 all-gather.2.cloned.1.call-update
  171.2 45.9 %all-gather.2.cloned.1.call-done = bf16[16,65536]{1,0:T(8,128)(2,1)} async-done(((bf16[16,16384]{1,0:T(8,128)(2,1)}), bf16[16,65536]{1,0:T(8,128)(2,1)}) %all-gather.2.cloned.1.call-update) | async-done | bytes 2097168 | tf_op jit(solution)/shard_map/all_gather | solution.py:61
  217.2 11.0 %fusion.21 = f32[16,128]{1,0:T(8,128)S(1)} fusion(bf16[16,65536]{1,0:T(8,128)(2,1)} %all-gather.2.cloned.1.call-done, bf16[128,65536]{1,0:T(8,128)(2,1)} %param.13), kind=kOutput, calls=%fused_computation.28 | convolution fusion | flops 268435456 | bytes 18882560 | tf_op jit(solution)/shard_map/pc,ec->pe/dot_general | solution.py:65
  228.1 0.0 collective-permute-start
  228.1 1.2 collective-permute-done
  229.3 1.5 collective-permute-start.1
  230.8 2.2 collective-permute-done.1
  233.0 1.6 collective-permute-start.2
  234.5 0.0 copy-done.1
  234.5 8.5 %convolution_convert_fusion = bf16[128,65536]{1,0:T(8,128)(2,1)} fusion(bf16[16,128]{1,0:T(8,128)(2,1)S(1)} %convolution_convert_fusion.3, bf16[16,65536]{1,0:T(8,128)(2,1)S(1)} %copy-done.1), kind=kOutput, calls=%fused_computation.1 | convolution fusion | flops 276824064 | bytes 18878464 | tf_op jit(solution)/shard_map/pe,pc->ec/dot_general | solution.py:62
  243.1 0.0 collective-permute-done.2
  243.1 0.0 copy-done.5
  243.1 0.0 copy-done.6
  243.1 1.0 fusion.11
  (6 shorter events, 0.0 us)
Async XLA Ops:
  7.2 0.8 copy-start
  7.2 91.4 %reduce-scatter.2.cloned.1.call-start = ((), (), s32[]{:S(2)}) async-start(), calls=%async_computation.3 | async-start | bytes 5242880 | tf_op jit(solution)/shard_map/reduce_scatter | solution.py:25
  18.9 0.7 copy-start.4
  19.0 87.7 %copy-start.3 = (bf16[1024,256]{1,0:T(8,128)(2,1)S(1)}, bf16[1024,256]{1,0:T(8,128)(2,1)}, u32[]{:S(2)}) copy-start(bf16[1024,256]{1,0:T(8,128)(2,1)} %param.8) | copy-start | bytes 1572868
  101.6 30.2 %all-to-all-start = ((bf16[32,64,256]{2,1,0:T(8,128)(2,1)}), bf16[32,64,256]{2,1,0:T(8,128)(2,1)S(1)}, u32[]{:S(2)}, u32[]{:S(2)}) async-start(bf16[32,64,256]{2,1,0:T(8,128)(2,1)} %gather_fusion), calls=%async_computation.1 | async-start | bytes 2097152 | tf_op jit(solution)/shard_map/all_to_all | solution.py:34
  131.7 3.9 %copy-start.2 = (bf16[1024,2048]{0,1:T(8,128)(2,1)S(1)}, bf16[1024,2048]{0,1:T(8,128)(2,1)}, u32[]{:S(2)}) copy-start(bf16[1024,2048]{0,1:T(8,128)(2,1)} %copy.18) | copy-start | bytes 12582916
  140.2 29.5 %all-to-all-start.1 = ((bf16[32,64,256]{2,1,0:T(8,128)(2,1)}), bf16[32,64,256]{2,1,0:T(8,128)(2,1)S(1)}, u32[]{:S(2)}, u32[]{:S(2)}) async-start(bf16[32,64,256]{2,1,0:T(8,128)(2,1)} %copy.21), calls=%async_computation.2 | async-start | bytes 2097152 | tf_op jit(solution)/shard_map/all_to_all | solution.py:52
  144.6 72.5 %all-gather.2.cloned.1.call-start = ((), (), s32[]{:S(2)}) async-start(), calls=%async_computation.4 | async-start | bytes 2621440 | tf_op jit(solution)/shard_map/all_gather | solution.py:61
  217.2 17.4 %copy-start.1 = (bf16[16,65536]{1,0:T(8,128)(2,1)S(1)}, bf16[16,65536]{1,0:T(8,128)(2,1)}, u32[]{:S(2)}) copy-start(bf16[16,65536]{1,0:T(8,128)(2,1)} %all-gather.2.cloned.1.call-done) | copy-start | bytes 6291460
  228.1 1.2 collective-permute-start
  229.3 3.7 %collective-permute-start.1 = (f32[16,128]{1,0:T(8,128)S(1)}, f32[16,128]{1,0:T(8,128)S(1)}, u32[]{:S(2)}, u32[]{:S(2)}) collective-permute-start(f32[16,128]{1,0:T(8,128)S(1)} %add.25), channel_id=1, source_target_pairs={{0,2},{1,3},{2,0},{3,1},{4,6},{5,7},{6,4},{7,5},{8,10},{9,11},{10,... | collective-permute-start | bytes 24584 | tf_op jit(solution)/shard_map/ppermute | solution.py:72
  233.0 10.1 %copy-start.5 = (s32[16]{0:T(128)S(1)}, s32[16]{0:T(128)}, u32[]{:S(2)}) copy-start(s32[16]{0:T(128)} %param.11) | copy-start | bytes 196
  233.0 10.1 %copy-start.6 = (s32[16]{0:T(128)S(1)}, s32[16]{0:T(128)}, u32[]{:S(2)}) copy-start(s32[16]{0:T(128)} %param.10) | copy-start | bytes 196
  233.0 10.1 %collective-permute-start.2 = (f32[16,128]{1,0:T(8,128)S(1)}, f32[16,128]{1,0:T(8,128)S(1)}, u32[]{:S(2)}, u32[]{:S(2)}) collective-permute-start(f32[16,128]{1,0:T(8,128)S(1)} %add.26), channel_id=1, source_target_pairs={{0,4},{1,5},{2,6},{3,7},{4,0},{5,1},{6,2},{7,3},{8,12},{9,13},{10,... | collective-permute-start | bytes 24584 | tf_op jit(solution)/shard_map/ppermute | solution.py:72
Sparse Core Ops, SparseCore 0:
  19.1 79.4 reduce-scatter.1
  171.3 45.7 all-gather.1

commit v12 on v8

--- a/solution.py
+++ b/solution.py
@@ -9,7 +9,8 @@
 TAIL_COLS = 8192
 
 
-def _tail_kernel(embed_t_ref, grad_ref, gen_ref, out_ref, pair_ref):
+def _tail_kernel(own_ref, embed_t_ref, grad_ref, gen_ref, *rest):
+    out_ref, pair_ref = rest[-2], rest[-1]
     step = pl.program_id(0)
     grad_tile = grad_ref[...]
     out_ref[...] = jnp.dot(
@@ -28,33 +29,50 @@
         pair_ref[...] += part
 
 
-def grad_tail(embed_t, grad_rounded, generator):
+def grad_tail(own, embed_t, grads, generator, parts, previous=None):
     feats, cols = generator.shape
-    pairs = grad_rounded.shape[0]
-    tile = min(TAIL_COLS, cols)
+    pairs = grads.shape[0]
+    quarter = cols // parts
+    tile = min(TAIL_COLS, quarter)
+    per_quarter = quarter // tile
+    if previous is None:
+        steps = per_quarter
+        grad_map = lambda i, o: (0, i)
+        col_map = lambda i, o: (0, o[0] * per_quarter + i)
+        extra_specs, extra_args, aliases = [], [], {}
+    else:
+        steps = (parts - 1) * per_quarter
+
+        def col_map(i, o):
+            q = (o[0] + 1 + i // per_quarter) % parts
+            return (0, q * per_quarter + i % per_quarter)
+
+        grad_map = col_map
+        extra_specs = [pl.BlockSpec(memory_space=pl.ANY)]
+        extra_args = [previous]
+        aliases = {4: 0}
     return pl.pallas_call(
         _tail_kernel,
-        grid=(cols // tile,),
-        in_specs=[
-            pl.BlockSpec((feats, pairs), lambda i: (0, 0)),
-            pl.BlockSpec((pairs, tile), lambda i: (0, i)),
-            pl.BlockSpec((feats, tile), lambda i: (0, i)),
-        ],
-        out_specs=[
-            pl.BlockSpec((feats, tile), lambda i: (0, i)),
-            pl.BlockSpec((feats, pairs), lambda i: (0, 0)),
-        ],
+        grid_spec=pltpu.PrefetchScalarGridSpec(
+            num_scalar_prefetch=1,
+            grid=(steps,),
+            in_specs=[
+                pl.BlockSpec((feats, pairs), lambda i, o: (0, 0)),
+                pl.BlockSpec((pairs, tile), grad_map),
+                pl.BlockSpec((feats, tile), col_map),
+            ] + extra_specs,
+            out_specs=[
+                pl.BlockSpec((feats, tile), col_map),
+                pl.BlockSpec((feats, pairs), lambda i, o: (0, 0)),
+            ],
+        ),
         out_shape=[
             jax.ShapeDtypeStruct((feats, cols), jnp.bfloat16),
             jax.ShapeDtypeStruct((feats, pairs), jnp.float32),
         ],
+        input_output_aliases=aliases,
         compiler_params=pltpu.CompilerParams(dimension_semantics=("arbitrary",)),
-        cost_estimate=pl.CostEstimate(
-            flops=4 * feats * cols * pairs,
-            transcendentals=0,
-            bytes_accessed=2 * (2 * feats * cols + pairs * cols),
-        ),
-    )(embed_t, grad_rounded, generator)
+    )(own, embed_t, grads, generator, *extra_args)
 
 
 def shards(tokens, cotangent, block_pair, src_lang, tgt_lang, lang_embed, generator):
@@ -79,7 +97,9 @@
     flat_pairs = block_pair[:, 0]
     gen_major_pairs = flat_pairs.reshape(pair_count_axis, gen_count).T.reshape(-1)
     rows_per = quarter // adapter_rank
-    outgoing = jnp.take(adapter_part.reshape(pair_count, rows_per, adapter_rank), gen_major_pairs, axis=0)
+    outgoing = jnp.take(
+        adapter_part.reshape(pair_count, rows_per, adapter_rank), gen_major_pairs, axis=0, mode="clip"
+    )
     incoming = lax.all_to_all(outgoing, ("gen", "pair"), 0, 0, tiled=True)
     adapters = incoming.reshape(blocks_here, model_width, adapter_rank)
     token_blocks = tokens.reshape(blocks_here, BLK, model_width)
@@ -106,9 +126,13 @@
         .astype(jnp.bfloat16)
         .reshape(pair_count, quarter)
     )
+    grad_tokens, row_grad = lax.optimization_barrier((grad_tokens, row_grad))
     grad_rounded = lax.all_gather(row_grad, "pair", axis=1, tiled=True)
-    grad_generator, pair_part_t = grad_tail(pair_embed.T, grad_rounded, generator)
-    partial_pair = pair_part_t.T
+    own = lax.axis_index("pair").astype(jnp.int32).reshape(1)
+    embed_t = pair_embed.T
+    first, own_part = grad_tail(own, embed_t, row_grad, generator, pair_count_axis)
+    grad_generator, rest_part = grad_tail(own, embed_t, grad_rounded, generator, pair_count_axis, first)
+    partial_pair = (own_part + rest_part).T
     grad_pair = partial_pair
     span = 1
     while span < gen_count:

time: 253 us -> 249 us (0.984)
  blocking collectives: 29.3 us -> 0 us
  waiting for transfers between devices: 147 us -> 165 us
  starting transfers between devices: 8.25 us -> 13 us
    all_to_all x1 -> x0, blocking collectives: 29.3 us -> none  [shards(): returned = lax.all_to_all(by_owner, ('gen', 'pair'), 0, 0, tiled=True)]
    all_to_all x0 -> x1, waiting for transfers between devices: none -> 21.5 us  [shards(): returned = lax.all_to_all(by_owner, ('gen', 'pair'), 0, 0, tiled=True)]
    all_gather x1, waiting for transfers between devices: 45.9 us -> 40.4 us  [shards(): grad_rounded = lax.all_gather(row_grad, 'pair', axis=1, tiled=True)]
    all_to_all x0 -> x1, starting transfers between devices: none -> 4.45 us  [shards(): returned = lax.all_to_all(by_owner, ('gen', 'pair'), 0, 0, tiled=True)]
    ppermute x3, waiting for transfers between devices: 4.26 us -> 6.82 us  [shards(): grad_pair = grad_pair + lax.ppermute(grad_pair, 'gen', swap)]
    pallas_call x1 -> x2, Pallas kernels: 18.1 us -> 19.4 us  [grad_tail(): pl.pallas_call(_tail_kernel, grid_spec=pltpu.PrefetchScalarGridSpec(num_s...]
    unnamed x18 -> x20, local copies, waits for them, and re-layouts: 8.13 us -> 8.11 us
  transfers between devices with their start and end apart: 6 -> 7, of which waited for: 5 -> 7; matrix products, arithmetic and copies ran while one was open for 5% -> 5% of each run, Pallas kernels for 0% -> 2%
where the time goes in v12:
time: 249 us
  waiting for transfers between devices  165 us (66%)
  matrix products  21.9 us (9%)
  Pallas kernels  19.4 us (8%)
  between operations  14.2 us (6%)
  starting transfers between devices  13 us (5%)
  local copies, waits for them, and re-layouts  12.4 us (5%)
  other arithmetic  2.81 us (1%)
    reduce_scatter x1, waiting for transfers between devices, shards(): lax.psum_scatter(partial_value, 'pair', scatter_dimension=1, tiled=True)  78.1 us
    all_gather x1, waiting for transfers between devices, shards(): grad_rounded = lax.all_gather(row_grad, 'pair', axis=1, tiled=True)  40.4 us
    all_to_all x1, waiting for transfers between devices, shards(): returned = lax.all_to_all(by_owner, ('gen', 'pair'), 0, 0, tiled=True)  21.5 us
    pallas_call x2, Pallas kernels, grad_tail(): pl.pallas_call(_tail_kernel, grid_spec=pltpu.PrefetchScalarGridSpec(num_s...  19.4 us
    all_to_all x1, waiting for transfers between devices, shards(): incoming = lax.all_to_all(outgoing, ('gen', 'pair'), 0, 0, tiled=True)  18.4 us
    dot_general x1, matrix products, shards(): jnp.dot(pair_embed, generator, preferred_element_type=jnp.float32)  9.06 us
    unnamed x20, local copies, waits for them, and re-layouts  8.11 us
    ppermute x3, waiting for transfers between devices, shards(): grad_pair = grad_pair + lax.ppermute(grad_pair, 'gen', swap)  6.82 us
  transfers between devices with their start and end apart: 7, of which 7 were waited for; matrix products, arithmetic and copies ran while one was open for 5% of the time, Pallas kernels for 2%

profile of v12, /device:TPU:0, one launch (start us, length us, event | category | flops | bytes accessed | tf_op | source)
XLA Modules:
  0.0 248.8 jit_solution(9671078561556784273)
XLA Ops:
  7.2 0.0 copy-start
  7.2 0.0 reduce-scatter.2.cloned.1.call-start
  7.2 0.7 copy-done
  8.0 1.0 convolution_convert_fusion.2
  9.0 0.0 copy-start.3
  9.0 9.1 %fusion.20 = f32[16,65536]{1,0:T(8,128)} fusion(bf16[16,128]{0,1:T(8,128)(2,1)S(1)} %convolution_convert_fusion.2, bf16[128,65536]{1,0:T(8,128)(2,1)} %gen_ref.3), kind=kOutput, calls=%fused_computation.27 | convolution fusion | flops 268435456 | bytes 20975616 | tf_op jit(solution)/shard_map/dot_general | solution.py:93
  18.0 0.0 copy-done.3
  18.0 0.0 reduce-scatter.2.cloned.1.call-update
  18.1 0.0 copy-start.2
  18.1 0.5 broadcast.18
  18.6 0.1 copy-done.7
  18.7 0.7 reduce.3
  19.3 0.1 reshape_squeeze.3
  19.4 0.1 copy.22
  19.5 0.1 reshape.63
  19.6 78.1 %reduce-scatter.2.cloned.1.call-done = f32[16,16384]{1,0:T(8,128)} async-done(((f32[16,65536]{1,0:T(8,128)}), f32[16,16384]{1,0:T(8,128)}) %reduce-scatter.2.cloned.1.call-update) | async-done | bytes 1048592 | tf_op jit(solution)/shard_map/reduce_scatter | solution.py:94
  97.7 1.3 convert_element_type.43
  98.9 0.1 copy.33
  99.1 1.6 gather_fusion
  100.6 5.1 %all-to-all-start = ((bf16[32,64,256]{2,1,0:T(8,128)(2,1)}), bf16[32,64,256]{2,1,0:T(8,128)(2,1)S(1)}, u32[]{:S(2)}, u32[]{:S(2)}) async-start(bf16[32,64,256]{2,1,0:T(8,128)(2,1)} %gather_fusion), calls=%async_computation.1 | async-start | bytes 2097152 | tf_op jit(solution)/shard_map/all_to_all | solution.py:103
  105.8 0.0 copy-done.2
  105.8 0.2 copy.20
  106.0 6.4 %copy.23 = bf16[1024,2048]{0,1:T(8,128)(2,1)} copy(bf16[1024,2048]{1,0:T(8,128)(2,1)} %param.7) | data formatting | bytes 8388608 | tf_op args[0]
  112.4 18.4 %all-to-all-done = bf16[32,64,256]{2,1,0:T(8,128)(2,1)S(1)} async-done(((bf16[32,64,256]{2,1,0:T(8,128)(2,1)}), bf16[32,64,256]{2,1,0:T(8,128)(2,1)S(1)}, u32[]{:S(2)}, u32[]{:S(2)}) %all-to-all-start) | async-done | bytes 1048608 | tf_op jit(solution)/shard_map/all_to_all | solution.py:103
  130.8 3.9 %multiply_convert_fusion = bf16[1024,256]{0,1:T(8,128)(2,1)S(1)} fusion(bf16[2048,256]{1,0:T(8,128)(2,1)S(1)} %bitcast.37, bf16[1024,2048]{1,0:T(8,128)(2,1)} %param.7, bf16[1024,256]{0,1:T(8,128)(2,1)S(1)} %copy.20), kind=kOutput, calls=%fused_computation.11 | convolution fusion | flops 1076363264 | bytes 6291456 | tf_op jit(solution)/shard_map/btd,bdr->btr/dot_general | solution.py:107
  134.7 0.0 copy-done.1
  134.7 3.0 %fusion.5 = bf16[32,64,256]{2,0,1:T(8,128)(2,1)S(1)} fusion(bf16[32,64,1024]{2,1,0:T(8,128)(2,1)S(1)} %bitcast.39, bf16[1024,256]{0,1:T(8,128)(2,1)S(1)} %multiply_convert_fusion), kind=kOutput, calls=%fused_computation.5 | convolution fusion | flops 1074266112 | bytes 5767168 | tf_op jit(solution)/shard_map/btd,btr->bdr/dot_general | solution.py:117
  137.7 1.6 copy.26
  139.3 4.5 %all-to-all-start.1 = ((bf16[32,64,256]{2,1,0:T(8,128)(2,1)}), bf16[32,64,256]{2,1,0:T(8,128)(2,1)S(1)}, u32[]{:S(2)}, u32[]{:S(2)}) async-start(bf16[32,64,256]{2,1,0:T(8,128)(2,1)} %copy.26), calls=%async_computation.2 | async-start | bytes 2097152 | tf_op jit(solution)/shard_map/all_to_all | solution.py:121
  143.7 0.2 all-gather.2.cloned.1.call-start
  144.0 3.3 %convolution_convert_fusion = bf16[1024,2048]{1,0:T(8,128)(2,1)} fusion(bf16[1024,256]{0,1:T(8,128)(2,1)S(1)} %multiply_convert_fusion, bf16[2048,256]{1,0:T(8,128)(2,1)S(1)} %bitcast.38), kind=kOutput, calls=%fused_computation.3 | convolution fusion | flops 1075838976 | bytes 5767168 | tf_op jit(solution)/shard_map/btr,bdr->btd/dot_general | solution.py:113
  147.3 21.5 %all-to-all-done.1 = bf16[32,64,256]{2,1,0:T(8,128)(2,1)S(1)} async-done(((bf16[32,64,256]{2,1,0:T(8,128)(2,1)}), bf16[32,64,256]{2,1,0:T(8,128)(2,1)S(1)}, u32[]{:S(2)}, u32[]{:S(2)}) %all-to-all-start.1) | async-done | bytes 1048608 | tf_op jit(solution)/shard_map/all_to_all | solution.py:121
  168.8 0.7 fusion.8
  169.5 0.9 copy.32
  170.3 0.0 all-gather.2.cloned.1.call-update
  170.3 5.5 %shard_map.94 = (bf16[128,65536]{1,0:T(8,128)(2,1)}, f32[128,16]{1,0:T(8,128)}) custom-call(s32[1]{0:T(128)} %bitcast.8.own_ref, bf16[128,16]{1,0:T(8,128)(2,1)} %bitcast.41, bf16[16,16384]{1,0:T(8,128)(2,1)} %bitcast.35, bf16[128,65536]{1,0:T(8,128)(2,1)} %gen_ref.3), custom_call_target="tpu_custom_call" | custom-call | tf_op jit(solution)/shard_map/pallas_call | solution.py:54
  175.9 40.4 %all-gather.2.cloned.1.call-done.grad_ref = bf16[16,65536]{1,0:T(8,128)(2,1)} async-done(((bf16[16,16384]{1,0:T(8,128)(2,1)}), bf16[16,65536]{1,0:T(8,128)(2,1)}) %all-gather.2.cloned.1.call-update) | async-done | bytes 2097168 | tf_op jit(solution)/shard_map/all_gather | solution.py:130
  216.3 13.9 %shard_map.95 = (bf16[128,65536]{1,0:T(8,128)(2,1)}, f32[128,16]{1,0:T(8,128)}) custom-call(s32[1]{0:T(128)} %bitcast.8.own_ref, bf16[128,16]{1,0:T(8,128)(2,1)} %bitcast.42, bf16[16,65536]{1,0:T(8,128)(2,1)} %all-gather.2.cloned.1.call-done.grad_ref, bf16[128,65536]{1,0:T(8,128)(2,1)} %gen_ref.3, ...), custom_call_target="tpu_custom_call", output_to_operand_aliasing={{0}: (4, {})} | custom-call | tf_op jit(solution)/shard_map/pallas_call | solution.py:54
  230.1 0.0 copy-done.4
  230.1 0.8 add_bitcast_fusion
  231.0 0.1 collective-permute-start
  231.1 1.2 collective-permute-done
  232.3 1.5 collective-permute-start.1
  233.9 2.8 %collective-permute-done.1 = f32[16,128]{0,1:T(8,128)S(1)} collective-permute-done((f32[16,128]{0,1:T(8,128)S(1)}, f32[16,128]{0,1:T(8,128)S(1)}, u32[]{:S(2)}, u32[]{:S(2)}) %collective-permute-start.1) | collective-permute-done | bytes 8224 | tf_op jit(solution)/shard_map/ppermute | solution.py:140
  236.7 1.6 collective-permute-start.2
  238.2 2.8 %collective-permute-done.2 = f32[16,128]{0,1:T(8,128)S(1)} collective-permute-done((f32[16,128]{0,1:T(8,128)S(1)}, f32[16,128]{0,1:T(8,128)S(1)}, u32[]{:S(2)}, u32[]{:S(2)}) %collective-permute-start.2) | collective-permute-done | bytes 8224 | tf_op jit(solution)/shard_map/ppermute | solution.py:140
  241.0 0.0 copy-done.5
  241.0 1.0 fusion.11
  (9 shorter events, 0.0 us)
Async XLA Ops:
  7.2 0.8 copy-start
  7.2 90.5 %reduce-scatter.2.cloned.1.call-start = ((), (), s32[]{:S(2)}) async-start(), calls=%async_computation.3 | async-start | bytes 5242880 | tf_op jit(solution)/shard_map/reduce_scatter | solution.py:94
  9.0 9.1 %copy-start.3 = (bf16[16,128]{0,1:T(8,128)(2,1)}, bf16[16,128]{0,1:T(8,128)(2,1)S(1)}, u32[]{:S(2)}) copy-start(bf16[16,128]{0,1:T(8,128)(2,1)S(1)} %convolution_convert_fusion.2) | copy-start | bytes 12292
  18.0 0.7 copy-start.7
  18.1 87.7 %copy-start.2 = (bf16[1024,256]{1,0:T(8,128)(2,1)S(1)}, bf16[1024,256]{1,0:T(8,128)(2,1)}, u32[]{:S(2)}) copy-start(bf16[1024,256]{1,0:T(8,128)(2,1)} %param.8) | copy-start | bytes 1572868
  100.6 30.2 %all-to-all-start = ((bf16[32,64,256]{2,1,0:T(8,128)(2,1)}), bf16[32,64,256]{2,1,0:T(8,128)(2,1)S(1)}, u32[]{:S(2)}, u32[]{:S(2)}) async-start(bf16[32,64,256]{2,1,0:T(8,128)(2,1)} %gather_fusion), calls=%async_computation.1 | async-start | bytes 2097152 | tf_op jit(solution)/shard_map/all_to_all | solution.py:103
  130.8 3.9 %copy-start.1 = (bf16[1024,2048]{0,1:T(8,128)(2,1)S(1)}, bf16[1024,2048]{0,1:T(8,128)(2,1)}, u32[]{:S(2)}) copy-start(bf16[1024,2048]{0,1:T(8,128)(2,1)} %copy.23) | copy-start | bytes 12582916
  139.3 29.5 %all-to-all-start.1 = ((bf16[32,64,256]{2,1,0:T(8,128)(2,1)}), bf16[32,64,256]{2,1,0:T(8,128)(2,1)S(1)}, u32[]{:S(2)}, u32[]{:S(2)}) async-start(bf16[32,64,256]{2,1,0:T(8,128)(2,1)} %copy.26), calls=%async_computation.2 | async-start | bytes 2097152 | tf_op jit(solution)/shard_map/all_to_all | solution.py:121
  143.7 72.5 %all-gather.2.cloned.1.call-start = ((), (), s32[]{:S(2)}) async-start(), calls=%async_computation.4 | async-start | bytes 2621440 | tf_op jit(solution)/shard_map/all_gather | solution.py:130
  216.3 13.9 %copy-start.4 = (f32[128,16]{1,0:T(8,128)S(1)}, f32[128,16]{1,0:T(8,128)}, u32[]{:S(2)}) copy-start(f32[128,16]{1,0:T(8,128)} %get-tuple-element.13) | copy-start | bytes 24580
  216.3 24.7 %copy-start.5 = (s32[16]{0:T(128)S(1)}, s32[16]{0:T(128)}, u32[]{:S(2)}) copy-start(s32[16]{0:T(128)} %param.11) | copy-start | bytes 196
  216.3 24.7 %copy-start.6 = (s32[16]{0:T(128)S(1)}, s32[16]{0:T(128)}, u32[]{:S(2)}) copy-start(s32[16]{0:T(128)} %param.10) | copy-start | bytes 196
  231.0 1.3 collective-permute-start
  232.3 4.3 %collective-permute-start.1 = (f32[16,128]{0,1:T(8,128)S(1)}, f32[16,128]{0,1:T(8,128)S(1)}, u32[]{:S(2)}, u32[]{:S(2)}) collective-permute-start(f32[16,128]{0,1:T(8,128)S(1)} %add.29), channel_id=1, source_target_pairs={{0,2},{1,3},{2,0},{3,1},{4,6},{5,7},{6,4},{7,5},{8,10},{9,11},{10,... | collective-permute-start | bytes 24584 | tf_op jit(solution)/shard_map/ppermute | solution.py:140
  236.7 4.3 %collective-permute-start.2 = (f32[16,128]{0,1:T(8,128)S(1)}, f32[16,128]{0,1:T(8,128)S(1)}, u32[]{:S(2)}, u32[]{:S(2)}) collective-permute-start(f32[16,128]{0,1:T(8,128)S(1)} %add.30), channel_id=1, source_target_pairs={{0,4},{1,5},{2,6},{3,7},{4,0},{5,1},{6,2},{7,3},{8,12},{9,13},{10,... | collective-permute-start | bytes 24584 | tf_op jit(solution)/shard_map/ppermute | solution.py:140
Sparse Core Ops, SparseCore 0:
  18.2 79.4 reduce-scatter.1
  170.5 45.7 all-gather.1

commit v13 on v11

--- a/solution.py
+++ b/solution.py
@@ -2,8 +2,92 @@
 import jax.numpy as jnp
 from jax import lax
 from jax.sharding import PartitionSpec as P
+from jax.experimental import pallas as pl
+from jax.experimental.pallas import tpu as pltpu
 
 BLK = 1024
+TAIL_COLS = 8192
+
+
+def _make_tail_kernel(do_gen, do_pair, aliased):
+    def kernel(own_ref, *refs):
+        refs = list(refs)
+        embed_t_ref = refs.pop(0) if do_gen else None
+        grad_ref = refs.pop(0)
+        gen_ref = refs.pop(0) if do_pair else None
+        if aliased:
+            refs.pop(0)
+        out_ref = refs.pop(0) if do_gen else None
+        pair_ref = refs.pop(0) if do_pair else None
+        grad_tile = grad_ref[...]
+        if do_gen:
+            out_ref[...] = jnp.dot(
+                embed_t_ref[...], grad_tile, preferred_element_type=jnp.float32
+            ).astype(out_ref.dtype)
+        if do_pair:
+            step = pl.program_id(0)
+            part = lax.dot_general(
+                gen_ref[...], grad_tile, (((1,), (1,)), ((), ())), preferred_element_type=jnp.float32
+            )
+
+            @pl.when(step == 0)
+            def _():
+                pair_ref[...] = part
+
+            @pl.when(step > 0)
+            def _():
+                pair_ref[...] += part
+
+    return kernel
+
+
+def grad_tail(own, embed_t, grads, generator, parts, previous=None, do_gen=True, do_pair=True):
+    feats, cols = generator.shape
+    pairs = grads.shape[0]
+    quarter = cols // parts
+    tile = min(TAIL_COLS, quarter)
+    per_quarter = quarter // tile
+    if previous is None:
+        steps = per_quarter
+        grad_map = lambda i, o: (0, i)
+        col_map = lambda i, o: (0, o[0] * per_quarter + i)
+    else:
+        steps = (parts - 1) * per_quarter
+
+        def col_map(i, o):
+            q = (o[0] + 1 + i // per_quarter) % parts
+            return (0, q * per_quarter + i % per_quarter)
+
+        grad_map = col_map
+    in_specs, args, out_specs, out_shape = [], [], [], []
+    if do_gen:
+        in_specs.append(pl.BlockSpec((feats, pairs), lambda i, o: (0, 0)))
+        args.append(embed_t)
+    in_specs.append(pl.BlockSpec((pairs, tile), grad_map))
+    args.append(grads)
+    if do_pair:
+        in_specs.append(pl.BlockSpec((feats, tile), col_map))
+        args.append(generator)
+    aliases = {}
+    if previous is not None and do_gen:
+        aliases = {len(args) + 1: 0}
+        in_specs.append(pl.BlockSpec(memory_space=pl.ANY))
+        args.append(previous)
+    if do_gen:
+        out_specs.append(pl.BlockSpec((feats, tile), col_map))
+        out_shape.append(jax.ShapeDtypeStruct((feats, cols), jnp.bfloat16))
+    if do_pair:
+        out_specs.append(pl.BlockSpec((feats, pairs), lambda i, o: (0, 0)))
+        out_shape.append(jax.ShapeDtypeStruct((feats, pairs), jnp.float32))
+    return pl.pallas_call(
+        _make_tail_kernel(do_gen, do_pair, bool(aliases)),
+        grid_spec=pltpu.PrefetchScalarGridSpec(
+            num_scalar_prefetch=1, grid=(steps,), in_specs=in_specs, out_specs=out_specs,
+        ),
+        out_shape=out_shape,
+        input_output_aliases=aliases,
+        compiler_params=pltpu.CompilerParams(dimension_semantics=("arbitrary",)),
+    )(own, *args)
 
 
 def shards(tokens, cotangent, block_pair, src_lang, tgt_lang, lang_embed, generator):
@@ -59,18 +143,22 @@
     )
     grad_tokens, row_grad = lax.optimization_barrier((grad_tokens, row_grad))
     grad_rounded = lax.all_gather(row_grad, "pair", axis=1, tiled=True)
-    grad_generator = jnp.einsum(
-        "pe,pc->ec", pair_embed, grad_rounded, preferred_element_type=jnp.float32
-    ).astype(jnp.bfloat16)
-    partial_pair = jnp.einsum(
-        "pc,ec->pe", grad_rounded, generator, preferred_element_type=jnp.float32
+    own = lax.axis_index("pair").astype(jnp.int32).reshape(1)
+    embed_t = pair_embed.T
+    first, own_part = grad_tail(own, embed_t, row_grad, generator, pair_count_axis)
+    (rest_part,) = grad_tail(
+        own, embed_t, grad_rounded, generator, pair_count_axis, first, do_gen=False
     )
+    partial_pair = (own_part + rest_part).T
     grad_pair = partial_pair
     span = 1
     while span < gen_count:
         swap = [(i, i ^ span) for i in range(gen_count)]
         grad_pair = grad_pair + lax.ppermute(grad_pair, "gen", swap)
         span *= 2
+    (grad_generator,) = grad_tail(
+        own, embed_t, grad_rounded, generator, pair_count_axis, first, do_pair=False
+    )
     grad_embed = jnp.dot(hot_both.T, grad_pair, precision=lax.Precision.HIGHEST)
     return (grad_tokens, grad_generator, grad_embed)
 

time: 251 us -> 250 us (level)
  Pallas kernels: 0 us -> 22.5 us
  matrix products: 42.3 us -> 21.9 us
  waiting for transfers between devices: 167 us -> 162 us
    pallas_call x0 -> x3, Pallas kernels: none -> 22.5 us  [grad_tail(): pl.pallas_call(_make_tail_kernel(do_gen, do_pair, bool(aliases)), grid_sp...]
    dot_general x2 -> x0, matrix products: 19.5 us -> none  [the longest x1 11 us: shards(): jnp.einsum('pc,ec->pe', grad_rounded, generator, preferred_element_type=j...]
    all_gather x1, waiting for transfers between devices: 45.9 us -> 40.4 us  [shards(): grad_rounded = lax.all_gather(row_grad, 'pair', axis=1, tiled=True)]
    unnamed x18 -> x20, local copies, waits for them, and re-layouts: 8.11 us -> 8.11 us
  transfers between devices with their start and end apart: 7 -> 7, of which waited for: 6 -> 6; matrix products, arithmetic and copies ran while one was open for 8% -> 5% of each run, Pallas kernels for 0% -> 5%
where the time goes in v13:
time: 250 us; the launch traced here: 249 us
  waiting for transfers between devices  162 us (65%)
  Pallas kernels  22.5 us (9%)
  matrix products  21.9 us (9%)
  between operations  14.2 us (6%)
  starting transfers between devices  13 us (5%)
  local copies, waits for them, and re-layouts  12.4 us (5%)
  other arithmetic  2.81 us (1%)
    reduce_scatter x1, waiting for transfers between devices, shards(): lax.psum_scatter(partial_value, 'pair', scatter_dimension=1, tiled=True)  78.1 us
    all_gather x1, waiting for transfers between devices, shards(): grad_rounded = lax.all_gather(row_grad, 'pair', axis=1, tiled=True)  40.4 us
    pallas_call x3, Pallas kernels, grad_tail(): pl.pallas_call(_make_tail_kernel(do_gen, do_pair, bool(aliases)), grid_sp...  22.5 us
    all_to_all x1, waiting for transfers between devices, shards(): returned = lax.all_to_all(by_owner, ('gen', 'pair'), 0, 0, tiled=True)  21.5 us
    all_to_all x1, waiting for transfers between devices, shards(): incoming = lax.all_to_all(outgoing, ('gen', 'pair'), 0, 0, tiled=True)  18.4 us
    dot_general x1, matrix products, shards(): jnp.dot(pair_embed, generator, preferred_element_type=jnp.float32)  9.06 us
    unnamed x20, local copies, waits for them, and re-layouts  8.11 us
    all_to_all x1, starting transfers between devices, shards(): incoming = lax.all_to_all(outgoing, ('gen', 'pair'), 0, 0, tiled=True)  5.11 us
  transfers between devices with their start and end apart: 7, of which 6 were waited for; matrix products, arithmetic and copies ran while one was open for 5% of the time, Pallas kernels for 5%

profile of v13, /device:TPU:0, one launch (start us, length us, event | category | flops | bytes accessed | tf_op | source)
XLA Modules:
  0.0 249.1 jit_solution(5711521656575844673)
XLA Ops:
  7.2 0.0 copy-start
  7.2 0.0 reduce-scatter.2.cloned.1.call-start
  7.2 0.7 copy-done
  8.0 1.0 convolution_convert_fusion.2
  9.0 0.0 copy-start.3
  9.0 9.1 %fusion.20 = f32[16,65536]{1,0:T(8,128)} fusion(bf16[16,128]{0,1:T(8,128)(2,1)S(1)} %convolution_convert_fusion.2, bf16[128,65536]{1,0:T(8,128)(2,1)} %refs_1_.1), kind=kOutput, calls=%fused_computation.27 | convolution fusion | flops 268435456 | bytes 20975616 | tf_op jit(solution)/shard_map/dot_general | solution.py:108
  18.0 0.0 copy-done.3
  18.0 0.0 reduce-scatter.2.cloned.1.call-update
  18.1 0.0 copy-start.2
  18.1 0.5 broadcast.18
  18.6 0.1 copy-done.7
  18.7 0.7 reduce.3
  19.3 0.1 reshape_squeeze.3
  19.4 0.1 copy.22
  19.5 0.1 reshape.63
  19.6 78.1 %reduce-scatter.2.cloned.1.call-done = f32[16,16384]{1,0:T(8,128)} async-done(((f32[16,65536]{1,0:T(8,128)}), f32[16,16384]{1,0:T(8,128)}) %reduce-scatter.2.cloned.1.call-update) | async-done | bytes 1048592 | tf_op jit(solution)/shard_map/reduce_scatter | solution.py:109
  97.7 1.3 convert_element_type.43
  98.9 0.1 copy.33
  99.1 1.6 gather_fusion
  100.6 5.1 %all-to-all-start = ((bf16[32,64,256]{2,1,0:T(8,128)(2,1)}), bf16[32,64,256]{2,1,0:T(8,128)(2,1)S(1)}, u32[]{:S(2)}, u32[]{:S(2)}) async-start(bf16[32,64,256]{2,1,0:T(8,128)(2,1)} %gather_fusion), calls=%async_computation.1 | async-start | bytes 2097152 | tf_op jit(solution)/shard_map/all_to_all | solution.py:118
  105.8 0.0 copy-done.2
  105.8 0.2 copy.20
  106.0 6.4 %copy.23 = bf16[1024,2048]{0,1:T(8,128)(2,1)} copy(bf16[1024,2048]{1,0:T(8,128)(2,1)} %param.7) | data formatting | bytes 8388608 | tf_op args[0]
  112.4 18.4 %all-to-all-done = bf16[32,64,256]{2,1,0:T(8,128)(2,1)S(1)} async-done(((bf16[32,64,256]{2,1,0:T(8,128)(2,1)}), bf16[32,64,256]{2,1,0:T(8,128)(2,1)S(1)}, u32[]{:S(2)}, u32[]{:S(2)}) %all-to-all-start) | async-done | bytes 1048608 | tf_op jit(solution)/shard_map/all_to_all | solution.py:118
  130.8 3.9 %multiply_convert_fusion = bf16[1024,256]{0,1:T(8,128)(2,1)S(1)} fusion(bf16[2048,256]{1,0:T(8,128)(2,1)S(1)} %bitcast.37, bf16[1024,2048]{1,0:T(8,128)(2,1)} %param.7, bf16[1024,256]{0,1:T(8,128)(2,1)S(1)} %copy.20), kind=kOutput, calls=%fused_computation.11 | convolution fusion | flops 1076363264 | bytes 6291456 | tf_op jit(solution)/shard_map/btd,bdr->btr/dot_general | solution.py:122
  134.7 0.0 copy-done.1
  134.7 3.0 %fusion.5 = bf16[32,64,256]{2,0,1:T(8,128)(2,1)S(1)} fusion(bf16[32,64,1024]{2,1,0:T(8,128)(2,1)S(1)} %bitcast.39, bf16[1024,256]{0,1:T(8,128)(2,1)S(1)} %multiply_convert_fusion), kind=kOutput, calls=%fused_computation.5 | convolution fusion | flops 1074266112 | bytes 5767168 | tf_op jit(solution)/shard_map/btd,btr->bdr/dot_general | solution.py:132
  137.7 1.6 copy.26
  139.3 4.5 %all-to-all-start.1 = ((bf16[32,64,256]{2,1,0:T(8,128)(2,1)}), bf16[32,64,256]{2,1,0:T(8,128)(2,1)S(1)}, u32[]{:S(2)}, u32[]{:S(2)}) async-start(bf16[32,64,256]{2,1,0:T(8,128)(2,1)} %copy.26), calls=%async_computation.2 | async-start | bytes 2097152 | tf_op jit(solution)/shard_map/all_to_all | solution.py:136
  143.7 0.2 all-gather.2.cloned.1.call-start
  144.0 3.3 %convolution_convert_fusion = bf16[1024,2048]{1,0:T(8,128)(2,1)} fusion(bf16[1024,256]{0,1:T(8,128)(2,1)S(1)} %multiply_convert_fusion, bf16[2048,256]{1,0:T(8,128)(2,1)S(1)} %bitcast.38), kind=kOutput, calls=%fused_computation.3 | convolution fusion | flops 1075838976 | bytes 5767168 | tf_op jit(solution)/shard_map/btr,bdr->btd/dot_general | solution.py:128
  147.3 21.5 %all-to-all-done.1 = bf16[32,64,256]{2,1,0:T(8,128)(2,1)S(1)} async-done(((bf16[32,64,256]{2,1,0:T(8,128)(2,1)}), bf16[32,64,256]{2,1,0:T(8,128)(2,1)S(1)}, u32[]{:S(2)}, u32[]{:S(2)}) %all-to-all-start.1) | async-done | bytes 1048608 | tf_op jit(solution)/shard_map/all_to_all | solution.py:136
  168.8 0.7 fusion.8
  169.5 0.9 copy.32
  170.3 0.0 all-gather.2.cloned.1.call-update
  170.3 5.5 %shard_map.94 = (bf16[128,65536]{1,0:T(8,128)(2,1)}, f32[128,16]{1,0:T(8,128)}) custom-call(s32[1]{0:T(128)} %bitcast.8.own_ref, bf16[128,16]{1,0:T(8,128)(2,1)} %bitcast.41, bf16[16,16384]{1,0:T(8,128)(2,1)} %bitcast.35, bf16[128,65536]{1,0:T(8,128)(2,1)} %refs_1_.1), custom_call_target="tpu_custom_call" | custom-call | tf_op jit(solution)/shard_map/pallas_call | solution.py:82
  175.9 40.4 %all-gather.2.cloned.1.call-done.refs_1_.refs_0_ = bf16[16,65536]{1,0:T(8,128)(2,1)} async-done(((bf16[16,16384]{1,0:T(8,128)(2,1)}), bf16[16,65536]{1,0:T(8,128)(2,1)}) %all-gather.2.cloned.1.call-update) | async-done | bytes 2097168 | tf_op jit(solution)/shard_map/all_gather | solution.py:145
  216.3 8.8 %shard_map.96 = f32[128,16]{1,0:T(8,128)} custom-call(s32[1]{0:T(128)} %bitcast.8.own_ref, bf16[16,65536]{1,0:T(8,128)(2,1)} %all-gather.2.cloned.1.call-done.refs_1_.refs_0_, bf16[128,65536]{1,0:T(8,128)(2,1)} %refs_1_.1), custom_call_target="tpu_custom_call" | custom-call | tf_op jit(solution)/shard_map/pallas_call | solution.py:82
  225.1 0.0 copy-done.4
  225.1 0.8 add_bitcast_fusion
  225.9 0.1 collective-permute-start
  226.0 1.2 collective-permute-done
  227.3 1.6 collective-permute-start.1
  228.8 2.8 %collective-permute-done.1 = f32[16,128]{0,1:T(8,128)S(1)} collective-permute-done((f32[16,128]{0,1:T(8,128)S(1)}, f32[16,128]{0,1:T(8,128)S(1)}, u32[]{:S(2)}, u32[]{:S(2)}) %collective-permute-start.1) | collective-permute-done | bytes 8224 | tf_op jit(solution)/shard_map/ppermute | solution.py:157
  231.6 1.6 collective-permute-start.2
  233.2 8.1 %shard_map.95 = bf16[128,65536]{1,0:T(8,128)(2,1)} custom-call(s32[1]{0:T(128)} %bitcast.8.own_ref, bf16[128,16]{1,0:T(8,128)(2,1)} %bitcast.42, bf16[16,65536]{1,0:T(8,128)(2,1)} %all-gather.2.cloned.1.call-done.refs_1_.refs_0_, bf16[128,65536]{1,0:T(8,128)(2,1)} %get-tuple-element.9.refs_2_), custom_call_target="tpu_custom_call", output_to_operand_aliasing={{}: (3, {})} | custom-call | tf_op jit(solution)/shard_map/pallas_call | solution.py:82
  241.3 0.0 collective-permute-done.2
  241.3 1.0 fusion.11
  (10 shorter events, 0.0 us)
Async XLA Ops:
  7.2 0.8 copy-start
  7.2 90.5 %reduce-scatter.2.cloned.1.call-start = ((), (), s32[]{:S(2)}) async-start(), calls=%async_computation.3 | async-start | bytes 5242880 | tf_op jit(solution)/shard_map/reduce_scatter | solution.py:109
  9.0 9.1 %copy-start.3 = (bf16[16,128]{0,1:T(8,128)(2,1)}, bf16[16,128]{0,1:T(8,128)(2,1)S(1)}, u32[]{:S(2)}) copy-start(bf16[16,128]{0,1:T(8,128)(2,1)S(1)} %convolution_convert_fusion.2) | copy-start | bytes 12292
  18.0 0.7 copy-start.7
  18.1 87.7 %copy-start.2 = (bf16[1024,256]{1,0:T(8,128)(2,1)S(1)}, bf16[1024,256]{1,0:T(8,128)(2,1)}, u32[]{:S(2)}) copy-start(bf16[1024,256]{1,0:T(8,128)(2,1)} %param.8) | copy-start | bytes 1572868
  100.6 30.2 %all-to-all-start = ((bf16[32,64,256]{2,1,0:T(8,128)(2,1)}), bf16[32,64,256]{2,1,0:T(8,128)(2,1)S(1)}, u32[]{:S(2)}, u32[]{:S(2)}) async-start(bf16[32,64,256]{2,1,0:T(8,128)(2,1)} %gather_fusion), calls=%async_computation.1 | async-start | bytes 2097152 | tf_op jit(solution)/shard_map/all_to_all | solution.py:118
  130.8 3.9 %copy-start.1 = (bf16[1024,2048]{0,1:T(8,128)(2,1)S(1)}, bf16[1024,2048]{0,1:T(8,128)(2,1)}, u32[]{:S(2)}) copy-start(bf16[1024,2048]{0,1:T(8,128)(2,1)} %copy.23) | copy-start | bytes 12582916
  139.3 29.5 %all-to-all-start.1 = ((bf16[32,64,256]{2,1,0:T(8,128)(2,1)}), bf16[32,64,256]{2,1,0:T(8,128)(2,1)S(1)}, u32[]{:S(2)}, u32[]{:S(2)}) async-start(bf16[32,64,256]{2,1,0:T(8,128)(2,1)} %copy.26), calls=%async_computation.2 | async-start | bytes 2097152 | tf_op jit(solution)/shard_map/all_to_all | solution.py:136
  143.7 72.5 %all-gather.2.cloned.1.call-start = ((), (), s32[]{:S(2)}) async-start(), calls=%async_computation.4 | async-start | bytes 2621440 | tf_op jit(solution)/shard_map/all_gather | solution.py:145
  175.9 49.2 %copy-start.4 = (f32[128,16]{1,0:T(8,128)S(1)}, f32[128,16]{1,0:T(8,128)}, u32[]{:S(2)}) copy-start(f32[128,16]{1,0:T(8,128)} %get-tuple-element.10) | copy-start | bytes 24580
  225.9 1.3 collective-permute-start
  227.3 4.3 %collective-permute-start.1 = (f32[16,128]{0,1:T(8,128)S(1)}, f32[16,128]{0,1:T(8,128)S(1)}, u32[]{:S(2)}, u32[]{:S(2)}) collective-permute-start(f32[16,128]{0,1:T(8,128)S(1)} %add.29), channel_id=1, source_target_pairs={{0,2},{1,3},{2,0},{3,1},{4,6},{5,7},{6,4},{7,5},{8,10},{9,11},{10,... | collective-permute-start | bytes 24584 | tf_op jit(solution)/shard_map/ppermute | solution.py:157
  231.6 9.7 %collective-permute-start.2 = (f32[16,128]{0,1:T(8,128)S(1)}, f32[16,128]{0,1:T(8,128)S(1)}, u32[]{:S(2)}, u32[]{:S(2)}) collective-permute-start(f32[16,128]{0,1:T(8,128)S(1)} %add.30), channel_id=1, source_target_pairs={{0,4},{1,5},{2,6},{3,7},{4,0},{5,1},{6,2},{7,3},{8,12},{9,13},{10,... | collective-permute-start | bytes 24584 | tf_op jit(solution)/shard_map/ppermute | solution.py:157
  233.2 8.1 %copy-start.5 = (s32[16]{0:T(128)S(1)}, s32[16]{0:T(128)}, u32[]{:S(2)}) copy-start(s32[16]{0:T(128)} %param.11) | copy-start | bytes 196
  233.2 8.1 %copy-start.6 = (s32[16]{0:T(128)S(1)}, s32[16]{0:T(128)}, u32[]{:S(2)}) copy-start(s32[16]{0:T(128)} %param.10) | copy-start | bytes 196
Sparse Core Ops, SparseCore 0:
  18.2 79.4 reduce-scatter.1
  170.5 45.7 all-gather.1

commit v14 on v12

--- a/solution.py
+++ b/solution.py
@@ -122,9 +122,10 @@
     pair_ids = jnp.arange(pair_count, dtype=jnp.int32)
     segment_hot = (pair_ids[:, None] == gen_major_pairs[None, :]).astype(jnp.float32)
     row_grad = (
-        jnp.einsum("pb,bxr->pxr", segment_hot, returned.astype(jnp.float32), precision=lax.Precision.HIGHEST)
-        .astype(jnp.bfloat16)
-        .reshape(pair_count, quarter)
+        jnp.dot(
+            segment_hot.astype(jnp.bfloat16), returned.reshape(pair_count_axis * gen_count, quarter),
+            preferred_element_type=jnp.float32,
+        ).astype(jnp.bfloat16)
     )
     grad_tokens, row_grad = lax.optimization_barrier((grad_tokens, row_grad))
     grad_rounded = lax.all_gather(row_grad, "pair", axis=1, tiled=True)

time: 249 us -> 247 us (level)
    unnamed x20 -> x21, local copies, waits for them, and re-layouts: 8.11 us -> 8.7 us
where the time goes in v14:
time: 247 us
  waiting for transfers between devices  165 us (67%)
  matrix products  21.6 us (9%)
  Pallas kernels  19.4 us (8%)
  between operations  14.2 us (6%)
  starting transfers between devices  12.9 us (5%)
  local copies, waits for them, and re-layouts  10.5 us (4%)
  other arithmetic  2.81 us (1%)
    reduce_scatter x1, waiting for transfers between devices, shards(): lax.psum_scatter(partial_value, 'pair', scatter_dimension=1, tiled=True)  78.1 us
    all_gather x1, waiting for transfers between devices, shards(): grad_rounded = lax.all_gather(row_grad, 'pair', axis=1, tiled=True)  40.4 us
    all_to_all x1, waiting for transfers between devices, shards(): returned = lax.all_to_all(by_owner, ('gen', 'pair'), 0, 0, tiled=True)  21.7 us
    pallas_call x2, Pallas kernels, grad_tail(): pl.pallas_call(_tail_kernel, grid_spec=pltpu.PrefetchScalarGridSpec(num_s...  19.4 us
    all_to_all x1, waiting for transfers between devices, shards(): incoming = lax.all_to_all(outgoing, ('gen', 'pair'), 0, 0, tiled=True)  18.4 us
    dot_general x1, matrix products, shards(): jnp.dot(pair_embed, generator, preferred_element_type=jnp.float32)  9.06 us
    unnamed x21, local copies, waits for them, and re-layouts  8.7 us
    ppermute x3, waiting for transfers between devices, shards(): grad_pair = grad_pair + lax.ppermute(grad_pair, 'gen', swap)  6.75 us
  transfers between devices with their start and end apart: 7, of which 7 were waited for; matrix products, arithmetic and copies ran while one was open for 5% of the time, Pallas kernels for 2%

profile of v14, /device:TPU:0, one launch (start us, length us, event | category | flops | bytes accessed | tf_op | source)
XLA Modules:
  0.0 246.7 jit_solution(14492290014259374714)
XLA Ops:
  7.2 0.0 copy-start
  7.2 0.0 reduce-scatter.2.cloned.1.call-start
  7.2 0.7 copy-done
  8.0 1.0 convolution_convert_fusion.3
  9.0 0.0 copy-start.3
  9.0 9.1 %fusion.9 = f32[16,65536]{1,0:T(8,128)} fusion(bf16[16,128]{0,1:T(8,128)(2,1)S(1)} %convolution_convert_fusion.3, bf16[128,65536]{1,0:T(8,128)(2,1)} %gen_ref.3), kind=kOutput, calls=%fused_computation.23 | convolution fusion | flops 268435456 | bytes 20975616 | tf_op jit(solution)/shard_map/dot_general | solution.py:93
  18.0 0.0 copy-done.3
  18.0 0.0 reduce-scatter.2.cloned.1.call-update
  18.1 0.0 copy-start.2
  18.1 0.5 broadcast.18
  18.6 0.1 copy-done.7
  18.7 0.7 reduce.3
  19.3 0.1 reshape_squeeze.3
  19.4 0.1 copy.18
  19.5 0.1 reshape.63
  19.6 78.1 %reduce-scatter.2.cloned.1.call-done = f32[16,16384]{1,0:T(8,128)} async-done(((f32[16,65536]{1,0:T(8,128)}), f32[16,16384]{1,0:T(8,128)}) %reduce-scatter.2.cloned.1.call-update) | async-done | bytes 1048592 | tf_op jit(solution)/shard_map/reduce_scatter | solution.py:94
  97.7 1.3 convert_element_type.47
  98.9 0.1 copy.24
  99.1 1.6 gather_fusion
  100.6 5.1 %all-to-all-start = ((bf16[32,64,256]{2,1,0:T(8,128)(2,1)}), bf16[32,64,256]{2,1,0:T(8,128)(2,1)S(1)}, u32[]{:S(2)}, u32[]{:S(2)}) async-start(bf16[32,64,256]{2,1,0:T(8,128)(2,1)} %gather_fusion), calls=%async_computation.1 | async-start | bytes 2097152 | tf_op jit(solution)/shard_map/all_to_all | solution.py:103
  105.8 0.0 copy-done.2
  105.8 0.2 copy.16
  106.0 6.4 %copy.19 = bf16[1024,2048]{0,1:T(8,128)(2,1)} copy(bf16[1024,2048]{1,0:T(8,128)(2,1)} %param.7) | data formatting | bytes 8388608 | tf_op args[0]
  112.4 18.4 %all-to-all-done = bf16[32,64,256]{2,1,0:T(8,128)(2,1)S(1)} async-done(((bf16[32,64,256]{2,1,0:T(8,128)(2,1)}), bf16[32,64,256]{2,1,0:T(8,128)(2,1)S(1)}, u32[]{:S(2)}, u32[]{:S(2)}) %all-to-all-start) | async-done | bytes 1048608 | tf_op jit(solution)/shard_map/all_to_all | solution.py:103
  130.8 3.9 %multiply_convert_fusion = bf16[1024,256]{0,1:T(8,128)(2,1)S(1)} fusion(bf16[2048,256]{1,0:T(8,128)(2,1)S(1)} %bitcast.33, bf16[1024,2048]{1,0:T(8,128)(2,1)} %param.7, bf16[1024,256]{0,1:T(8,128)(2,1)S(1)} %copy.16), kind=kOutput, calls=%fused_computation.7 | convolution fusion | flops 1076363264 | bytes 6291456 | tf_op jit(solution)/shard_map/btd,bdr->btr/dot_general | solution.py:107
  134.7 0.0 copy-done.1
  134.7 2.3 fusion
  137.0 4.5 %all-to-all-start.1 = ((bf16[32,64,256]{2,1,0:T(8,128)(2,1)}), bf16[32,64,256]{2,1,0:T(8,128)(2,1)S(1)}, u32[]{:S(2)}, u32[]{:S(2)}) async-start(bf16[32,64,256]{2,1,0:T(8,128)(2,1)} %fusion), calls=%async_computation.2 | async-start | bytes 2097152 | tf_op jit(solution)/shard_map/all_to_all | solution.py:121
  141.5 0.0 all-gather.2.cloned.1.call-start
  141.5 3.3 %convolution_convert_fusion.1 = bf16[1024,2048]{1,0:T(8,128)(2,1)} fusion(bf16[1024,256]{0,1:T(8,128)(2,1)S(1)} %multiply_convert_fusion, bf16[2048,256]{1,0:T(8,128)(2,1)S(1)} %bitcast.34), kind=kOutput, calls=%fused_computation.2 | convolution fusion | flops 1075838976 | bytes 5767168 | tf_op jit(solution)/shard_map/btr,bdr->btd/dot_general | solution.py:113
  144.8 21.7 %all-to-all-done.1 = bf16[32,64,256]{2,1,0:T(8,128)(2,1)S(1)} async-done(((bf16[32,64,256]{2,1,0:T(8,128)(2,1)}), bf16[32,64,256]{2,1,0:T(8,128)(2,1)S(1)}, u32[]{:S(2)}, u32[]{:S(2)}) %all-to-all-start.1) | async-done | bytes 1048608 | tf_op jit(solution)/shard_map/all_to_all | solution.py:121
  166.5 0.6 copy.25
  167.1 1.1 convolution_convert_fusion.grad_ref
  168.2 0.0 all-gather.2.cloned.1.call-update
  168.3 5.5 %shard_map.94 = (bf16[128,65536]{1,0:T(8,128)(2,1)}, f32[128,16]{1,0:T(8,128)}) custom-call(s32[1]{0:T(128)} %bitcast.7.own_ref, bf16[128,16]{1,0:T(8,128)(2,1)} %bitcast.39, bf16[16,16384]{1,0:T(8,128)(2,1)} %convolution_convert_fusion.grad_ref, bf16[128,65536]{1,0:T(8,128)(2,1)} %gen_ref.3), custom_call_target="tpu_custom_call" | custom-call | tf_op jit(solution)/shard_map/pallas_call | solution.py:54
  173.8 40.4 %all-gather.2.cloned.1.call-done.grad_ref = bf16[16,65536]{1,0:T(8,128)(2,1)} async-done(((bf16[16,16384]{1,0:T(8,128)(2,1)}), bf16[16,65536]{1,0:T(8,128)(2,1)}) %all-gather.2.cloned.1.call-update) | async-done | bytes 2097168 | tf_op jit(solution)/shard_map/all_gather | solution.py:131
  214.2 13.8 %shard_map.95 = (bf16[128,65536]{1,0:T(8,128)(2,1)}, f32[128,16]{1,0:T(8,128)}) custom-call(s32[1]{0:T(128)} %bitcast.7.own_ref, bf16[128,16]{1,0:T(8,128)(2,1)} %bitcast.40, bf16[16,65536]{1,0:T(8,128)(2,1)} %all-gather.2.cloned.1.call-done.grad_ref, bf16[128,65536]{1,0:T(8,128)(2,1)} %gen_ref.3, ...), custom_call_target="tpu_custom_call", output_to_operand_aliasing={{0}: (4, {})} | custom-call | tf_op jit(solution)/shard_map/pallas_call | solution.py:54
  228.0 0.0 copy-done.4
  228.0 0.8 add_bitcast_fusion
  228.9 0.1 collective-permute-start
  229.0 1.2 collective-permute-done
  230.2 1.6 collective-permute-start.1
  231.8 2.8 %collective-permute-done.1 = f32[16,128]{0,1:T(8,128)S(1)} collective-permute-done((f32[16,128]{0,1:T(8,128)S(1)}, f32[16,128]{0,1:T(8,128)S(1)}, u32[]{:S(2)}, u32[]{:S(2)}) %collective-permute-start.1) | collective-permute-done | bytes 8224 | tf_op jit(solution)/shard_map/ppermute | solution.py:141
  234.6 1.6 collective-permute-start.2
  236.1 2.7 %collective-permute-done.2 = f32[16,128]{0,1:T(8,128)S(1)} collective-permute-done((f32[16,128]{0,1:T(8,128)S(1)}, f32[16,128]{0,1:T(8,128)S(1)}, u32[]{:S(2)}, u32[]{:S(2)}) %collective-permute-start.2) | collective-permute-done | bytes 8224 | tf_op jit(solution)/shard_map/ppermute | solution.py:141
  238.9 0.0 copy-done.5
  238.9 0.0 copy-done.6
  238.9 1.0 fusion.2
  (8 shorter events, 0.0 us)
Async XLA Ops:
  7.2 0.8 copy-start
  7.2 90.5 %reduce-scatter.2.cloned.1.call-start = ((), (), s32[]{:S(2)}) async-start(), calls=%async_computation.3 | async-start | bytes 5242880 | tf_op jit(solution)/shard_map/reduce_scatter | solution.py:94
  9.0 9.1 %copy-start.3 = (bf16[16,128]{0,1:T(8,128)(2,1)}, bf16[16,128]{0,1:T(8,128)(2,1)S(1)}, u32[]{:S(2)}) copy-start(bf16[16,128]{0,1:T(8,128)(2,1)S(1)} %convolution_convert_fusion.3) | copy-start | bytes 12292
  18.0 0.7 copy-start.7
  18.1 87.7 %copy-start.2 = (bf16[1024,256]{1,0:T(8,128)(2,1)S(1)}, bf16[1024,256]{1,0:T(8,128)(2,1)}, u32[]{:S(2)}) copy-start(bf16[1024,256]{1,0:T(8,128)(2,1)} %param.8) | copy-start | bytes 1572868
  100.6 30.2 %all-to-all-start = ((bf16[32,64,256]{2,1,0:T(8,128)(2,1)}), bf16[32,64,256]{2,1,0:T(8,128)(2,1)S(1)}, u32[]{:S(2)}, u32[]{:S(2)}) async-start(bf16[32,64,256]{2,1,0:T(8,128)(2,1)} %gather_fusion), calls=%async_computation.1 | async-start | bytes 2097152 | tf_op jit(solution)/shard_map/all_to_all | solution.py:103
  130.8 3.9 %copy-start.1 = (bf16[1024,2048]{0,1:T(8,128)(2,1)S(1)}, bf16[1024,2048]{0,1:T(8,128)(2,1)}, u32[]{:S(2)}) copy-start(bf16[1024,2048]{0,1:T(8,128)(2,1)} %copy.19) | copy-start | bytes 12582916
  137.0 29.5 %all-to-all-start.1 = ((bf16[32,64,256]{2,1,0:T(8,128)(2,1)}), bf16[32,64,256]{2,1,0:T(8,128)(2,1)S(1)}, u32[]{:S(2)}, u32[]{:S(2)}) async-start(bf16[32,64,256]{2,1,0:T(8,128)(2,1)} %fusion), calls=%async_computation.2 | async-start | bytes 2097152 | tf_op jit(solution)/shard_map/all_to_all | solution.py:121
  141.5 72.7 %all-gather.2.cloned.1.call-start = ((), (), s32[]{:S(2)}) async-start(), calls=%async_computation.4 | async-start | bytes 2621440 | tf_op jit(solution)/shard_map/all_gather | solution.py:131
  214.2 13.9 %copy-start.4 = (f32[128,16]{1,0:T(8,128)S(1)}, f32[128,16]{1,0:T(8,128)}, u32[]{:S(2)}) copy-start(f32[128,16]{1,0:T(8,128)} %get-tuple-element.13) | copy-start | bytes 24580
  214.2 24.7 %copy-start.5 = (s32[16]{0:T(128)S(1)}, s32[16]{0:T(128)}, u32[]{:S(2)}) copy-start(s32[16]{0:T(128)} %param.11) | copy-start | bytes 196
  214.2 24.7 %copy-start.6 = (s32[16]{0:T(128)S(1)}, s32[16]{0:T(128)}, u32[]{:S(2)}) copy-start(s32[16]{0:T(128)} %param.10) | copy-start | bytes 196
  228.9 1.3 collective-permute-start
  230.2 4.3 %collective-permute-start.1 = (f32[16,128]{0,1:T(8,128)S(1)}, f32[16,128]{0,1:T(8,128)S(1)}, u32[]{:S(2)}, u32[]{:S(2)}) collective-permute-start(f32[16,128]{0,1:T(8,128)S(1)} %add.29), channel_id=1, source_target_pairs={{0,2},{1,3},{2,0},{3,1},{4,6},{5,7},{6,4},{7,5},{8,10},{9,11},{10,... | collective-permute-start | bytes 24584 | tf_op jit(solution)/shard_map/ppermute | solution.py:141
  234.6 4.3 %collective-permute-start.2 = (f32[16,128]{0,1:T(8,128)S(1)}, f32[16,128]{0,1:T(8,128)S(1)}, u32[]{:S(2)}, u32[]{:S(2)}) collective-permute-start(f32[16,128]{0,1:T(8,128)S(1)} %add.30), channel_id=1, source_target_pairs={{0,4},{1,5},{2,6},{3,7},{4,0},{5,1},{6,2},{7,3},{8,12},{9,13},{10,... | collective-permute-start | bytes 24584 | tf_op jit(solution)/shard_map/ppermute | solution.py:141
Sparse Core Ops, SparseCore 0:
  18.2 79.4 reduce-scatter.1
  168.4 45.7 all-gather.1

commit v15 on v14

--- a/solution.py
+++ b/solution.py
@@ -93,13 +93,13 @@
     partial_value = jnp.dot(pair_embed, generator, preferred_element_type=jnp.float32)
     adapter_part = lax.psum_scatter(
         partial_value, "pair", scatter_dimension=1, tiled=True
-    ).astype(jnp.bfloat16)
+    )
     flat_pairs = block_pair[:, 0]
     gen_major_pairs = flat_pairs.reshape(pair_count_axis, gen_count).T.reshape(-1)
     rows_per = quarter // adapter_rank
     outgoing = jnp.take(
         adapter_part.reshape(pair_count, rows_per, adapter_rank), gen_major_pairs, axis=0, mode="clip"
-    )
+    ).astype(jnp.bfloat16)
     incoming = lax.all_to_all(outgoing, ("gen", "pair"), 0, 0, tiled=True)
     adapters = incoming.reshape(blocks_here, model_width, adapter_rank)
     token_blocks = tokens.reshape(blocks_here, BLK, model_width)

time: 247 us -> 248 us (level)
  no operation moved by 1% of the time
where the time goes in v15:
time: 248 us; the launch traced here: 247 us
  waiting for transfers between devices  165 us (67%)
  matrix products  21.6 us (9%)
  Pallas kernels  19.4 us (8%)
  between operations  14.1 us (6%)
  starting transfers between devices  12.8 us (5%)
  local copies, waits for them, and re-layouts  11.9 us (5%)
    reduce_scatter x1, waiting for transfers between devices, shards(): lax.psum_scatter(partial_value, 'pair', scatter_dimension=1, tiled=True)  78.1 us
    all_gather x1, waiting for transfers between devices, shards(): grad_rounded = lax.all_gather(row_grad, 'pair', axis=1, tiled=True)  40.4 us
    all_to_all x1, waiting for transfers between devices, shards(): returned = lax.all_to_all(by_owner, ('gen', 'pair'), 0, 0, tiled=True)  21.7 us
    pallas_call x2, Pallas kernels, grad_tail(): pl.pallas_call(_tail_kernel, grid_spec=pltpu.PrefetchScalarGridSpec(num_s...  19.4 us
    all_to_all x1, waiting for transfers between devices, shards(): incoming = lax.all_to_all(outgoing, ('gen', 'pair'), 0, 0, tiled=True)  18.4 us
    unnamed x21, local copies, waits for them, and re-layouts  10.1 us
    dot_general x1, matrix products, shards(): jnp.dot(pair_embed, generator, preferred_element_type=jnp.float32)  9.06 us
    ppermute x3, waiting for transfers between devices, shards(): grad_pair = grad_pair + lax.ppermute(grad_pair, 'gen', swap)  6.81 us
  transfers between devices with their start and end apart: 7, of which 7 were waited for; matrix products, arithmetic and copies ran while one was open for 5% of the time, Pallas kernels for 2%

profile of v15, /device:TPU:0, one launch (start us, length us, event | category | flops | bytes accessed | tf_op | source)
XLA Modules:
  0.0 246.9 jit_solution(11232109257943834900)
XLA Ops:
  7.2 0.0 copy-start
  7.2 0.0 reduce-scatter.2.cloned.1.call-start
  7.2 0.7 copy-done
  8.0 1.0 convolution_convert_fusion.3
  9.0 0.0 copy-start.3
  9.0 9.1 %fusion.9 = f32[16,65536]{1,0:T(8,128)} fusion(bf16[16,128]{0,1:T(8,128)(2,1)S(1)} %convolution_convert_fusion.3, bf16[128,65536]{1,0:T(8,128)(2,1)} %gen_ref.3), kind=kOutput, calls=%fused_computation.23 | convolution fusion | flops 268435456 | bytes 20975616 | tf_op jit(solution)/shard_map/dot_general | solution.py:93
  18.0 0.0 copy-done.3
  18.0 0.0 copy-start.7
  18.0 0.0 copy-start.2
  18.0 0.0 reduce-scatter.2.cloned.1.call-update
  18.1 0.5 broadcast.18
  18.6 0.1 copy-done.7
  18.7 0.7 reduce.3
  19.3 0.1 reshape_squeeze.3
  19.4 0.1 copy.18
  19.5 0.1 reshape.63
  19.6 78.1 %reduce-scatter.2.cloned.1.call-done = f32[16,16384]{1,0:T(8,128)} async-done(((f32[16,65536]{1,0:T(8,128)}), f32[16,16384]{1,0:T(8,128)}) %reduce-scatter.2.cloned.1.call-update) | async-done | bytes 1048592 | tf_op jit(solution)/shard_map/reduce_scatter | solution.py:94
  97.7 1.5 copy.24
  99.2 1.6 gather_fusion
  100.8 5.1 %all-to-all-start = ((bf16[32,64,256]{2,1,0:T(8,128)(2,1)}), bf16[32,64,256]{2,1,0:T(8,128)(2,1)S(1)}, u32[]{:S(2)}, u32[]{:S(2)}) async-start(bf16[32,64,256]{2,1,0:T(8,128)(2,1)} %gather_fusion), calls=%async_computation.1 | async-start | bytes 2097152 | tf_op jit(solution)/shard_map/all_to_all | solution.py:103
  105.9 0.0 copy-done.2
  105.9 0.2 copy.16
  106.1 6.4 %copy.19 = bf16[1024,2048]{0,1:T(8,128)(2,1)} copy(bf16[1024,2048]{1,0:T(8,128)(2,1)} %param.7) | data formatting | bytes 8388608 | tf_op args[0]
  112.5 18.4 %all-to-all-done = bf16[32,64,256]{2,1,0:T(8,128)(2,1)S(1)} async-done(((bf16[32,64,256]{2,1,0:T(8,128)(2,1)}), bf16[32,64,256]{2,1,0:T(8,128)(2,1)S(1)}, u32[]{:S(2)}, u32[]{:S(2)}) %all-to-all-start) | async-done | bytes 1048608 | tf_op jit(solution)/shard_map/all_to_all | solution.py:103
  130.9 3.9 %multiply_convert_fusion = bf16[1024,256]{0,1:T(8,128)(2,1)S(1)} fusion(bf16[2048,256]{1,0:T(8,128)(2,1)S(1)} %bitcast.33, bf16[1024,2048]{1,0:T(8,128)(2,1)} %param.7, bf16[1024,256]{0,1:T(8,128)(2,1)S(1)} %copy.16), kind=kOutput, calls=%fused_computation.7 | convolution fusion | flops 1076363264 | bytes 6291456 | tf_op jit(solution)/shard_map/btd,bdr->btr/dot_general | solution.py:107
  134.9 0.0 copy-done.1
  134.9 2.3 fusion
  137.1 4.5 %all-to-all-start.1 = ((bf16[32,64,256]{2,1,0:T(8,128)(2,1)}), bf16[32,64,256]{2,1,0:T(8,128)(2,1)S(1)}, u32[]{:S(2)}, u32[]{:S(2)}) async-start(bf16[32,64,256]{2,1,0:T(8,128)(2,1)} %fusion), calls=%async_computation.2 | async-start | bytes 2097152 | tf_op jit(solution)/shard_map/all_to_all | solution.py:121
  141.6 0.0 all-gather.2.cloned.1.call-start
  141.6 3.3 %convolution_convert_fusion.1 = bf16[1024,2048]{1,0:T(8,128)(2,1)} fusion(bf16[1024,256]{0,1:T(8,128)(2,1)S(1)} %multiply_convert_fusion, bf16[2048,256]{1,0:T(8,128)(2,1)S(1)} %bitcast.34), kind=kOutput, calls=%fused_computation.2 | convolution fusion | flops 1075838976 | bytes 5767168 | tf_op jit(solution)/shard_map/btr,bdr->btd/dot_general | solution.py:113
  145.0 21.7 %all-to-all-done.1 = bf16[32,64,256]{2,1,0:T(8,128)(2,1)S(1)} async-done(((bf16[32,64,256]{2,1,0:T(8,128)(2,1)}), bf16[32,64,256]{2,1,0:T(8,128)(2,1)S(1)}, u32[]{:S(2)}, u32[]{:S(2)}) %all-to-all-start.1) | async-done | bytes 1048608 | tf_op jit(solution)/shard_map/all_to_all | solution.py:121
  166.6 0.6 copy.25
  167.2 1.1 convolution_convert_fusion.grad_ref
  168.3 0.0 all-gather.2.cloned.1.call-update
  168.4 5.5 %shard_map.94 = (bf16[128,65536]{1,0:T(8,128)(2,1)}, f32[128,16]{1,0:T(8,128)}) custom-call(s32[1]{0:T(128)} %bitcast.7.own_ref, bf16[128,16]{1,0:T(8,128)(2,1)} %bitcast.39, bf16[16,16384]{1,0:T(8,128)(2,1)} %convolution_convert_fusion.grad_ref, bf16[128,65536]{1,0:T(8,128)(2,1)} %gen_ref.3), custom_call_target="tpu_custom_call" | custom-call | tf_op jit(solution)/shard_map/pallas_call | solution.py:54
  173.9 40.4 %all-gather.2.cloned.1.call-done.grad_ref = bf16[16,65536]{1,0:T(8,128)(2,1)} async-done(((bf16[16,16384]{1,0:T(8,128)(2,1)}), bf16[16,65536]{1,0:T(8,128)(2,1)}) %all-gather.2.cloned.1.call-update) | async-done | bytes 2097168 | tf_op jit(solution)/shard_map/all_gather | solution.py:131
  214.3 13.9 %shard_map.95 = (bf16[128,65536]{1,0:T(8,128)(2,1)}, f32[128,16]{1,0:T(8,128)}) custom-call(s32[1]{0:T(128)} %bitcast.7.own_ref, bf16[128,16]{1,0:T(8,128)(2,1)} %bitcast.40, bf16[16,65536]{1,0:T(8,128)(2,1)} %all-gather.2.cloned.1.call-done.grad_ref, bf16[128,65536]{1,0:T(8,128)(2,1)} %gen_ref.3, ...), custom_call_target="tpu_custom_call", output_to_operand_aliasing={{0}: (4, {})} | custom-call | tf_op jit(solution)/shard_map/pallas_call | solution.py:54
  228.2 0.0 copy-done.4
  228.2 0.8 add_bitcast_fusion
  229.1 0.1 collective-permute-start
  229.1 1.2 collective-permute-done
  230.4 1.6 collective-permute-start.1
  231.9 2.8 %collective-permute-done.1 = f32[16,128]{0,1:T(8,128)S(1)} collective-permute-done((f32[16,128]{0,1:T(8,128)S(1)}, f32[16,128]{0,1:T(8,128)S(1)}, u32[]{:S(2)}, u32[]{:S(2)}) %collective-permute-start.1) | collective-permute-done | bytes 8224 | tf_op jit(solution)/shard_map/ppermute | solution.py:141
  234.7 1.5 collective-permute-start.2
  236.3 2.8 %collective-permute-done.2 = f32[16,128]{0,1:T(8,128)S(1)} collective-permute-done((f32[16,128]{0,1:T(8,128)S(1)}, f32[16,128]{0,1:T(8,128)S(1)}, u32[]{:S(2)}, u32[]{:S(2)}) %collective-permute-start.2) | collective-permute-done | bytes 8224 | tf_op jit(solution)/shard_map/ppermute | solution.py:141
  239.1 0.0 copy-done.5
  239.1 0.0 copy-done.6
  239.1 1.0 fusion.2
  (7 shorter events, 0.0 us)
Async XLA Ops:
  7.2 0.8 copy-start
  7.2 90.5 %reduce-scatter.2.cloned.1.call-start = ((), (), s32[]{:S(2)}) async-start(), calls=%async_computation.3 | async-start | bytes 5242880 | tf_op jit(solution)/shard_map/reduce_scatter | solution.py:94
  9.0 9.1 %copy-start.3 = (bf16[16,128]{0,1:T(8,128)(2,1)}, bf16[16,128]{0,1:T(8,128)(2,1)S(1)}, u32[]{:S(2)}) copy-start(bf16[16,128]{0,1:T(8,128)(2,1)S(1)} %convolution_convert_fusion.3) | copy-start | bytes 12292
  18.0 0.7 copy-start.7
  18.0 87.9 %copy-start.2 = (bf16[1024,256]{1,0:T(8,128)(2,1)S(1)}, bf16[1024,256]{1,0:T(8,128)(2,1)}, u32[]{:S(2)}) copy-start(bf16[1024,256]{1,0:T(8,128)(2,1)} %param.8) | copy-start | bytes 1572868
  100.8 30.2 %all-to-all-start = ((bf16[32,64,256]{2,1,0:T(8,128)(2,1)}), bf16[32,64,256]{2,1,0:T(8,128)(2,1)S(1)}, u32[]{:S(2)}, u32[]{:S(2)}) async-start(bf16[32,64,256]{2,1,0:T(8,128)(2,1)} %gather_fusion), calls=%async_computation.1 | async-start | bytes 2097152 | tf_op jit(solution)/shard_map/all_to_all | solution.py:103
  130.9 3.9 %copy-start.1 = (bf16[1024,2048]{0,1:T(8,128)(2,1)S(1)}, bf16[1024,2048]{0,1:T(8,128)(2,1)}, u32[]{:S(2)}) copy-start(bf16[1024,2048]{0,1:T(8,128)(2,1)} %copy.19) | copy-start | bytes 12582916
  137.1 29.5 %all-to-all-start.1 = ((bf16[32,64,256]{2,1,0:T(8,128)(2,1)}), bf16[32,64,256]{2,1,0:T(8,128)(2,1)S(1)}, u32[]{:S(2)}, u32[]{:S(2)}) async-start(bf16[32,64,256]{2,1,0:T(8,128)(2,1)} %fusion), calls=%async_computation.2 | async-start | bytes 2097152 | tf_op jit(solution)/shard_map/all_to_all | solution.py:121
  141.6 72.7 %all-gather.2.cloned.1.call-start = ((), (), s32[]{:S(2)}) async-start(), calls=%async_computation.4 | async-start | bytes 2621440 | tf_op jit(solution)/shard_map/all_gather | solution.py:131
  214.3 13.9 %copy-start.4 = (f32[128,16]{1,0:T(8,128)S(1)}, f32[128,16]{1,0:T(8,128)}, u32[]{:S(2)}) copy-start(f32[128,16]{1,0:T(8,128)} %get-tuple-element.13) | copy-start | bytes 24580
  214.3 24.7 %copy-start.5 = (s32[16]{0:T(128)S(1)}, s32[16]{0:T(128)}, u32[]{:S(2)}) copy-start(s32[16]{0:T(128)} %param.11) | copy-start | bytes 196
  214.3 24.7 %copy-start.6 = (s32[16]{0:T(128)S(1)}, s32[16]{0:T(128)}, u32[]{:S(2)}) copy-start(s32[16]{0:T(128)} %param.10) | copy-start | bytes 196
  229.1 1.3 collective-permute-start
  230.4 4.3 %collective-permute-start.1 = (f32[16,128]{0,1:T(8,128)S(1)}, f32[16,128]{0,1:T(8,128)S(1)}, u32[]{:S(2)}, u32[]{:S(2)}) collective-permute-start(f32[16,128]{0,1:T(8,128)S(1)} %add.29), channel_id=1, source_target_pairs={{0,2},{1,3},{2,0},{3,1},{4,6},{5,7},{6,4},{7,5},{8,10},{9,11},{10,... | collective-permute-start | bytes 24584 | tf_op jit(solution)/shard_map/ppermute | solution.py:141
  234.7 4.3 %collective-permute-start.2 = (f32[16,128]{0,1:T(8,128)S(1)}, f32[16,128]{0,1:T(8,128)S(1)}, u32[]{:S(2)}, u32[]{:S(2)}) collective-permute-start(f32[16,128]{0,1:T(8,128)S(1)} %add.30), channel_id=1, source_target_pairs={{0,4},{1,5},{2,6},{3,7},{4,0},{5,1},{6,2},{7,3},{8,12},{9,13},{10,... | collective-permute-start | bytes 24584 | tf_op jit(solution)/shard_map/ppermute | solution.py:141
Sparse Core Ops, SparseCore 0:
  18.2 79.4 reduce-scatter.1
  168.5 45.7 all-gather.1

commit v16 on v14

--- a/solution.py
+++ b/solution.py
@@ -6,7 +6,7 @@
 from jax.experimental.pallas import tpu as pltpu
 
 BLK = 1024
-TAIL_COLS = 8192
+TAIL_COLS = 16384
 
 
 def _tail_kernel(own_ref, embed_t_ref, grad_ref, gen_ref, *rest):

time: 247 us -> 248 us (level)
  transfers between devices with their start and end apart: 7 -> 7, of which waited for: 7 -> 7; matrix products, arithmetic and copies ran while one was open for 5% -> 5% of each run, Pallas kernels for 2% -> 3%
where the time goes in v16:
time: 248 us; the launch traced here: 247 us
  waiting for transfers between devices  164 us (66%)
  matrix products  21.6 us (9%)
  Pallas kernels  21 us (8%)
  between operations  14.2 us (6%)
  starting transfers between devices  12.9 us (5%)
  local copies, waits for them, and re-layouts  10.5 us (4%)
  other arithmetic  2.81 us (1%)
    reduce_scatter x1, waiting for transfers between devices, shards(): lax.psum_scatter(partial_value, 'pair', scatter_dimension=1, tiled=True)  78.1 us
    all_gather x1, waiting for transfers between devices, shards(): grad_rounded = lax.all_gather(row_grad, 'pair', axis=1, tiled=True)  39.3 us
    all_to_all x1, waiting for transfers between devices, shards(): returned = lax.all_to_all(by_owner, ('gen', 'pair'), 0, 0, tiled=True)  21.5 us
    pallas_call x2, Pallas kernels, grad_tail(): pl.pallas_call(_tail_kernel, grid_spec=pltpu.PrefetchScalarGridSpec(num_s...  21 us
    all_to_all x1, waiting for transfers between devices, shards(): incoming = lax.all_to_all(outgoing, ('gen', 'pair'), 0, 0, tiled=True)  18.4 us
    dot_general x1, matrix products, shards(): jnp.dot(pair_embed, generator, preferred_element_type=jnp.float32)  9.06 us
    unnamed x21, local copies, waits for them, and re-layouts  8.7 us
    ppermute x3, waiting for transfers between devices, shards(): grad_pair = grad_pair + lax.ppermute(grad_pair, 'gen', swap)  6.87 us
  transfers between devices with their start and end apart: 7, of which 7 were waited for; matrix products, arithmetic and copies ran while one was open for 5% of the time, Pallas kernels for 3%

profile of v16, /device:TPU:0, one launch (start us, length us, event | category | flops | bytes accessed | tf_op | source)
XLA Modules:
  0.0 247.2 jit_solution(3968358201648364164)
XLA Ops:
  7.2 0.0 copy-start
  7.2 0.0 reduce-scatter.2.cloned.1.call-start
  7.2 0.7 copy-done
  8.0 1.0 convolution_convert_fusion.3
  9.0 0.0 copy-start.3
  9.0 9.1 %fusion.9 = f32[16,65536]{1,0:T(8,128)} fusion(bf16[16,128]{0,1:T(8,128)(2,1)S(1)} %convolution_convert_fusion.3, bf16[128,65536]{1,0:T(8,128)(2,1)} %gen_ref.3), kind=kOutput, calls=%fused_computation.23 | convolution fusion | flops 268435456 | bytes 20975616 | tf_op jit(solution)/shard_map/dot_general | solution.py:93
  18.0 0.0 copy-done.3
  18.0 0.0 reduce-scatter.2.cloned.1.call-update
  18.1 0.0 copy-start.2
  18.1 0.5 broadcast.18
  18.6 0.1 copy-done.7
  18.7 0.7 reduce.3
  19.3 0.1 reshape_squeeze.3
  19.4 0.1 copy.18
  19.5 0.1 reshape.63
  19.6 78.1 %reduce-scatter.2.cloned.1.call-done = f32[16,16384]{1,0:T(8,128)} async-done(((f32[16,65536]{1,0:T(8,128)}), f32[16,16384]{1,0:T(8,128)}) %reduce-scatter.2.cloned.1.call-update) | async-done | bytes 1048592 | tf_op jit(solution)/shard_map/reduce_scatter | solution.py:94
  97.7 1.3 convert_element_type.47
  98.9 0.1 copy.24
  99.1 1.6 gather_fusion
  100.6 5.1 %all-to-all-start = ((bf16[32,64,256]{2,1,0:T(8,128)(2,1)}), bf16[32,64,256]{2,1,0:T(8,128)(2,1)S(1)}, u32[]{:S(2)}, u32[]{:S(2)}) async-start(bf16[32,64,256]{2,1,0:T(8,128)(2,1)} %gather_fusion), calls=%async_computation.1 | async-start | bytes 2097152 | tf_op jit(solution)/shard_map/all_to_all | solution.py:103
  105.8 0.0 copy-done.2
  105.8 0.2 copy.16
  106.0 6.4 %copy.19 = bf16[1024,2048]{0,1:T(8,128)(2,1)} copy(bf16[1024,2048]{1,0:T(8,128)(2,1)} %param.7) | data formatting | bytes 8388608 | tf_op args[0]
  112.4 18.4 %all-to-all-done = bf16[32,64,256]{2,1,0:T(8,128)(2,1)S(1)} async-done(((bf16[32,64,256]{2,1,0:T(8,128)(2,1)}), bf16[32,64,256]{2,1,0:T(8,128)(2,1)S(1)}, u32[]{:S(2)}, u32[]{:S(2)}) %all-to-all-start) | async-done | bytes 1048608 | tf_op jit(solution)/shard_map/all_to_all | solution.py:103
  130.8 3.9 %multiply_convert_fusion = bf16[1024,256]{0,1:T(8,128)(2,1)S(1)} fusion(bf16[2048,256]{1,0:T(8,128)(2,1)S(1)} %bitcast.33, bf16[1024,2048]{1,0:T(8,128)(2,1)} %param.7, bf16[1024,256]{0,1:T(8,128)(2,1)S(1)} %copy.16), kind=kOutput, calls=%fused_computation.7 | convolution fusion | flops 1076363264 | bytes 6291456 | tf_op jit(solution)/shard_map/btd,bdr->btr/dot_general | solution.py:107
  134.7 0.0 copy-done.1
  134.7 2.3 fusion
  137.0 4.5 %all-to-all-start.1 = ((bf16[32,64,256]{2,1,0:T(8,128)(2,1)}), bf16[32,64,256]{2,1,0:T(8,128)(2,1)S(1)}, u32[]{:S(2)}, u32[]{:S(2)}) async-start(bf16[32,64,256]{2,1,0:T(8,128)(2,1)} %fusion), calls=%async_computation.2 | async-start | bytes 2097152 | tf_op jit(solution)/shard_map/all_to_all | solution.py:121
  141.5 0.2 all-gather.2.cloned.1.call-start
  141.7 3.3 %convolution_convert_fusion.1 = bf16[1024,2048]{1,0:T(8,128)(2,1)} fusion(bf16[1024,256]{0,1:T(8,128)(2,1)S(1)} %multiply_convert_fusion, bf16[2048,256]{1,0:T(8,128)(2,1)S(1)} %bitcast.34), kind=kOutput, calls=%fused_computation.2 | convolution fusion | flops 1075838976 | bytes 5767168 | tf_op jit(solution)/shard_map/btr,bdr->btd/dot_general | solution.py:113
  145.0 21.5 %all-to-all-done.1 = bf16[32,64,256]{2,1,0:T(8,128)(2,1)S(1)} async-done(((bf16[32,64,256]{2,1,0:T(8,128)(2,1)}), bf16[32,64,256]{2,1,0:T(8,128)(2,1)S(1)}, u32[]{:S(2)}, u32[]{:S(2)}) %all-to-all-start.1) | async-done | bytes 1048608 | tf_op jit(solution)/shard_map/all_to_all | solution.py:121
  166.5 0.6 copy.25
  167.1 1.1 convolution_convert_fusion.grad_ref
  168.2 0.0 all-gather.2.cloned.1.call-update
  168.3 6.7 %shard_map.94 = (bf16[128,65536]{1,0:T(8,128)(2,1)}, f32[128,16]{1,0:T(8,128)}) custom-call(s32[1]{0:T(128)} %bitcast.7.own_ref, bf16[128,16]{1,0:T(8,128)(2,1)} %bitcast.39, bf16[16,16384]{1,0:T(8,128)(2,1)} %convolution_convert_fusion.grad_ref, bf16[128,65536]{1,0:T(8,128)(2,1)} %gen_ref.3), custom_call_target="tpu_custom_call" | custom-call | tf_op jit(solution)/shard_map/pallas_call | solution.py:54
  174.9 39.3 %all-gather.2.cloned.1.call-done.grad_ref = bf16[16,65536]{1,0:T(8,128)(2,1)} async-done(((bf16[16,16384]{1,0:T(8,128)(2,1)}), bf16[16,65536]{1,0:T(8,128)(2,1)}) %all-gather.2.cloned.1.call-update) | async-done | bytes 2097168 | tf_op jit(solution)/shard_map/all_gather | solution.py:131
  214.2 14.4 %shard_map.95 = (bf16[128,65536]{1,0:T(8,128)(2,1)}, f32[128,16]{1,0:T(8,128)}) custom-call(s32[1]{0:T(128)} %bitcast.7.own_ref, bf16[128,16]{1,0:T(8,128)(2,1)} %bitcast.40, bf16[16,65536]{1,0:T(8,128)(2,1)} %all-gather.2.cloned.1.call-done.grad_ref, bf16[128,65536]{1,0:T(8,128)(2,1)} %gen_ref.3, ...), custom_call_target="tpu_custom_call", output_to_operand_aliasing={{0}: (4, {})} | custom-call | tf_op jit(solution)/shard_map/pallas_call | solution.py:54
  228.6 0.0 copy-done.4
  228.6 0.8 add_bitcast_fusion
  229.4 0.1 collective-permute-start
  229.5 1.2 collective-permute-done
  230.8 1.5 collective-permute-start.1
  232.3 2.8 %collective-permute-done.1 = f32[16,128]{0,1:T(8,128)S(1)} collective-permute-done((f32[16,128]{0,1:T(8,128)S(1)}, f32[16,128]{0,1:T(8,128)S(1)}, u32[]{:S(2)}, u32[]{:S(2)}) %collective-permute-start.1) | collective-permute-done | bytes 8224 | tf_op jit(solution)/shard_map/ppermute | solution.py:141
  235.1 1.5 collective-permute-start.2
  236.6 2.8 %collective-permute-done.2 = f32[16,128]{0,1:T(8,128)S(1)} collective-permute-done((f32[16,128]{0,1:T(8,128)S(1)}, f32[16,128]{0,1:T(8,128)S(1)}, u32[]{:S(2)}, u32[]{:S(2)}) %collective-permute-start.2) | collective-permute-done | bytes 8224 | tf_op jit(solution)/shard_map/ppermute | solution.py:141
  239.4 0.0 copy-done.5
  239.4 0.0 copy-done.6
  239.4 1.0 fusion.2
  (8 shorter events, 0.0 us)
Async XLA Ops:
  7.2 0.8 copy-start
  7.2 90.5 %reduce-scatter.2.cloned.1.call-start = ((), (), s32[]{:S(2)}) async-start(), calls=%async_computation.3 | async-start | bytes 5242880 | tf_op jit(solution)/shard_map/reduce_scatter | solution.py:94
  9.0 9.1 %copy-start.3 = (bf16[16,128]{0,1:T(8,128)(2,1)}, bf16[16,128]{0,1:T(8,128)(2,1)S(1)}, u32[]{:S(2)}) copy-start(bf16[16,128]{0,1:T(8,128)(2,1)S(1)} %convolution_convert_fusion.3) | copy-start | bytes 12292
  18.0 0.7 copy-start.7
  18.1 87.7 %copy-start.2 = (bf16[1024,256]{1,0:T(8,128)(2,1)S(1)}, bf16[1024,256]{1,0:T(8,128)(2,1)}, u32[]{:S(2)}) copy-start(bf16[1024,256]{1,0:T(8,128)(2,1)} %param.8) | copy-start | bytes 1572868
  100.6 30.2 %all-to-all-start = ((bf16[32,64,256]{2,1,0:T(8,128)(2,1)}), bf16[32,64,256]{2,1,0:T(8,128)(2,1)S(1)}, u32[]{:S(2)}, u32[]{:S(2)}) async-start(bf16[32,64,256]{2,1,0:T(8,128)(2,1)} %gather_fusion), calls=%async_computation.1 | async-start | bytes 2097152 | tf_op jit(solution)/shard_map/all_to_all | solution.py:103
  130.8 3.9 %copy-start.1 = (bf16[1024,2048]{0,1:T(8,128)(2,1)S(1)}, bf16[1024,2048]{0,1:T(8,128)(2,1)}, u32[]{:S(2)}) copy-start(bf16[1024,2048]{0,1:T(8,128)(2,1)} %copy.19) | copy-start | bytes 12582916
  137.0 29.5 %all-to-all-start.1 = ((bf16[32,64,256]{2,1,0:T(8,128)(2,1)}), bf16[32,64,256]{2,1,0:T(8,128)(2,1)S(1)}, u32[]{:S(2)}, u32[]{:S(2)}) async-start(bf16[32,64,256]{2,1,0:T(8,128)(2,1)} %fusion), calls=%async_computation.2 | async-start | bytes 2097152 | tf_op jit(solution)/shard_map/all_to_all | solution.py:121
  141.5 72.7 %all-gather.2.cloned.1.call-start = ((), (), s32[]{:S(2)}) async-start(), calls=%async_computation.4 | async-start | bytes 2621440 | tf_op jit(solution)/shard_map/all_gather | solution.py:131
  214.2 14.4 %copy-start.4 = (f32[128,16]{1,0:T(8,128)S(1)}, f32[128,16]{1,0:T(8,128)}, u32[]{:S(2)}) copy-start(f32[128,16]{1,0:T(8,128)} %get-tuple-element.13) | copy-start | bytes 24580
  214.2 25.2 %copy-start.5 = (s32[16]{0:T(128)S(1)}, s32[16]{0:T(128)}, u32[]{:S(2)}) copy-start(s32[16]{0:T(128)} %param.11) | copy-start | bytes 196
  214.2 25.2 %copy-start.6 = (s32[16]{0:T(128)S(1)}, s32[16]{0:T(128)}, u32[]{:S(2)}) copy-start(s32[16]{0:T(128)} %param.10) | copy-start | bytes 196
  229.4 1.3 collective-permute-start
  230.8 4.3 %collective-permute-start.1 = (f32[16,128]{0,1:T(8,128)S(1)}, f32[16,128]{0,1:T(8,128)S(1)}, u32[]{:S(2)}, u32[]{:S(2)}) collective-permute-start(f32[16,128]{0,1:T(8,128)S(1)} %add.29), channel_id=1, source_target_pairs={{0,2},{1,3},{2,0},{3,1},{4,6},{5,7},{6,4},{7,5},{8,10},{9,11},{10,... | collective-permute-start | bytes 24584 | tf_op jit(solution)/shard_map/ppermute | solution.py:141
  235.1 4.3 %collective-permute-start.2 = (f32[16,128]{0,1:T(8,128)S(1)}, f32[16,128]{0,1:T(8,128)S(1)}, u32[]{:S(2)}, u32[]{:S(2)}) collective-permute-start(f32[16,128]{0,1:T(8,128)S(1)} %add.30), channel_id=1, source_target_pairs={{0,4},{1,5},{2,6},{3,7},{4,0},{5,1},{6,2},{7,3},{8,12},{9,13},{10,... | collective-permute-start | bytes 24584 | tf_op jit(solution)/shard_map/ppermute | solution.py:141
Sparse Core Ops, SparseCore 0:
  18.2 79.4 reduce-scatter.1
  168.4 45.7 all-gather.1
